TPU v7x, 512 devices: a whole 4x8x8 slice. The times are simulated.
512 devices in a mesh: sub: 128 (over z_hi, x, y, core), scen: 4 (over z_lo).
Axes of the slice: x: 4, y: 8, z: 8 (z_hi: 2, z_lo: 4; z = z_hi * 4 + z_lo), core: 2. Of those that a mesh axis runs over, the one named last changes fastest.
Arguments:
- inverse_matrix: bfloat16 [128, 1024, 1024], P('sub'), may hold values from -1 to 1
- objective_grad: bfloat16 [48, 128, 64, 1024], P(None, 'sub', 'scen'), may hold values from -6 to 6
- final_adjoint: float32 [128, 64, 1024], P('sub', 'scen'), may hold values from -6 to 6
- companion: float32 [128, 1024], P('sub'), may hold values from 0.95 to 0.995
- port_node: int32 [128, 4, 8], P('sub'), may hold values from 0 to 1023
- line_count: int32 [128, 4], P('sub'), may hold values from 1 to 8, as said below
- line_delay: int32 [128, 4, 8], P('sub'), may hold values from 24 to 47, as said below
- line_admittance: float32 [128, 4, 8], P('sub'), may hold values from 0.3 to 1.2
- later_history: float32 [128, 4, 8, 48, 64], P('sub', None, None, None, 'scen'), may hold values from -6 to 6
- conv_node: int32 [128, 16], P('sub'), may hold values from 0 to 1023
- conv_drive: float32 [128, 48, 64, 16], P('sub', None, 'scen'), may hold values from -0.25 to 0.25
- fault_bus: int32 [64], P('scen'), may hold values from 0 to 131071
- fault_current: float32 [48, 64], P(None, 'scen'), may hold values from -12 to 12
- fault_voltage: float32 [48, 64], P(None, 'scen'), may hold values from -2 to 2
Outputs:
- adjoint_start: float32 [128, 64, 1024], P('sub', 'scen')
- earlier_history: float32 [128, 4, 8, 48, 64], P('sub', None, None, None, 'scen')
- control_sens: float32 [128, 16], P('sub')
- fault_sens: float32 [64], P('scen')
Inputs may be any that keep to these rules, and one draw needn't show every extreme that they name: line_count[p, e] equals line_count of the partner subnetwork in the opposite direction; the most is reached in every draw. `line_delay`: both ends of a line have the same delay; both ends of the range are reached in every draw.
All inputs are finite; a program needn't handle non-finite values.
Results may differ from a plain program's by a relative error of at most 0.0088.
Values sent between devices are 32-bit elements; how exact they have to be, the bound alone decides.
No kernel may reach another device: no remote copies, remote signals or barrier semaphores. Data moves between devices by JAX's collectives and lax.ppermute only.
A program may use at most 64 MiB of HBM per device.

v0:
```python
import jax
import jax.numpy as jnp
from jax import lax
from jax.sharding import PartitionSpec as P

PRECISE = lax.Precision.HIGHEST


def passed_along(value, axis, steps):
    count = lax.axis_size(axis)
    pairs = [(source, (source + steps) % count) for source in range(count)]
    return lax.ppermute(value, axis, pairs)


def body(
    inverse_matrix,
    objective_grad,
    final_adjoint,
    companion,
    port_node,
    line_count,
    line_delay,
    line_admittance,
    later_history,
    conv_node,
    conv_drive,
    fault_bus,
    fault_current,
    fault_voltage,
):
    node_count = inverse_matrix.shape[1]
    scen_rows = objective_grad.shape[2]
    slot_count = port_node.shape[2]
    port_total = 4 * slot_count
    conv_count = conv_node.shape[1]
    block_len = later_history.shape[3] // 2
    blocks = objective_grad.shape[0] // block_len
    sub_count = lax.axis_size("sub")
    grid_width = max(2, sub_count // 16)
    offsets = (1, -1, grid_width, -grid_width)
    opposite = (1, 0, 3, 2)
    sub_index = lax.axis_index("sub")
    weights = inverse_matrix[0]
    live_mask = (lax.iota(jnp.int32, slot_count)[None, :] < line_count[0][:, None]).astype(
        jnp.float32
    )
    node_iota = lax.iota(jnp.int32, node_count)
    pick_table = jnp.concatenate(
        [
            node_iota[:, None] == port_node[0].reshape(port_total)[None, :],
            node_iota[:, None] == conv_node[0][None, :],
        ],
        axis=1,
    ).astype(jnp.float32)
    spread_table = jnp.transpose(pick_table[:, :port_total])
    line_scale = (line_admittance[0] * live_mask).reshape(port_total)
    fault_table = (node_iota[None, :] == (fault_bus - sub_index * node_count)[:, None]).astype(
        jnp.float32
    )
    window = later_history[0]
    adjoint_next = final_adjoint[0]
    control_local = jnp.zeros((conv_count,), jnp.float32)
    fault_local = jnp.zeros((scen_rows,), jnp.float32)
    block_rows = lax.iota(jnp.int32, block_len)
    time_iota = lax.iota(jnp.int32, 2 * block_len)

    def one_step(adjoint_prev, inputs):
        grad_now, inflow_now, current_now = inputs
        right_side = (
            grad_now.astype(jnp.float32)
            + companion[0][None, :] * adjoint_prev
            + inflow_now
            + current_now[:, None] * fault_table
        )
        adjoint = jnp.dot(
            right_side.astype(jnp.bfloat16), weights, preferred_element_type=jnp.float32
        )
        return (adjoint, adjoint)

    for block_id in reversed(range(blocks)):
        block_start = block_id * block_len
        target = block_rows[None, None, :] + line_delay[0][:, :, None] - block_len
        time_table = (target[..., None] == time_iota).astype(jnp.float32)
        picked = (
            jnp.einsum("ecji,ecis->jsec", time_table, window, precision=PRECISE).reshape(
                block_len * scen_rows, port_total
            )
            * line_scale[None, :]
        )
        inflow = jnp.dot(picked, spread_table, precision=PRECISE).reshape(
            block_len, scen_rows, node_count
        )
        adjoint_next, adjoint_block = lax.scan(
            one_step,
            adjoint_next,
            (
                objective_grad[block_start : block_start + block_len, 0],
                inflow,
                fault_current[block_start : block_start + block_len],
            ),
            reverse=True,
        )
        samples = jnp.dot(
            adjoint_block.reshape(block_len * scen_rows, node_count), pick_table, precision=PRECISE
        )
        series = (
            jnp.transpose(
                samples[:, :port_total].reshape(block_len, scen_rows, 4, slot_count), (2, 3, 0, 1)
            )
            * live_mask[:, :, None, None]
        )
        outbound = series.reshape(4, slot_count, block_len * scen_rows)
        control_term = jnp.sum(
            samples[:, port_total:].reshape(block_len, scen_rows, conv_count)
            * conv_drive[0, block_start : block_start + block_len],
            axis=(0, 1),
        )
        fault_term = jnp.sum(
            jnp.sum(adjoint_block * fault_table[None], axis=2)
            * fault_voltage[block_start : block_start + block_len],
            axis=0,
        )
        control_local = control_local + lax.psum(control_term, "scen")
        fault_local = fault_local + lax.psum(fault_term, "sub")
        received = jnp.stack(
            [
                passed_along(outbound[opposite[direction]], "sub", -offsets[direction])
                for direction in range(4)
            ]
        )
        window = jnp.concatenate(
            [received.reshape(4, slot_count, block_len, scen_rows), window[:, :, :block_len]],
            axis=2,
        )
    return (adjoint_next[None], window[None], control_local[None], fault_local)


def solution(mesh):
    return jax.shard_map(
        body,
        mesh=mesh,
        in_specs=(
            P("sub", None, None),
            P(None, "sub", "scen", None),
            P("sub", "scen", None),
            P("sub", None),
            P("sub", None, None),
            P("sub", None),
            P("sub", None, None),
            P("sub", None, None),
            P("sub", None, None, None, "scen"),
            P("sub", None),
            P("sub", None, "scen", None),
            P("scen"),
            P(None, "scen"),
            P(None, "scen"),
        ),
        out_specs=(
            P("sub", "scen", None),
            P("sub", None, None, None, "scen"),
            P("sub", None),
            P("scen"),
        ),
        check_vma=False,
    )
```

profile of v0, /device:TPU:64, one launch (start us, length us, event | category | flops | bytes accessed | tf_op | source)
XLA Modules:
  0.0 630.8 jit_solution(12138053387449394268)
XLA Ops:
  6.0 2.4 slice_bitcast_fusion
  9.2 2.0 fusion.45
  12.6 46.1 %while.34 = (s32[]{:T(128)}, f32[16,1024]{1,0:T(8,128)S(1)}, f32[24,16,1024]{2,1,0:T(8,128)}, bf16[24,16,1024]{2,1,0:T(8,128)(2,1)}, f32[1,1024]{1,0:T(1,128)S(1...) while((s32[]{:T(128)}, f32[16,1024]{1,0:T(8,128)S(1)}, ...), condition=%wide.region_1.2_spmd.clone, body=%wide.region_0.1_spmd.clone.sunk | while | flops 33685504 | bytes 2528637 | solution.py:93
  12.7 1.9 bitcast_dynamic-update-slice_fusion.4
  14.6 1.9 bitcast_dynamic-update-slice_fusion.4
  22.3 1.9 bitcast_dynamic-update-slice_fusion.4
  26.1 1.9 bitcast_dynamic-update-slice_fusion.4
  28.0 1.9 bitcast_dynamic-update-slice_fusion.4
  45.3 1.9 bitcast_dynamic-update-slice_fusion.4
  53.0 1.9 bitcast_dynamic-update-slice_fusion.4
  54.9 1.9 bitcast_dynamic-update-slice_fusion.4
  58.9 2.3 fusion.57
  63.5 14.5 %collective-permute-start = (f32[8,384]{1,0:T(8,128)}, f32[8,384]{1,0:T(8,128)S(1)}, u32[]{:S(2)}, u32[]{:S(2)}) collective-permute-start(f32[8,384]{1,0:T(8,128)} %squeeze.91), channel_id=1, source_target_pairs={{0,508},{4,0},{8,4},{12,8},{16,12},{20,16},{24,20},{28,24},{32,28}... | collective-permute-start | bytes 36872 | tf_op jit(solution)/shard_map/ppermute | solution.py:12
  78.1 1.9 collective-permute-start.1
  80.8 5.3 collective-permute-start.2
  86.2 4.4 collective-permute-start.3
  98.0 4.7 collective-permute-done.3
  105.3 2.0 fusion.43
  108.7 62.3 %while.35 = (s32[]{:T(128)}, f32[16,1024]{1,0:T(8,128)S(1)}, f32[24,16,1024]{2,1,0:T(8,128)}, bf16[24,16,1024]{2,1,0:T(8,128)(2,1)S(1)}, f32[1,1024]{1,0:T(1,128...) while((s32[]{:T(128)}, f32[16,1024]{1,0:T(8,128)S(1)}, ...), condition=%wide.region_3.4_spmd.clone, body=%wide.region_2.3_spmd.clone.sunk | while | flops 33685504 | bytes 2529533 | solution.py:93
  109.4 1.9 bitcast_dynamic-update-slice_fusion.5
  122.4 1.9 bitcast_dynamic-update-slice_fusion.5
  125.0 1.9 bitcast_dynamic-update-slice_fusion.5
  127.6 1.9 bitcast_dynamic-update-slice_fusion.5
  145.8 1.9 bitcast_dynamic-update-slice_fusion.5
  151.0 1.9 bitcast_dynamic-update-slice_fusion.5
  171.0 2.3 multiply_reduce_fusion
  174.8 13.4 %collective-permute-start.4 = (f32[8,384]{1,0:T(8,128)S(1)}, f32[8,384]{1,0:T(8,128)S(1)}, u32[]{:S(2)}, u32[]{:S(2)}) collective-permute-start(f32[8,384]{1,0:T(8,128)S(1)} %squeeze.95), channel_id=1, source_target_pairs={{0,508},{4,0},{8,4},{12,8},{16,12},{20,16},{24,20},{28,24},{32,28}... | collective-permute-start | bytes 36872 | tf_op jit(solution)/shard_map/ppermute | solution.py:12
  188.3 1.9 collective-permute-start.5
  190.3 1.9 collective-permute-start.6
  192.3 7.8 %collective-permute-start.7 = (f32[8,384]{1,0:T(8,128)S(1)}, f32[8,384]{1,0:T(8,128)S(1)}, u32[]{:S(2)}, u32[]{:S(2)}) collective-permute-start(f32[8,384]{1,0:T(8,128)S(1)} %squeeze.98), channel_id=1, source_target_pairs={{0,32},{4,36},{8,40},{12,44},{16,48},{20,52},{24,56},{28,60},{32,6... | collective-permute-start | bytes 36872 | tf_op jit(solution)/shard_map/ppermute | solution.py:12
  201.1 417.3 %psum.33 = f32[16]{0:T(128)} all-reduce(f32[16]{0:T(128)S(1)} %add.136), channel_id=1, replica_groups=mesh['sub'=128,'scen'=4] {'sub'}, use_global_device_ids=true, to_apply=%region_10.11 | all-reduce | flops 16 | bytes 128 | tf_op jit(solution)/shard_map/psum | solution.py:124
  618.5 10.8 %psum.32 = f32[16]{0:T(128)} all-reduce(f32[16]{0:T(128)S(1)} %add.135), channel_id=1, replica_groups=mesh['sub'=128,'scen'=4] {'scen'}, use_global_device_ids=true, to_apply=%region_5.6 | all-reduce | flops 16 | bytes 128 | tf_op jit(solution)/shard_map/psum | solution.py:123
  (262 shorter events, 107.5 us)
Async XLA Ops:
  3.6 5.6 copy-start.24
  6.0 2.5 copy-start.20
  8.4 2.8 copy-start.29
  9.2 49.7 %copy-start.11 = (pred[1024,32]{0,1:T(8,128)(4,1)}, pred[1024,32]{0,1:T(8,128)(4,1)S(1)}, u32[]{:S(2)}) copy-start(pred[1024,32]{0,1:T(8,128)(4,1)S(1)} %iota_compare_fusion.5) | copy-start | bytes 98308
  9.2 3.4 copy-start.26
  9.2 3.4 copy-start
  9.2 3.4 copy-start.3
  9.2 3.4 copy-start.9
  12.6 46.2 %copy-start.28 = (s32[1,16]{1,0:T(1,128)S(1)}, s32[1,16]{1,0:T(1,128)}, u32[]{:S(2)}) copy-start(s32[1,16]{1,0:T(1,128)} %param.27) | copy-start | bytes 196
  61.8 29.5 %copy-start.8 = (f32[1,48,16,16]{1,3,2,0:T(8,128)S(1)}, f32[1,48,16,16]{1,3,2,0:T(8,128)}, u32[]{:S(2)}) copy-start(f32[1,48,16,16]{1,3,2,0:T(8,128)} %param.28) | copy-start | bytes 147460
  61.8 30.2 %copy-start.21 = (f32[48,16]{0,1:T(8,128)S(1)}, f32[48,16]{0,1:T(8,128)}, u32[]{:S(2)}) copy-start(f32[48,16]{0,1:T(8,128)} %param.31) | copy-start | bytes 9220
  62.0 30.1 %copy-start.22 = (f32[24,16]{0,1:T(8,128)S(1)}, f32[24,16]{0,1:T(8,128)}, u32[]{:S(2)}) copy-start(f32[24,16]{0,1:T(8,128)} %get-tuple-element.466) | copy-start | bytes 4612
  63.5 33.2 %collective-permute-start = (f32[8,384]{1,0:T(8,128)}, f32[8,384]{1,0:T(8,128)S(1)}, u32[]{:S(2)}, u32[]{:S(2)}) collective-permute-start(f32[8,384]{1,0:T(8,128)} %squeeze.91), channel_id=1, source_target_pairs={{0,508},{4,0},{8,4},{12,8},{16,12},{20,16},{24,20},{28,24},{32,28}... | collective-permute-start | bytes 36872 | tf_op jit(solution)/shard_map/ppermute | solution.py:12
  78.1 18.7 %collective-permute-start.1 = (f32[8,384]{1,0:T(8,128)S(1)}, f32[8,384]{1,0:T(8,128)S(1)}, u32[]{:S(2)}, u32[]{:S(2)}) collective-permute-start(f32[8,384]{1,0:T(8,128)S(1)} %squeeze.92), channel_id=1, source_target_pairs={{0,4},{4,8},{8,12},{12,16},{16,20},{20,24},{24,28},{28,32},{32,36}... | collective-permute-start | bytes 36872 | tf_op jit(solution)/shard_map/ppermute | solution.py:12
  80.8 16.3 %collective-permute-start.2 = (f32[8,384]{1,0:T(8,128)}, f32[8,384]{1,0:T(8,128)}, u32[]{:S(2)}, u32[]{:S(2)}) collective-permute-start(f32[8,384]{1,0:T(8,128)} %squeeze.93), channel_id=1, source_target_pairs={{0,480},{4,484},{8,488},{12,492},{16,496},{20,500},{24,504},{28,50... | collective-permute-start | bytes 36872 | tf_op jit(solution)/shard_map/ppermute | solution.py:12
  86.2 16.5 %collective-permute-start.3 = (f32[8,384]{1,0:T(8,128)S(1)}, f32[8,384]{1,0:T(8,128)}, u32[]{:S(2)}, u32[]{:S(2)}) collective-permute-start(f32[8,384]{1,0:T(8,128)S(1)} %squeeze.94), channel_id=1, source_target_pairs={{0,32},{4,36},{8,40},{12,44},{16,48},{20,52},{24,56},{28,60},{32,6... | collective-permute-start | bytes 36872 | tf_op jit(solution)/shard_map/ppermute | solution.py:12
  95.1 10.2 %copy-start.25 = (s32[32]{0:T(128)S(1)}, s32[32]{0:T(128)}, u32[]{:S(2)}) copy-start(s32[32]{0:T(128)} %copy-done.24) | copy-start | bytes 388
  95.1 10.2 %copy-start.27 = (f32[32]{0:T(128)S(1)}, f32[32]{0:T(128)}, u32[]{:S(2)}) copy-start(f32[32]{0:T(128)} %copy-done.26) | copy-start | bytes 388
  97.9 7.2 %copy-start.4 = (f32[1,8,24,16]{2,3,1,0:T(8,128)}, f32[1,8,24,16]{2,3,1,0:T(8,128)S(1)}, u32[]{:S(2)}) copy-start(f32[1,8,24,16]{2,3,1,0:T(8,128)S(1)} %copy.48) | copy-start | bytes 36868
  108.7 62.3 %copy-start.13 = (f32[16,1024]{1,0:T(8,128)S(1)}, f32[16,1024]{1,0:T(8,128)}, u32[]{:S(2)}) copy-start(f32[16,1024]{1,0:T(8,128)} %fusion.55) | copy-start | bytes 196612
  171.0 2.4 copy-start.1
  171.0 2.4 copy-start.12
  174.3 25.9 %copy-start.16 = (f32[384,16]{0,1:T(8,128)S(1)}, f32[384,16]{0,1:T(8,128)}, u32[]{:S(2)}) copy-start(f32[384,16]{0,1:T(8,128)} %squeeze.100) | copy-start | bytes 73732
  174.3 25.9 %copy-start.17 = (f32[384,16]{0,1:T(8,128)S(1)}, f32[384,16]{0,1:T(8,128)}, u32[]{:S(2)}) copy-start(f32[384,16]{0,1:T(8,128)} %squeeze.99) | copy-start | bytes 73732
  174.3 26.8 %copy-start.18 = (f32[24,16]{1,0:T(8,128)S(1)}, f32[24,16]{1,0:T(8,128)}, u32[]{:S(2)}) copy-start(f32[24,16]{1,0:T(8,128)} %copy.62) | copy-start | bytes 4612
  174.3 26.8 %copy-start.19 = (f32[24,16]{1,0:T(8,128)S(1)}, f32[24,16]{1,0:T(8,128)}, u32[]{:S(2)}) copy-start(f32[24,16]{1,0:T(8,128)} %copy.63) | copy-start | bytes 4612
  174.5 455.5 %copy-start.5 = (f32[1,8,24,16]{2,3,1,0:T(8,128)S(1)}, f32[1,8,24,16]{2,3,1,0:T(8,128)}, u32[]{:S(2)}) copy-start(f32[1,8,24,16]{2,3,1,0:T(8,128)} %copy-done.4) | copy-start | bytes 36868
  174.5 455.5 %copy-start.7 = (f32[1,8,24,16]{2,3,1,0:T(8,128)S(1)}, f32[1,8,24,16]{2,3,1,0:T(8,128)}, u32[]{:S(2)}) copy-start(f32[1,8,24,16]{2,3,1,0:T(8,128)} %copy-done.6) | copy-start | bytes 36868
  174.8 454.5 %collective-permute-start.4 = (f32[8,384]{1,0:T(8,128)S(1)}, f32[8,384]{1,0:T(8,128)S(1)}, u32[]{:S(2)}, u32[]{:S(2)}) collective-permute-start(f32[8,384]{1,0:T(8,128)S(1)} %squeeze.95), channel_id=1, source_target_pairs={{0,508},{4,0},{8,4},{12,8},{16,12},{20,16},{24,20},{28,24},{32,28}... | collective-permute-start | bytes 36872 | tf_op jit(solution)/shard_map/ppermute | solution.py:12
  188.3 441.1 %collective-permute-start.5 = (f32[8,384]{1,0:T(8,128)S(1)}, f32[8,384]{1,0:T(8,128)S(1)}, u32[]{:S(2)}, u32[]{:S(2)}) collective-permute-start(f32[8,384]{1,0:T(8,128)S(1)} %squeeze.96), channel_id=1, source_target_pairs={{0,4},{4,8},{8,12},{12,16},{16,20},{20,24},{24,28},{28,32},{32,36}... | collective-permute-start | bytes 36872 | tf_op jit(solution)/shard_map/ppermute | solution.py:12
  190.3 439.3 %collective-permute-start.6 = (f32[8,384]{1,0:T(8,128)S(1)}, f32[8,384]{1,0:T(8,128)S(1)}, u32[]{:S(2)}, u32[]{:S(2)}) collective-permute-start(f32[8,384]{1,0:T(8,128)S(1)} %squeeze.97), channel_id=1, source_target_pairs={{0,480},{4,484},{8,488},{12,492},{16,496},{20,500},{24,504},{28,50... | collective-permute-start | bytes 36872 | tf_op jit(solution)/shard_map/ppermute | solution.py:12
  192.3 437.4 %collective-permute-start.7 = (f32[8,384]{1,0:T(8,128)S(1)}, f32[8,384]{1,0:T(8,128)S(1)}, u32[]{:S(2)}, u32[]{:S(2)}) collective-permute-start(f32[8,384]{1,0:T(8,128)S(1)} %squeeze.98), channel_id=1, source_target_pairs={{0,32},{4,36},{8,40},{12,44},{16,48},{20,52},{24,56},{28,60},{32,6... | collective-permute-start | bytes 36872 | tf_op jit(solution)/shard_map/ppermute | solution.py:12
  (6 other events, 10.4 us)
where the time goes:
time: 635 us; the launch traced here: 631 us
  blocking collectives  428 us (67%)
  matrix products  102 us (16%)
  starting transfers between devices  51.3 us (8%)
  local copies, waits for them, and re-layouts  35.8 us (6%)
  other arithmetic  7.83 us (1%)
    psum x1, blocking collectives, body(): fault_local = fault_local + lax.psum(fault_term, 'sub')  417 us
    dot_general x48, matrix products, one_step(): jnp.dot(right_side.astype(jnp.bfloat16), weights, preferred_element_type=...  91.4 us
    ppermute x8, starting transfers between devices, passed_along(): return lax.ppermute(value, axis, pairs)  51.3 us
    mul x48, local copies, waits for them, and re-layouts, one_step(): current_now[:, None] * fault_table  16.6 us
  transfers between devices with their start and end apart: 8, of which 1 were waited for; matrix products, arithmetic and copies ran while one was open for 2% of the time, Pallas kernels for 0%

commit v1 on v0

--- a/solution.py
+++ b/solution.py
@@ -1,9 +1,21 @@
 import jax
 import jax.numpy as jnp
+import numpy as np
+from jax.sharding import Mesh
 from jax import lax
 from jax.sharding import PartitionSpec as P
 
 PRECISE = lax.Precision.HIGHEST
+
+
+SUB = ("z_hi", "x", "y", "core")
+SUB_SIZES = (2, 4, 8, 2)
+
+
+def sum_over_sub(value):
+    for axis in reversed(SUB):
+        value = lax.psum(value, axis)
+    return value
 
 
 def passed_along(value, axis, steps):
@@ -35,11 +47,11 @@
     conv_count = conv_node.shape[1]
     block_len = later_history.shape[3] // 2
     blocks = objective_grad.shape[0] // block_len
-    sub_count = lax.axis_size("sub")
+    sub_count = lax.axis_size(SUB)
     grid_width = max(2, sub_count // 16)
     offsets = (1, -1, grid_width, -grid_width)
     opposite = (1, 0, 3, 2)
-    sub_index = lax.axis_index("sub")
+    sub_index = lax.axis_index(SUB)
     weights = inverse_matrix[0]
     live_mask = (lax.iota(jnp.int32, slot_count)[None, :] < line_count[0][:, None]).astype(
         jnp.float32
@@ -121,10 +133,10 @@
             axis=0,
         )
         control_local = control_local + lax.psum(control_term, "scen")
-        fault_local = fault_local + lax.psum(fault_term, "sub")
+        fault_local = fault_local + fault_term
         received = jnp.stack(
             [
-                passed_along(outbound[opposite[direction]], "sub", -offsets[direction])
+                passed_along(outbound[opposite[direction]], SUB, -offsets[direction])
                 for direction in range(4)
             ]
         )
@@ -132,33 +144,37 @@
             [received.reshape(4, slot_count, block_len, scen_rows), window[:, :, :block_len]],
             axis=2,
         )
+    fault_local = sum_over_sub(fault_local)
     return (adjoint_next[None], window[None], control_local[None], fault_local)
 
 
 def solution(mesh):
+    sub_mesh = Mesh(
+        np.asarray(mesh.devices).reshape(SUB_SIZES + (mesh.shape["scen"],)), SUB + ("scen",)
+    )
     return jax.shard_map(
         body,
-        mesh=mesh,
+        mesh=sub_mesh,
         in_specs=(
-            P("sub", None, None),
-            P(None, "sub", "scen", None),
-            P("sub", "scen", None),
-            P("sub", None),
-            P("sub", None, None),
-            P("sub", None),
-            P("sub", None, None),
-            P("sub", None, None),
-            P("sub", None, None, None, "scen"),
-            P("sub", None),
-            P("sub", None, "scen", None),
+            P(SUB, None, None),
+            P(None, SUB, "scen", None),
+            P(SUB, "scen", None),
+            P(SUB, None),
+            P(SUB, None, None),
+            P(SUB, None),
+            P(SUB, None, None),
+            P(SUB, None, None),
+            P(SUB, None, None, None, "scen"),
+            P(SUB, None),
+            P(SUB, None, "scen", None),
             P("scen"),
             P(None, "scen"),
             P(None, "scen"),
         ),
         out_specs=(
-            P("sub", "scen", None),
-            P("sub", None, None, None, "scen"),
-            P("sub", None),
+            P(SUB, "scen", None),
+            P(SUB, None, None, None, "scen"),
+            P(SUB, None),
             P("scen"),
         ),
         check_vma=False,

time: 635 us -> 262 us (0.41)
  the two profiles are of different devices: /device:TPU:64 before, /device:TPU:4 now
where the time goes in v1:
time: 262 us; the launch traced here: 258 us
  matrix products  101 us (39%)
  blocking collectives  77.8 us (30%)
  local copies, waits for them, and re-layouts  35.8 us (14%)
  starting transfers between devices  34.2 us (13%)
  other arithmetic  7.85 us (3%)
    dot_general x48, matrix products, one_step(): jnp.dot(right_side.astype(jnp.bfloat16), weights, preferred_element_type=...  91 us
    psum x4, blocking collectives, sum_over_sub(): value = lax.psum(value, axis)  65.6 us
    ppermute x8, starting transfers between devices, passed_along(): return lax.ppermute(value, axis, pairs)  34.2 us
    mul x48, local copies, waits for them, and re-layouts, one_step(): current_now[:, None] * fault_table  16.5 us
    psum x1, blocking collectives, body(): control_local = control_local + lax.psum(control_term, 'scen')  12.1 us
  transfers between devices with their start and end apart: 8, of which 0 were waited for; matrix products, arithmetic and copies ran while one was open for 4% of the time, Pallas kernels for 0%

profile of v1, /device:TPU:4, one launch (start us, length us, event | category | flops | bytes accessed | tf_op | source)
XLA Modules:
  0.0 258.3 jit_solution(13217957040212197619)
XLA Ops:
  6.0 2.5 slice_bitcast_fusion
  9.3 2.0 fusion.45
  12.7 45.9 %while.34 = (s32[]{:T(128)}, f32[16,1024]{1,0:T(8,128)S(1)}, f32[24,16,1024]{2,1,0:T(8,128)}, bf16[24,16,1024]{2,1,0:T(8,128)(2,1)}, f32[1,1024]{1,0:T(1,128)S(1...) while((s32[]{:T(128)}, f32[16,1024]{1,0:T(8,128)S(1)}, ...), condition=%wide.region_1.2_spmd.clone, body=%wide.region_0.1_spmd.clone.sunk | while | flops 33685504 | bytes 2528637 | solution.py:105
  12.7 1.9 bitcast_dynamic-update-slice_fusion.4
  20.4 1.9 bitcast_dynamic-update-slice_fusion.4
  24.2 1.9 bitcast_dynamic-update-slice_fusion.4
  29.9 1.9 bitcast_dynamic-update-slice_fusion.4
  41.4 1.9 bitcast_dynamic-update-slice_fusion.4
  45.2 1.9 bitcast_dynamic-update-slice_fusion.4
  51.0 1.9 bitcast_dynamic-update-slice_fusion.4
  52.9 1.9 bitcast_dynamic-update-slice_fusion.4
  54.8 1.9 bitcast_dynamic-update-slice_fusion.4
  56.7 1.9 bitcast_dynamic-update-slice_fusion.4
  58.7 2.3 fusion.57
  63.4 4.8 %collective-permute-start = (f32[8,384]{1,0:T(8,128)}, f32[8,384]{1,0:T(8,128)S(1)}, u32[]{:S(2)}, u32[]{:S(2)}) collective-permute-start(f32[8,384]{1,0:T(8,128)} %squeeze.91), channel_id=1, source_target_pairs={{0,508},{4,0},{8,4},{12,8},{16,12},{20,16},{24,20},{28,24},{32,28}... | collective-permute-start | bytes 36872 | tf_op jit(solution)/shard_map/ppermute | solution.py:24
  68.2 1.9 collective-permute-start.1
  70.8 5.3 %collective-permute-start.2 = (f32[8,384]{1,0:T(8,128)}, f32[8,384]{1,0:T(8,128)}, u32[]{:S(2)}, u32[]{:S(2)}) collective-permute-start(f32[8,384]{1,0:T(8,128)} %squeeze.93), channel_id=1, source_target_pairs={{0,480},{4,484},{8,488},{12,492},{16,496},{20,500},{24,504},{28,50... | collective-permute-start | bytes 36872 | tf_op jit(solution)/shard_map/ppermute | solution.py:24
  76.3 4.4 %collective-permute-start.3 = (f32[8,384]{1,0:T(8,128)S(1)}, f32[8,384]{1,0:T(8,128)}, u32[]{:S(2)}, u32[]{:S(2)}) collective-permute-start(f32[8,384]{1,0:T(8,128)S(1)} %squeeze.94), channel_id=1, source_target_pairs={{0,32},{4,36},{8,40},{12,44},{16,48},{20,52},{24,56},{28,60},{32,6... | collective-permute-start | bytes 36872 | tf_op jit(solution)/shard_map/ppermute | solution.py:24
  90.7 2.0 fusion.43
  94.1 62.0 %while.35 = (s32[]{:T(128)}, f32[16,1024]{1,0:T(8,128)S(1)}, f32[24,16,1024]{2,1,0:T(8,128)}, bf16[24,16,1024]{2,1,0:T(8,128)(2,1)S(1)}, f32[1,1024]{1,0:T(1,128...) while((s32[]{:T(128)}, f32[16,1024]{1,0:T(8,128)S(1)}, ...), condition=%wide.region_3.4_spmd.clone, body=%wide.region_2.3_spmd.clone.sunk | while | flops 33685504 | bytes 2529533 | solution.py:105
  125.8 1.9 bitcast_dynamic-update-slice_fusion.5
  141.3 1.9 bitcast_dynamic-update-slice_fusion.5
  156.1 2.3 multiply_reduce_fusion
  159.9 6.1 %collective-permute-start.4 = (f32[8,384]{1,0:T(8,128)S(1)}, f32[8,384]{1,0:T(8,128)S(1)}, u32[]{:S(2)}, u32[]{:S(2)}) collective-permute-start(f32[8,384]{1,0:T(8,128)S(1)} %squeeze.95), channel_id=1, source_target_pairs={{0,508},{4,0},{8,4},{12,8},{16,12},{20,16},{24,20},{28,24},{32,28}... | collective-permute-start | bytes 36872 | tf_op jit(solution)/shard_map/ppermute | solution.py:24
  166.1 1.9 collective-permute-start.5
  168.1 3.0 %collective-permute-start.6 = (f32[8,384]{1,0:T(8,128)S(1)}, f32[8,384]{1,0:T(8,128)S(1)}, u32[]{:S(2)}, u32[]{:S(2)}) collective-permute-start(f32[8,384]{1,0:T(8,128)S(1)} %squeeze.97), channel_id=1, source_target_pairs={{0,480},{4,484},{8,488},{12,492},{16,496},{20,500},{24,504},{28,50... | collective-permute-start | bytes 36872 | tf_op jit(solution)/shard_map/ppermute | solution.py:24
  171.3 6.7 %collective-permute-start.7 = (f32[8,384]{1,0:T(8,128)S(1)}, f32[8,384]{1,0:T(8,128)S(1)}, u32[]{:S(2)}, u32[]{:S(2)}) collective-permute-start(f32[8,384]{1,0:T(8,128)S(1)} %squeeze.98), channel_id=1, source_target_pairs={{0,32},{4,36},{8,40},{12,44},{16,48},{20,52},{24,56},{28,60},{32,6... | collective-permute-start | bytes 36872 | tf_op jit(solution)/shard_map/ppermute | solution.py:24
  178.9 2.5 psum.44
  181.4 18.4 %psum.45 = f32[16]{0:T(128)S(1)} all-reduce(f32[16]{0:T(128)S(1)} %psum.44), channel_id=1, replica_groups=mesh['z_hi'=2,'x'=4,'y'=8,'core'=2,'scen'=4] {'y'}, use_global_device_ids=true, to_apply=%region_13.14 | all-reduce | flops 16 | bytes 128 | tf_op jit(solution)/shard_map/psum | solution.py:17
  199.8 32.4 %psum.46 = f32[16]{0:T(128)S(1)} all-reduce(f32[16]{0:T(128)S(1)} %psum.45), channel_id=1, replica_groups=mesh['z_hi'=2,'x'=4,'y'=8,'core'=2,'scen'=4] {'x'}, use_global_device_ids=true, to_apply=%region_14.15 | all-reduce | flops 16 | bytes 128 | tf_op jit(solution)/shard_map/psum | solution.py:17
  232.2 12.4 %psum.47 = f32[16]{0:T(128)} all-reduce(f32[16]{0:T(128)S(1)} %psum.46), channel_id=1, replica_groups=mesh['z_hi'=2,'x'=4,'y'=8,'core'=2,'scen'=4] {'z_hi'}, use_global_device_ids=true, to_apply=%region_15.16 | all-reduce | flops 16 | bytes 128 | tf_op jit(solution)/shard_map/psum | solution.py:17
  244.6 12.1 %psum.48 = f32[16]{0:T(128)} all-reduce(f32[16]{0:T(128)S(1)} %add.151), channel_id=1, replica_groups=mesh['z_hi'=2,'x'=4,'y'=8,'core'=2,'scen'=4] {'scen'}, use_global_device_ids=true, to_apply=%region_5.6 | all-reduce | flops 16 | bytes 128 | tf_op jit(solution)/shard_map/psum | solution.py:135
  (265 shorter events, 111.0 us)
Async XLA Ops:
  3.6 5.7 %copy-start.24 = (s32[32]{0:T(128)}, s32[32]{0:T(128)S(1)}, u32[]{:S(2)}) copy-start(s32[32]{0:T(128)S(1)} %eq.71) | copy-start | bytes 388
  6.0 2.5 copy-start.20
  6.0 3.3 %copy-start.29 = (s32[16]{0:T(128)S(1)}, s32[16]{0:T(128)}, u32[]{:S(2)}) copy-start(s32[16]{0:T(128)} %param.29) | copy-start | bytes 196
  9.2 49.5 %copy-start.11 = (pred[1024,32]{0,1:T(8,128)(4,1)}, pred[1024,32]{0,1:T(8,128)(4,1)S(1)}, u32[]{:S(2)}) copy-start(pred[1024,32]{0,1:T(8,128)(4,1)S(1)} %iota_compare_fusion.5) | copy-start | bytes 98308
  9.3 3.4 %copy-start.26 = (f32[32]{0:T(128)}, f32[32]{0:T(128)S(1)}, u32[]{:S(2)}) copy-start(f32[32]{0:T(128)S(1)} %broadcast_select_fusion) | copy-start | bytes 388
  9.3 3.4 %copy-start = (bf16[1,1024,1024]{2,1,0:T(8,128)(2,1)S(1)}, bf16[1,1024,1024]{2,1,0:T(8,128)(2,1)}, u32[]{:S(2)}) copy-start(bf16[1,1024,1024]{2,1,0:T(8,128)(2,1)} %param.18) | copy-start | bytes 6291460
  9.3 3.4 %copy-start.3 = (f32[1,16,1024]{2,1,0:T(8,128)S(1)}, f32[1,16,1024]{2,1,0:T(8,128)}, u32[]{:S(2)}) copy-start(f32[1,16,1024]{2,1,0:T(8,128)} %param.20) | copy-start | bytes 196612
  9.3 3.4 %copy-start.9 = (f32[1,1024]{1,0:T(1,128)S(1)}, f32[1,1024]{1,0:T(1,128)}, u32[]{:S(2)}) copy-start(f32[1,1024]{1,0:T(1,128)} %param.21) | copy-start | bytes 12292
  12.7 45.9 %copy-start.28 = (s32[1,16]{1,0:T(1,128)S(1)}, s32[1,16]{1,0:T(1,128)}, u32[]{:S(2)}) copy-start(s32[1,16]{1,0:T(1,128)} %param.27) | copy-start | bytes 196
  61.6 19.8 %copy-start.8 = (f32[1,48,16,16]{1,3,2,0:T(8,128)S(1)}, f32[1,48,16,16]{1,3,2,0:T(8,128)}, u32[]{:S(2)}) copy-start(f32[1,48,16,16]{1,3,2,0:T(8,128)} %param.28) | copy-start | bytes 147460
  61.6 20.4 %copy-start.21 = (f32[48,16]{0,1:T(8,128)S(1)}, f32[48,16]{0,1:T(8,128)}, u32[]{:S(2)}) copy-start(f32[48,16]{0,1:T(8,128)} %param.31) | copy-start | bytes 9220
  61.8 20.3 %copy-start.22 = (f32[24,16]{0,1:T(8,128)S(1)}, f32[24,16]{0,1:T(8,128)}, u32[]{:S(2)}) copy-start(f32[24,16]{0,1:T(8,128)} %get-tuple-element.466) | copy-start | bytes 4612
  63.4 23.4 %collective-permute-start = (f32[8,384]{1,0:T(8,128)}, f32[8,384]{1,0:T(8,128)S(1)}, u32[]{:S(2)}, u32[]{:S(2)}) collective-permute-start(f32[8,384]{1,0:T(8,128)} %squeeze.91), channel_id=1, source_target_pairs={{0,508},{4,0},{8,4},{12,8},{16,12},{20,16},{24,20},{28,24},{32,28}... | collective-permute-start | bytes 36872 | tf_op jit(solution)/shard_map/ppermute | solution.py:24
  68.2 18.7 %collective-permute-start.1 = (f32[8,384]{1,0:T(8,128)S(1)}, f32[8,384]{1,0:T(8,128)S(1)}, u32[]{:S(2)}, u32[]{:S(2)}) collective-permute-start(f32[8,384]{1,0:T(8,128)S(1)} %squeeze.92), channel_id=1, source_target_pairs={{0,4},{4,8},{8,12},{12,16},{16,20},{20,24},{24,28},{28,32},{32,36}... | collective-permute-start | bytes 36872 | tf_op jit(solution)/shard_map/ppermute | solution.py:24
  70.8 16.3 %collective-permute-start.2 = (f32[8,384]{1,0:T(8,128)}, f32[8,384]{1,0:T(8,128)}, u32[]{:S(2)}, u32[]{:S(2)}) collective-permute-start(f32[8,384]{1,0:T(8,128)} %squeeze.93), channel_id=1, source_target_pairs={{0,480},{4,484},{8,488},{12,492},{16,496},{20,500},{24,504},{28,50... | collective-permute-start | bytes 36872 | tf_op jit(solution)/shard_map/ppermute | solution.py:24
  76.3 11.8 %collective-permute-start.3 = (f32[8,384]{1,0:T(8,128)S(1)}, f32[8,384]{1,0:T(8,128)}, u32[]{:S(2)}, u32[]{:S(2)}) collective-permute-start(f32[8,384]{1,0:T(8,128)S(1)} %squeeze.94), channel_id=1, source_target_pairs={{0,32},{4,36},{8,40},{12,44},{16,48},{20,52},{24,56},{28,60},{32,6... | collective-permute-start | bytes 36872 | tf_op jit(solution)/shard_map/ppermute | solution.py:24
  85.2 5.5 %copy-start.25 = (s32[32]{0:T(128)S(1)}, s32[32]{0:T(128)}, u32[]{:S(2)}) copy-start(s32[32]{0:T(128)} %copy-done.24) | copy-start | bytes 388
  85.2 5.5 %copy-start.27 = (f32[32]{0:T(128)S(1)}, f32[32]{0:T(128)}, u32[]{:S(2)}) copy-start(f32[32]{0:T(128)} %copy-done.26) | copy-start | bytes 388
  88.1 2.5 copy-start.4
  94.1 62.0 %copy-start.13 = (f32[16,1024]{1,0:T(8,128)S(1)}, f32[16,1024]{1,0:T(8,128)}, u32[]{:S(2)}) copy-start(f32[16,1024]{1,0:T(8,128)} %fusion.55) | copy-start | bytes 196612
  156.1 2.4 copy-start.1
  156.1 2.4 copy-start.12
  159.4 18.6 %copy-start.16 = (f32[384,16]{0,1:T(8,128)S(1)}, f32[384,16]{0,1:T(8,128)}, u32[]{:S(2)}) copy-start(f32[384,16]{0,1:T(8,128)} %squeeze.100) | copy-start | bytes 73732
  159.4 18.6 %copy-start.17 = (f32[384,16]{0,1:T(8,128)S(1)}, f32[384,16]{0,1:T(8,128)}, u32[]{:S(2)}) copy-start(f32[384,16]{0,1:T(8,128)} %squeeze.99) | copy-start | bytes 73732
  159.4 19.4 %copy-start.18 = (f32[24,16]{1,0:T(8,128)S(1)}, f32[24,16]{1,0:T(8,128)}, u32[]{:S(2)}) copy-start(f32[24,16]{1,0:T(8,128)} %copy.62) | copy-start | bytes 4612
  159.4 19.4 %copy-start.19 = (f32[24,16]{1,0:T(8,128)S(1)}, f32[24,16]{1,0:T(8,128)}, u32[]{:S(2)}) copy-start(f32[24,16]{1,0:T(8,128)} %copy.63) | copy-start | bytes 4612
  159.6 97.8 %copy-start.5 = (f32[1,8,24,16]{2,3,1,0:T(8,128)S(1)}, f32[1,8,24,16]{2,3,1,0:T(8,128)}, u32[]{:S(2)}) copy-start(f32[1,8,24,16]{2,3,1,0:T(8,128)} %copy-done.4) | copy-start | bytes 36868
  159.6 97.8 %copy-start.7 = (f32[1,8,24,16]{2,3,1,0:T(8,128)S(1)}, f32[1,8,24,16]{2,3,1,0:T(8,128)}, u32[]{:S(2)}) copy-start(f32[1,8,24,16]{2,3,1,0:T(8,128)} %copy-done.6) | copy-start | bytes 36868
  159.9 96.8 %collective-permute-start.4 = (f32[8,384]{1,0:T(8,128)S(1)}, f32[8,384]{1,0:T(8,128)S(1)}, u32[]{:S(2)}, u32[]{:S(2)}) collective-permute-start(f32[8,384]{1,0:T(8,128)S(1)} %squeeze.95), channel_id=1, source_target_pairs={{0,508},{4,0},{8,4},{12,8},{16,12},{20,16},{24,20},{28,24},{32,28}... | collective-permute-start | bytes 36872 | tf_op jit(solution)/shard_map/ppermute | solution.py:24
  166.1 90.8 %collective-permute-start.5 = (f32[8,384]{1,0:T(8,128)S(1)}, f32[8,384]{1,0:T(8,128)S(1)}, u32[]{:S(2)}, u32[]{:S(2)}) collective-permute-start(f32[8,384]{1,0:T(8,128)S(1)} %squeeze.96), channel_id=1, source_target_pairs={{0,4},{4,8},{8,12},{12,16},{16,20},{20,24},{24,28},{28,32},{32,36}... | collective-permute-start | bytes 36872 | tf_op jit(solution)/shard_map/ppermute | solution.py:24
  168.1 88.9 %collective-permute-start.6 = (f32[8,384]{1,0:T(8,128)S(1)}, f32[8,384]{1,0:T(8,128)S(1)}, u32[]{:S(2)}, u32[]{:S(2)}) collective-permute-start(f32[8,384]{1,0:T(8,128)S(1)} %squeeze.97), channel_id=1, source_target_pairs={{0,480},{4,484},{8,488},{12,492},{16,496},{20,500},{24,504},{28,50... | collective-permute-start | bytes 36872 | tf_op jit(solution)/shard_map/ppermute | solution.py:24
  171.3 86.0 %collective-permute-start.7 = (f32[8,384]{1,0:T(8,128)S(1)}, f32[8,384]{1,0:T(8,128)S(1)}, u32[]{:S(2)}, u32[]{:S(2)}) collective-permute-start(f32[8,384]{1,0:T(8,128)S(1)} %squeeze.98), channel_id=1, source_target_pairs={{0,32},{4,36},{8,40},{12,44},{16,48},{20,52},{24,56},{28,60},{32,6... | collective-permute-start | bytes 36872 | tf_op jit(solution)/shard_map/ppermute | solution.py:24
  (6 other events, 10.4 us)

commit v2 on v1

--- a/solution.py
+++ b/solution.py
@@ -2,6 +2,7 @@
 import jax.numpy as jnp
 import numpy as np
 from jax.sharding import Mesh
+from jax.experimental import pallas as pl
 from jax import lax
 from jax.sharding import PartitionSpec as P
 
@@ -16,6 +17,40 @@
     for axis in reversed(SUB):
         value = lax.psum(value, axis)
     return value
+
+
+def block_scan_kernel(
+    grad_ref, inflow_ref, current_ref, fault_ref, companion_ref, start_ref, weights_ref, out_ref, last_ref
+):
+    steps = grad_ref.shape[0]
+    companion = companion_ref[...]
+    fault_table = fault_ref[...]
+
+    def one_step(index, adjoint_prev):
+        step = steps - 1 - index
+        right_side = (
+            grad_ref[step].astype(jnp.float32)
+            + companion * adjoint_prev
+            + inflow_ref[step]
+            + current_ref[step] * fault_table
+        )
+        adjoint = jnp.dot(
+            right_side.astype(jnp.bfloat16), weights_ref[...], preferred_element_type=jnp.float32
+        )
+        out_ref[step] = adjoint
+        return adjoint
+
+    last_ref[...] = lax.fori_loop(0, steps, one_step, start_ref[...])
+
+
+def block_scan(grad, inflow, current, fault_table, companion, start, weights):
+    return pl.pallas_call(
+        block_scan_kernel,
+        out_shape=(
+            jax.ShapeDtypeStruct(inflow.shape, jnp.float32),
+            jax.ShapeDtypeStruct(start.shape, jnp.float32),
+        ),
+    )(grad, inflow, current[:, :, None], fault_table, companion, start, weights)
 
 
 def passed_along(value, axis, steps):
@@ -76,18 +111,6 @@
     block_rows = lax.iota(jnp.int32, block_len)
     time_iota = lax.iota(jnp.int32, 2 * block_len)
 
-    def one_step(adjoint_prev, inputs):
-        grad_now, inflow_now, current_now = inputs
-        right_side = (
-            grad_now.astype(jnp.float32)
-            + companion[0][None, :] * adjoint_prev
-            + inflow_now
-            + current_now[:, None] * fault_table
-        )
-        adjoint = jnp.dot(
-            right_side.astype(jnp.bfloat16), weights, preferred_element_type=jnp.float32
-        )
-        return (adjoint, adjoint)
 
     for block_id in reversed(range(blocks)):
         block_start = block_id * block_len
@@ -102,15 +125,14 @@
         inflow = jnp.dot(picked, spread_table, precision=PRECISE).reshape(
             block_len, scen_rows, node_count
         )
-        adjoint_next, adjoint_block = lax.scan(
-            one_step,
+        adjoint_block, adjoint_next = block_scan(
+            objective_grad[block_start : block_start + block_len, 0],
+            inflow,
+            fault_current[block_start : block_start + block_len],
+            fault_table,
+            companion,
             adjoint_next,
-            (
-                objective_grad[block_start : block_start + block_len, 0],
-                inflow,
-                fault_current[block_start : block_start + block_len],
-            ),
-            reverse=True,
+            weights,
         )
         samples = jnp.dot(
             adjoint_block.reshape(block_len * scen_rows, node_count), pick_table, precision=PRECISE

time: 262 us -> 167 us (0.64); the launches traced: 258 us -> 166 us
  matrix products: 101 us -> 9.12 us
  Pallas kernels: 0 us -> 27.9 us
  local copies, waits for them, and re-layouts: 35.8 us -> 9.87 us
  waiting for transfers between devices: 0.02 us -> 3.73 us
  starting transfers between devices: 34.2 us -> 30.7 us
    dot_general x48 -> x0, matrix products: 91 us -> none  [one_step(): jnp.dot(right_side.astype(jnp.bfloat16), weights, preferred_element_type=...]
    pallas_call x0 -> x2, Pallas kernels: none -> 27.9 us  [block_scan(): pl.pallas_call(block_scan_kernel, out_shape=(jax.ShapeDtypeStruct(inflow....]
    mul x48 -> x0, local copies, waits for them, and re-layouts: 16.5 us -> none  [one_step(): current_now[:, None] * fault_table]
    ppermute x8, waiting for transfers between devices: 0.02 us -> 3.73 us  [passed_along(): return lax.ppermute(value, axis, pairs)]
    ppermute x8, starting transfers between devices: 34.2 us -> 30.7 us  [passed_along(): return lax.ppermute(value, axis, pairs)]
    another operation x2 -> x0, local copies, waits for them, and re-layouts: 2.67 us -> none
    unnamed x64 -> x18, local copies, waits for them, and re-layouts: 2.87 us -> 0.25 us
  transfers between devices with their start and end apart: 8 -> 8, of which waited for: 0 -> 1; matrix products, arithmetic and copies ran while one was open for 4% -> 2% of each run, Pallas kernels for 0% -> 0%
where the time goes in v2:
time: 167 us; the launch traced here: 166 us
  blocking collectives  77.7 us (47%)
  starting transfers between devices  30.7 us (18%)
  Pallas kernels  27.9 us (17%)
  local copies, waits for them, and re-layouts  9.87 us (6%)
  matrix products  9.12 us (5%)
  other arithmetic  6.04 us (4%)
  waiting for transfers between devices  3.73 us (2%)
    psum x4, blocking collectives, sum_over_sub(): value = lax.psum(value, axis)  65.6 us
    ppermute x8, starting transfers between devices, passed_along(): return lax.ppermute(value, axis, pairs)  30.7 us
    pallas_call x2, Pallas kernels, block_scan(): pl.pallas_call(block_scan_kernel, out_shape=(jax.ShapeDtypeStruct(inflow....  27.9 us
    psum x1, blocking collectives, body(): control_local = control_local + lax.psum(control_term, 'scen')  12.1 us
    dot_general x2, matrix products, body(): jnp.dot(picked, spread_table, precision=PRECISE)  3.94 us
    ppermute x8, waiting for transfers between devices, passed_along(): return lax.ppermute(value, axis, pairs)  3.73 us
  transfers between devices with their start and end apart: 8, of which 1 were waited for; matrix products, arithmetic and copies ran while one was open for 2% of the time, Pallas kernels for 0%

profile of v2, /device:TPU:4, one launch (start us, length us, event | category | flops | bytes accessed | tf_op | source)
XLA Modules:
  0.0 166.2 jit_solution(9547666143307935922)
XLA Ops:
  0.6 0.7 broadcast_subtract_fusion
  1.3 0.7 fusion.23.fault_ref
  2.0 0.7 fusion.32
  2.8 0.8 squeeze.51
  3.6 0.8 eq.71
  4.3 0.8 add_add_fusion
  5.1 1.4 fusion.1
  6.8 2.8 %slice_bitcast_fusion = (bf16[24,16,1024]{2,1,0:T(8,128)(2,1)}, bf16[24,16,1024]{2,1,0:T(8,128)(2,1)}) fusion(bf16[48,1,16,1024]{3,2,0,1:T(8,128)(2,1)} %bitcast.74), kind=kLoop, calls=%fused_computation.2 | loop fusion | bytes 3145728 | tf_op jit(solution)/shard_map/squeeze | solution.py:129
  9.6 0.9 copy.45.current_ref
  10.7 2.0 %fusion.13.inflow_ref = f32[24,16,1024]{2,1,0:T(8,128)} fusion(f32[24,16,32]{2,1,0:T(8,128)S(1)} %copy.44, f32[32]{0:T(128)S(1)} %broadcast_select_fusion, s32[32]{0:T(128)S(1)} %eq.71), kind=kOutput, calls=%fused_computation.21 | convolution fusion | flops 151040000 | bytes 1622272 | tf_op jit(solution)/shard_map/dot_general | solution.py:125
  12.6 13.9 %shard_map.165 = (f32[24,16,1024]{2,1,0:T(8,128)}, f32[16,1024]{1,0:T(8,128)}) custom-call(bf16[24,16,1024]{2,1,0:T(8,128)(2,1)} %get-tuple-element.14.grad_ref, f32[24,16,1024]{2,1,0:T(8,128)} %fusion.13.inflow_ref, f32[24,16,1]{2,1,0:T(8,128)} %copy.45.current_ref, f32[16,1024]{1,0:T(8,128)} %fusion.23.fault_ref, f32[1,1024]{1,0:T(1,128)} %companion_ref.3, ...), custom_call_target="tpu_custom_call" | custom-call | tf_op jit(solution)/shard_map/pallas_call | solution.py:47
  26.6 2.3 %fusion.25 = f32[384,48]{0,1:T(8,128)S(1)} fusion(f32[384,1024]{1,0:T(8,128)} %bitcast.72, pred[1024,16]{0,1:T(8,128)(4,1)S(1)} %iota_compare_fusion.6, pred[1024,32]{0,1:T(8,128)(4,1)S(1)} %iota_compare_fusion.3), kind=kOutput, calls=%fused_computation.37 | convolution fusion | flops 226541568 | bytes 1695744 | tf_op jit(solution)/shard_map/dot_general | solution.py:137
  29.3 4.8 %collective-permute-start = (f32[8,384]{1,0:T(8,128)S(1)}, f32[8,384]{1,0:T(8,128)S(1)}, u32[]{:S(2)}, u32[]{:S(2)}) collective-permute-start(f32[8,384]{1,0:T(8,128)S(1)} %squeeze.54), channel_id=1, source_target_pairs={{0,508},{4,0},{8,4},{12,8},{16,12},{20,16},{24,20},{28,24},{32,28}... | collective-permute-start | bytes 36872 | tf_op jit(solution)/shard_map/ppermute | solution.py:59
  34.2 1.9 %collective-permute-start.1 = (f32[8,384]{1,0:T(8,128)S(1)}, f32[8,384]{1,0:T(8,128)S(1)}, u32[]{:S(2)}, u32[]{:S(2)}) collective-permute-start(f32[8,384]{1,0:T(8,128)S(1)} %squeeze.55), channel_id=1, source_target_pairs={{0,4},{4,8},{8,12},{12,16},{16,20},{20,24},{24,28},{28,32},{32,36}... | collective-permute-start | bytes 36872 | tf_op jit(solution)/shard_map/ppermute | solution.py:59
  36.2 5.5 %collective-permute-start.2 = (f32[8,384]{1,0:T(8,128)S(1)}, f32[8,384]{1,0:T(8,128)S(1)}, u32[]{:S(2)}, u32[]{:S(2)}) collective-permute-start(f32[8,384]{1,0:T(8,128)S(1)} %squeeze.56), channel_id=1, source_target_pairs={{0,480},{4,484},{8,488},{12,492},{16,496},{20,500},{24,504},{28,50... | collective-permute-start | bytes 36872 | tf_op jit(solution)/shard_map/ppermute | solution.py:59
  41.8 4.4 %collective-permute-start.3 = (f32[8,384]{1,0:T(8,128)S(1)}, f32[8,384]{1,0:T(8,128)S(1)}, u32[]{:S(2)}, u32[]{:S(2)}) collective-permute-start(f32[8,384]{1,0:T(8,128)S(1)} %squeeze.57), channel_id=1, source_target_pairs={{0,32},{4,36},{8,40},{12,44},{16,48},{20,52},{24,56},{28,60},{32,6... | collective-permute-start | bytes 36872 | tf_op jit(solution)/shard_map/ppermute | solution.py:59
  46.4 0.9 copy.51.current_ref
  48.5 3.7 %collective-permute-done.3 = f32[8,384]{1,0:T(8,128)S(1)} collective-permute-done((f32[8,384]{1,0:T(8,128)S(1)}, f32[8,384]{1,0:T(8,128)S(1)}, u32[]{:S(2)}, u32[]{:S(2)}) %collective-permute-start.3) | collective-permute-done | bytes 12320 | tf_op jit(solution)/shard_map/ppermute | solution.py:59
  53.1 2.0 %fusion.11.inflow_ref = f32[24,16,1024]{2,1,0:T(8,128)} fusion(f32[24,16,32]{2,1,0:T(8,128)S(1)} %copy.50, f32[32]{0:T(128)S(1)} %broadcast_select_fusion, s32[32]{0:T(128)S(1)} %eq.71), kind=kOutput, calls=%fused_computation.19 | convolution fusion | flops 151040000 | bytes 1622272 | tf_op jit(solution)/shard_map/dot_general | solution.py:125
  55.1 14.0 %shard_map.166 = (f32[24,16,1024]{2,1,0:T(8,128)}, f32[16,1024]{1,0:T(8,128)}) custom-call(bf16[24,16,1024]{2,1,0:T(8,128)(2,1)} %get-tuple-element.15.grad_ref, f32[24,16,1024]{2,1,0:T(8,128)} %fusion.11.inflow_ref, f32[24,16,1]{2,1,0:T(8,128)} %copy.51.current_ref, f32[16,1024]{1,0:T(8,128)} %fusion.23.fault_ref, f32[1,1024]{1,0:T(1,128)} %companion_ref.3, ...), custom_call_target="tpu_custom_call" | custom-call | tf_op jit(solution)/shard_map/pallas_call | solution.py:47
  69.1 1.8 %multiply_reduce_fusion = (f32[24,16]{1,0:T(8,128)S(1)}, f32[24,16]{1,0:T(8,128)S(1)}) fusion(f32[24,16,1024]{2,1,0:T(8,128)} %get-tuple-element.11, f32[16,1024]{1,0:T(8,128)S(1)} %copy-done.2, f32[24,16,1024]{2,1,0:T(8,128)S(1)} %copy-done), kind=kLoop, calls=%fused_computation | loop fusion | flops 1572096 | bytes 3214336 | tf_op jit(solution)/shard_map/reduce_sum | solution.py:153
  71.0 0.9 fusion.24
  72.3 2.4 %collective-permute-start.4 = (f32[8,384]{1,0:T(8,128)S(1)}, f32[8,384]{1,0:T(8,128)S(1)}, u32[]{:S(2)}, u32[]{:S(2)}) collective-permute-start(f32[8,384]{1,0:T(8,128)S(1)} %squeeze.58), channel_id=1, source_target_pairs={{0,508},{4,0},{8,4},{12,8},{16,12},{20,16},{24,20},{28,24},{32,28}... | collective-permute-start | bytes 36872 | tf_op jit(solution)/shard_map/ppermute | solution.py:59
  74.8 1.9 %collective-permute-start.5 = (f32[8,384]{1,0:T(8,128)S(1)}, f32[8,384]{1,0:T(8,128)S(1)}, u32[]{:S(2)}, u32[]{:S(2)}) collective-permute-start(f32[8,384]{1,0:T(8,128)S(1)} %squeeze.59), channel_id=1, source_target_pairs={{0,4},{4,8},{8,12},{12,16},{16,20},{20,24},{24,28},{28,32},{32,36}... | collective-permute-start | bytes 36872 | tf_op jit(solution)/shard_map/ppermute | solution.py:59
  76.8 6.3 %collective-permute-start.6 = (f32[8,384]{1,0:T(8,128)S(1)}, f32[8,384]{1,0:T(8,128)S(1)}, u32[]{:S(2)}, u32[]{:S(2)}) collective-permute-start(f32[8,384]{1,0:T(8,128)S(1)} %squeeze.60), channel_id=1, source_target_pairs={{0,480},{4,484},{8,488},{12,492},{16,496},{20,500},{24,504},{28,50... | collective-permute-start | bytes 36872 | tf_op jit(solution)/shard_map/ppermute | solution.py:59
  83.3 3.4 %collective-permute-start.7 = (f32[8,384]{1,0:T(8,128)S(1)}, f32[8,384]{1,0:T(8,128)S(1)}, u32[]{:S(2)}, u32[]{:S(2)}) collective-permute-start(f32[8,384]{1,0:T(8,128)S(1)} %squeeze.61), channel_id=1, source_target_pairs={{0,32},{4,36},{8,40},{12,44},{16,48},{20,52},{24,56},{28,60},{32,6... | collective-permute-start | bytes 36872 | tf_op jit(solution)/shard_map/ppermute | solution.py:59
  86.9 2.5 %psum.44 = f32[16]{0:T(128)S(1)} all-reduce(f32[16]{0:T(128)S(1)} %add.66), channel_id=1, replica_groups=mesh['z_hi'=2,'x'=4,'y'=8,'core'=2,'scen'=4] {'core'}, use_global_device_ids=true, to_apply=%region_8.0 | all-reduce | flops 16 | bytes 128 | tf_op jit(solution)/shard_map/psum | solution.py:18
  89.3 18.4 %psum.45 = f32[16]{0:T(128)S(1)} all-reduce(f32[16]{0:T(128)S(1)} %psum.44), channel_id=1, replica_groups=mesh['z_hi'=2,'x'=4,'y'=8,'core'=2,'scen'=4] {'y'}, use_global_device_ids=true, to_apply=%region_9.0 | all-reduce | flops 16 | bytes 128 | tf_op jit(solution)/shard_map/psum | solution.py:18
  107.7 32.4 %psum.46 = f32[16]{0:T(128)S(1)} all-reduce(f32[16]{0:T(128)S(1)} %psum.45), channel_id=1, replica_groups=mesh['z_hi'=2,'x'=4,'y'=8,'core'=2,'scen'=4] {'x'}, use_global_device_ids=true, to_apply=%region_10.0 | all-reduce | flops 16 | bytes 128 | tf_op jit(solution)/shard_map/psum | solution.py:18
  140.1 12.4 %psum.47 = f32[16]{0:T(128)} all-reduce(f32[16]{0:T(128)S(1)} %psum.46), channel_id=1, replica_groups=mesh['z_hi'=2,'x'=4,'y'=8,'core'=2,'scen'=4] {'z_hi'}, use_global_device_ids=true, to_apply=%region_11.0 | all-reduce | flops 16 | bytes 128 | tf_op jit(solution)/shard_map/psum | solution.py:18
  152.5 12.1 %psum.48 = f32[16]{0:T(128)} all-reduce(f32[16]{0:T(128)S(1)} %add.65), channel_id=1, replica_groups=mesh['z_hi'=2,'x'=4,'y'=8,'core'=2,'scen'=4] {'scen'}, use_global_device_ids=true, to_apply=%region_1.0 | all-reduce | flops 16 | bytes 128 | tf_op jit(solution)/shard_map/psum | solution.py:157
  165.4 0.9 maximum_bitcast_fusion
  (75 shorter events, 5.0 us)
Async XLA Ops:
  6.7 2.8 %copy-start.5 = (f32[48,16]{0,1:T(8,128)S(1)}, f32[48,16]{0,1:T(8,128)}, u32[]{:S(2)}) copy-start(f32[48,16]{0,1:T(8,128)} %param.26) | copy-start | bytes 9220
  6.7 3.8 %copy-start.7 = (s32[1,16]{1,0:T(1,128)S(1)}, s32[1,16]{1,0:T(1,128)}, u32[]{:S(2)}) copy-start(s32[1,16]{1,0:T(1,128)} %param.23) | copy-start | bytes 196
  28.9 17.4 %copy-start.4 = (f32[1,48,16,16]{1,3,2,0:T(8,128)S(1)}, f32[1,48,16,16]{1,3,2,0:T(8,128)}, u32[]{:S(2)}) copy-start(f32[1,48,16,16]{1,3,2,0:T(8,128)} %param.24) | copy-start | bytes 147460
  28.9 17.5 %copy-start.6 = (f32[48,16]{0,1:T(8,128)S(1)}, f32[48,16]{0,1:T(8,128)}, u32[]{:S(2)}) copy-start(f32[48,16]{0,1:T(8,128)} %param.27) | copy-start | bytes 9220
  29.3 18.6 %collective-permute-start = (f32[8,384]{1,0:T(8,128)S(1)}, f32[8,384]{1,0:T(8,128)S(1)}, u32[]{:S(2)}, u32[]{:S(2)}) collective-permute-start(f32[8,384]{1,0:T(8,128)S(1)} %squeeze.54), channel_id=1, source_target_pairs={{0,508},{4,0},{8,4},{12,8},{16,12},{20,16},{24,20},{28,24},{32,28}... | collective-permute-start | bytes 36872 | tf_op jit(solution)/shard_map/ppermute | solution.py:59
  34.2 13.9 %collective-permute-start.1 = (f32[8,384]{1,0:T(8,128)S(1)}, f32[8,384]{1,0:T(8,128)S(1)}, u32[]{:S(2)}, u32[]{:S(2)}) collective-permute-start(f32[8,384]{1,0:T(8,128)S(1)} %squeeze.55), channel_id=1, source_target_pairs={{0,4},{4,8},{8,12},{12,16},{16,20},{20,24},{24,28},{28,32},{32,36}... | collective-permute-start | bytes 36872 | tf_op jit(solution)/shard_map/ppermute | solution.py:59
  36.2 16.1 %copy-start.3 = (f32[1,4,8,48,16]{3,4,2,1,0:T(8,128)S(1)}, f32[1,4,8,48,16]{3,4,2,1,0:T(8,128)}, u32[]{:S(2)}) copy-start(f32[1,4,8,48,16]{3,4,2,1,0:T(8,128)} %param.22) | copy-start | bytes 294916
  36.2 12.1 %collective-permute-start.2 = (f32[8,384]{1,0:T(8,128)S(1)}, f32[8,384]{1,0:T(8,128)S(1)}, u32[]{:S(2)}, u32[]{:S(2)}) collective-permute-start(f32[8,384]{1,0:T(8,128)S(1)} %squeeze.56), channel_id=1, source_target_pairs={{0,480},{4,484},{8,488},{12,492},{16,496},{20,500},{24,504},{28,50... | collective-permute-start | bytes 36872 | tf_op jit(solution)/shard_map/ppermute | solution.py:59
  41.8 10.4 %collective-permute-start.3 = (f32[8,384]{1,0:T(8,128)S(1)}, f32[8,384]{1,0:T(8,128)S(1)}, u32[]{:S(2)}, u32[]{:S(2)}) collective-permute-start(f32[8,384]{1,0:T(8,128)S(1)} %squeeze.57), channel_id=1, source_target_pairs={{0,32},{4,36},{8,40},{12,44},{16,48},{20,52},{24,56},{28,60},{32,6... | collective-permute-start | bytes 36872 | tf_op jit(solution)/shard_map/ppermute | solution.py:59
  55.1 14.0 %copy-start = (f32[24,16,1024]{2,1,0:T(8,128)S(1)}, f32[24,16,1024]{2,1,0:T(8,128)}, u32[]{:S(2)}) copy-start(f32[24,16,1024]{2,1,0:T(8,128)} %get-tuple-element.8) | copy-start | bytes 4718596
  55.1 14.0 %copy-start.2 = (f32[16,1024]{1,0:T(8,128)S(1)}, f32[16,1024]{1,0:T(8,128)}, u32[]{:S(2)}) copy-start(f32[16,1024]{1,0:T(8,128)} %fusion.23.fault_ref) | copy-start | bytes 196612
  69.1 1.9 %copy-start.1 = (f32[24,16,1024]{2,1,0:T(8,128)S(1)}, f32[24,16,1024]{2,1,0:T(8,128)}, u32[]{:S(2)}) copy-start(f32[24,16,1024]{2,1,0:T(8,128)} %get-tuple-element.11) | copy-start | bytes 4718596
  72.3 92.3 %collective-permute-start.4 = (f32[8,384]{1,0:T(8,128)S(1)}, f32[8,384]{1,0:T(8,128)S(1)}, u32[]{:S(2)}, u32[]{:S(2)}) collective-permute-start(f32[8,384]{1,0:T(8,128)S(1)} %squeeze.58), channel_id=1, source_target_pairs={{0,508},{4,0},{8,4},{12,8},{16,12},{20,16},{24,20},{28,24},{32,28}... | collective-permute-start | bytes 36872 | tf_op jit(solution)/shard_map/ppermute | solution.py:59
  74.8 90.0 %collective-permute-start.5 = (f32[8,384]{1,0:T(8,128)S(1)}, f32[8,384]{1,0:T(8,128)S(1)}, u32[]{:S(2)}, u32[]{:S(2)}) collective-permute-start(f32[8,384]{1,0:T(8,128)S(1)} %squeeze.59), channel_id=1, source_target_pairs={{0,4},{4,8},{8,12},{12,16},{16,20},{20,24},{24,28},{28,32},{32,36}... | collective-permute-start | bytes 36872 | tf_op jit(solution)/shard_map/ppermute | solution.py:59
  76.8 88.1 %collective-permute-start.6 = (f32[8,384]{1,0:T(8,128)S(1)}, f32[8,384]{1,0:T(8,128)S(1)}, u32[]{:S(2)}, u32[]{:S(2)}) collective-permute-start(f32[8,384]{1,0:T(8,128)S(1)} %squeeze.60), channel_id=1, source_target_pairs={{0,480},{4,484},{8,488},{12,492},{16,496},{20,500},{24,504},{28,50... | collective-permute-start | bytes 36872 | tf_op jit(solution)/shard_map/ppermute | solution.py:59
  83.3 81.9 %collective-permute-start.7 = (f32[8,384]{1,0:T(8,128)S(1)}, f32[8,384]{1,0:T(8,128)S(1)}, u32[]{:S(2)}, u32[]{:S(2)}) collective-permute-start(f32[8,384]{1,0:T(8,128)S(1)} %squeeze.61), channel_id=1, source_target_pairs={{0,32},{4,36},{8,40},{12,44},{16,48},{20,52},{24,56},{28,60},{32,6... | collective-permute-start | bytes 36872 | tf_op jit(solution)/shard_map/ppermute | solution.py:59

commit v3 on v2

--- a/solution.py
+++ b/solution.py
@@ -13,10 +13,18 @@
 SUB_SIZES = (2, 4, 8, 2)
 
 
-def sum_over_sub(value):
-    for axis in reversed(SUB):
-        value = lax.psum(value, axis)
-    return value
+def sum_both(fault_value, control_value):
+    for axis in reversed(SUB[1:]):
+        fault_value = lax.psum(fault_value, axis)
+    scen_index = lax.axis_index("scen")
+    high_index = lax.axis_index(SUB[0])
+    fault_slots = jnp.zeros((lax.axis_size("scen"),) + fault_value.shape, jnp.float32)
+    control_slots = jnp.zeros((lax.axis_size(SUB[0]),) + control_value.shape, jnp.float32)
+    fault_slots, control_slots = lax.psum(
+        (fault_slots.at[scen_index].set(fault_value), control_slots.at[high_index].set(control_value)),
+        (SUB[0], "scen"),
+    )
+    return fault_slots[scen_index], control_slots[high_index]
 
 
 def block_scan_kernel(
@@ -154,7 +162,7 @@
             * fault_voltage[block_start : block_start + block_len],
             axis=0,
         )
-        control_local = control_local + lax.psum(control_term, "scen")
+        control_local = control_local + control_term
         fault_local = fault_local + fault_term
         received = jnp.stack(
             [
@@ -166,7 +174,7 @@
             [received.reshape(4, slot_count, block_len, scen_rows), window[:, :, :block_len]],
             axis=2,
         )
-    fault_local = sum_over_sub(fault_local)
+    fault_local, control_local = sum_both(fault_local, control_local)
     return (adjoint_next[None], window[None], control_local[None], fault_local)
 
 

time: 167 us -> 175 us (1.048)
  the two profiles are of different devices: /device:TPU:4 before, /device:TPU:25 now
where the time goes in v3:
time: 175 us; the launch traced here: 174 us
  starting transfers between devices  62.3 us (36%)
  blocking collectives  30.8 us (18%)
  Pallas kernels  27.9 us (16%)
  waiting for transfers between devices  19.6 us (11%)
  local copies, waits for them, and re-layouts  13.3 us (8%)
  matrix products  9.92 us (6%)
  other arithmetic  8.82 us (5%)
    ppermute x8, starting transfers between devices, passed_along(): return lax.ppermute(value, axis, pairs)  62.3 us
    pallas_call x2, Pallas kernels, block_scan(): pl.pallas_call(block_scan_kernel, out_shape=(jax.ShapeDtypeStruct(inflow....  27.9 us
    ppermute x8, waiting for transfers between devices, passed_along(): return lax.ppermute(value, axis, pairs)  19.6 us
    psum x3, blocking collectives, sum_both(): fault_value = lax.psum(fault_value, axis)  18.9 us
    psum x1, blocking collectives, sum_both(): lax.psum((fault_slots.at[scen_index].set(fault_value), control_slots.at[h...  12 us
    dot_general x2, matrix products, body(): jnp.dot(adjoint_block.reshape(block_len * scen_rows, node_count), pick_ta...  3.97 us
    dot_general x2, matrix products, body(): jnp.dot(picked, spread_table, precision=PRECISE)  3.95 us
  transfers between devices with their start and end apart: 8, of which 2 were waited for; matrix products, arithmetic and copies ran while one was open for 4% of the time, Pallas kernels for 0%

profile of v3, /device:TPU:25, one launch (start us, length us, event | category | flops | bytes accessed | tf_op | source)
XLA Modules:
  0.0 174.0 jit_solution(13521818549110207889)
XLA Ops:
  1.3 0.7 fusion.23.fault_ref
  2.0 0.7 fusion.34
  2.8 0.8 squeeze.54
  3.6 0.8 eq.71
  4.4 0.8 add_add_fusion
  5.1 1.4 fusion.1
  6.8 2.8 %slice_bitcast_fusion = (bf16[24,16,1024]{2,1,0:T(8,128)(2,1)}, bf16[24,16,1024]{2,1,0:T(8,128)(2,1)}) fusion(bf16[48,1,16,1024]{3,2,0,1:T(8,128)(2,1)} %bitcast.81), kind=kLoop, calls=%fused_computation.2 | loop fusion | bytes 3145728 | tf_op jit(solution)/shard_map/squeeze | solution.py:137
  9.6 0.9 copy.45.current_ref
  10.7 2.0 %fusion.13.inflow_ref = f32[24,16,1024]{2,1,0:T(8,128)} fusion(f32[24,16,32]{2,1,0:T(8,128)S(1)} %copy.44, f32[32]{0:T(128)S(1)} %broadcast_select_fusion.2, s32[32]{0:T(128)S(1)} %eq.71), kind=kOutput, calls=%fused_computation.21 | convolution fusion | flops 151040000 | bytes 1622272 | tf_op jit(solution)/shard_map/dot_general | solution.py:133
  12.7 13.9 %shard_map.165 = (f32[24,16,1024]{2,1,0:T(8,128)}, f32[16,1024]{1,0:T(8,128)}) custom-call(bf16[24,16,1024]{2,1,0:T(8,128)(2,1)} %get-tuple-element.40.grad_ref, f32[24,16,1024]{2,1,0:T(8,128)} %fusion.13.inflow_ref, f32[24,16,1]{2,1,0:T(8,128)} %copy.45.current_ref, f32[16,1024]{1,0:T(8,128)} %fusion.23.fault_ref, f32[1,1024]{1,0:T(1,128)} %companion_ref.3, ...), custom_call_target="tpu_custom_call" | custom-call | tf_op jit(solution)/shard_map/pallas_call | solution.py:55
  26.6 2.3 %fusion.25 = f32[384,48]{0,1:T(8,128)S(1)} fusion(f32[384,1024]{1,0:T(8,128)} %bitcast.79, pred[1024,16]{0,1:T(8,128)(4,1)S(1)} %iota_compare_fusion.6, pred[1024,32]{0,1:T(8,128)(4,1)S(1)} %iota_compare_fusion.3), kind=kOutput, calls=%fused_computation.37 | convolution fusion | flops 226541568 | bytes 1695744 | tf_op jit(solution)/shard_map/dot_general | solution.py:145
  29.4 2.6 %collective-permute-start = (f32[8,384]{1,0:T(8,128)S(1)}, f32[8,384]{1,0:T(8,128)S(1)}, u32[]{:S(2)}, u32[]{:S(2)}) collective-permute-start(f32[8,384]{1,0:T(8,128)S(1)} %squeeze.57), channel_id=1, source_target_pairs={{0,508},{4,0},{8,4},{12,8},{16,12},{20,16},{24,20},{28,24},{32,28}... | collective-permute-start | bytes 36872 | tf_op jit(solution)/shard_map/ppermute | solution.py:67
  32.0 4.3 %collective-permute-start.1 = (f32[8,384]{1,0:T(8,128)S(1)}, f32[8,384]{1,0:T(8,128)S(1)}, u32[]{:S(2)}, u32[]{:S(2)}) collective-permute-start(f32[8,384]{1,0:T(8,128)S(1)} %squeeze.58), channel_id=1, source_target_pairs={{0,4},{4,8},{8,12},{12,16},{16,20},{20,24},{24,28},{28,32},{32,36}... | collective-permute-start | bytes 36872 | tf_op jit(solution)/shard_map/ppermute | solution.py:67
  36.5 22.2 %collective-permute-start.2 = (f32[8,384]{1,0:T(8,128)S(1)}, f32[8,384]{1,0:T(8,128)S(1)}, u32[]{:S(2)}, u32[]{:S(2)}) collective-permute-start(f32[8,384]{1,0:T(8,128)S(1)} %squeeze.59), channel_id=1, source_target_pairs={{0,480},{4,484},{8,488},{12,492},{16,496},{20,500},{24,504},{28,50... | collective-permute-start | bytes 36872 | tf_op jit(solution)/shard_map/ppermute | solution.py:67
  58.8 1.9 %collective-permute-start.3 = (f32[8,384]{1,0:T(8,128)S(1)}, f32[8,384]{1,0:T(8,128)S(1)}, u32[]{:S(2)}, u32[]{:S(2)}) collective-permute-start(f32[8,384]{1,0:T(8,128)S(1)} %squeeze.60), channel_id=1, source_target_pairs={{0,32},{4,36},{8,40},{12,44},{16,48},{20,52},{24,56},{28,60},{32,6... | collective-permute-start | bytes 36872 | tf_op jit(solution)/shard_map/ppermute | solution.py:67
  60.9 0.8 and_reduce_fusion
  62.4 0.9 copy.51.current_ref
  66.8 7.3 %collective-permute-done.3 = f32[8,384]{1,0:T(8,128)S(1)} collective-permute-done((f32[8,384]{1,0:T(8,128)S(1)}, f32[8,384]{1,0:T(8,128)S(1)}, u32[]{:S(2)}, u32[]{:S(2)}) %collective-permute-start.3) | collective-permute-done | bytes 12320 | tf_op jit(solution)/shard_map/ppermute | solution.py:67
  75.1 2.0 %fusion.11.inflow_ref = f32[24,16,1024]{2,1,0:T(8,128)} fusion(f32[24,16,32]{2,1,0:T(8,128)S(1)} %copy.50, f32[32]{0:T(128)S(1)} %broadcast_select_fusion.2, s32[32]{0:T(128)S(1)} %eq.71), kind=kOutput, calls=%fused_computation.19 | convolution fusion | flops 151040000 | bytes 1622272 | tf_op jit(solution)/shard_map/dot_general | solution.py:133
  77.0 14.0 %shard_map.166 = (f32[24,16,1024]{2,1,0:T(8,128)}, f32[16,1024]{1,0:T(8,128)}) custom-call(bf16[24,16,1024]{2,1,0:T(8,128)(2,1)} %get-tuple-element.41.grad_ref, f32[24,16,1024]{2,1,0:T(8,128)} %fusion.11.inflow_ref, f32[24,16,1]{2,1,0:T(8,128)} %copy.51.current_ref, f32[16,1024]{1,0:T(8,128)} %fusion.23.fault_ref, f32[1,1024]{1,0:T(1,128)} %companion_ref.3, ...), custom_call_target="tpu_custom_call" | custom-call | tf_op jit(solution)/shard_map/pallas_call | solution.py:55
  91.1 1.8 %multiply_reduce_fusion = (f32[24,16]{1,0:T(8,128)S(1)}, f32[24,16]{1,0:T(8,128)S(1)}) fusion(f32[24,16,1024]{2,1,0:T(8,128)} %get-tuple-element.35, f32[16,1024]{1,0:T(8,128)S(1)} %copy-done.2, f32[24,16,1024]{2,1,0:T(8,128)S(1)} %copy-done), kind=kLoop, calls=%fused_computation | loop fusion | flops 1572096 | bytes 3214336 | tf_op jit(solution)/shard_map/reduce_sum | solution.py:161
  93.0 2.5 %psum.36 = f32[16]{0:T(128)S(1)} all-reduce(f32[16]{0:T(128)S(1)} %add.84), channel_id=1, replica_groups=mesh['z_hi'=2,'x'=4,'y'=8,'core'=2,'scen'=4] {'core'}, use_global_device_ids=true, to_apply=%region_9.0 | all-reduce | flops 16 | bytes 128 | tf_op jit(solution)/shard_map/psum | solution.py:18
  95.5 10.4 %psum.37 = f32[16]{0:T(128)S(1)} all-reduce(f32[16]{0:T(128)S(1)} %psum.36), channel_id=1, replica_groups=mesh['z_hi'=2,'x'=4,'y'=8,'core'=2,'scen'=4] {'y'}, use_global_device_ids=true, to_apply=%region_10.0 | all-reduce | flops 16 | bytes 128 | tf_op jit(solution)/shard_map/psum | solution.py:18
  105.9 6.0 %psum.38 = f32[16]{0:T(128)S(1)} all-reduce(f32[16]{0:T(128)S(1)} %psum.37), channel_id=1, replica_groups=mesh['z_hi'=2,'x'=4,'y'=8,'core'=2,'scen'=4] {'x'}, use_global_device_ids=true, to_apply=%region_11.0 | all-reduce | flops 16 | bytes 128 | tf_op jit(solution)/shard_map/psum | solution.py:18
  111.9 1.7 fusion.24
  115.1 12.0 %all-reduce = (f32[2,16]{1,0:T(2,128)S(1)}, f32[4,16]{1,0:T(4,128)S(1)}) all-reduce(f32[2,16]{1,0:T(2,128)S(1)} %scatter.6, f32[4,16]{1,0:T(4,128)S(1)} %scatter.9), channel_id=1, replica_groups=mesh['z_hi'=2,'x'=4,'y'=8,'core'=2,'scen'=4] {'z_hi','scen'}, use_global_device_ids=true, to_apply=%region_3.0 | all-reduce | flops 96 | bytes 768 | tf_op jit(solution)/shard_map/psum | solution.py:23
  128.0 11.3 %collective-permute-start.4 = (f32[8,384]{1,0:T(8,128)S(1)}, f32[8,384]{1,0:T(8,128)S(1)}, u32[]{:S(2)}, u32[]{:S(2)}) collective-permute-start(f32[8,384]{1,0:T(8,128)S(1)} %squeeze.61), channel_id=1, source_target_pairs={{0,508},{4,0},{8,4},{12,8},{16,12},{20,16},{24,20},{28,24},{32,28}... | collective-permute-start | bytes 36872 | tf_op jit(solution)/shard_map/ppermute | solution.py:67
  139.4 4.8 %collective-permute-start.5 = (f32[8,384]{1,0:T(8,128)S(1)}, f32[8,384]{1,0:T(8,128)S(1)}, u32[]{:S(2)}, u32[]{:S(2)}) collective-permute-start(f32[8,384]{1,0:T(8,128)S(1)} %squeeze.62), channel_id=1, source_target_pairs={{0,4},{4,8},{8,12},{12,16},{16,20},{20,24},{24,28},{28,32},{32,36}... | collective-permute-start | bytes 36872 | tf_op jit(solution)/shard_map/ppermute | solution.py:67
  144.3 13.3 %collective-permute-start.6 = (f32[8,384]{1,0:T(8,128)S(1)}, f32[8,384]{1,0:T(8,128)S(1)}, u32[]{:S(2)}, u32[]{:S(2)}) collective-permute-start(f32[8,384]{1,0:T(8,128)S(1)} %squeeze.63), channel_id=1, source_target_pairs={{0,480},{4,484},{8,488},{12,492},{16,496},{20,500},{24,504},{28,50... | collective-permute-start | bytes 36872 | tf_op jit(solution)/shard_map/ppermute | solution.py:67
  157.7 1.9 %collective-permute-start.7 = (f32[8,384]{1,0:T(8,128)S(1)}, f32[8,384]{1,0:T(8,128)S(1)}, u32[]{:S(2)}, u32[]{:S(2)}) collective-permute-start(f32[8,384]{1,0:T(8,128)S(1)} %squeeze.64), channel_id=1, source_target_pairs={{0,32},{4,36},{8,40},{12,44},{16,48},{20,52},{24,56},{28,60},{32,6... | collective-permute-start | bytes 36872 | tf_op jit(solution)/shard_map/ppermute | solution.py:67
  160.7 12.3 %collective-permute-done.7 = f32[8,384]{1,0:T(8,128)S(1)} collective-permute-done((f32[8,384]{1,0:T(8,128)S(1)}, f32[8,384]{1,0:T(8,128)S(1)}, u32[]{:S(2)}, u32[]{:S(2)}) %collective-permute-start.7) | collective-permute-done | bytes 12320 | tf_op jit(solution)/shard_map/ppermute | solution.py:67
  173.1 0.9 maximum_bitcast_fusion
  (99 shorter events, 11.1 us)
Async XLA Ops:
  6.7 2.8 %copy-start.11 = (f32[48,16]{0,1:T(8,128)S(1)}, f32[48,16]{0,1:T(8,128)}, u32[]{:S(2)}) copy-start(f32[48,16]{0,1:T(8,128)} %param.30) | copy-start | bytes 9220
  6.8 3.8 %copy-start.13 = (s32[1,16]{1,0:T(1,128)S(1)}, s32[1,16]{1,0:T(1,128)}, u32[]{:S(2)}) copy-start(s32[1,16]{1,0:T(1,128)} %param.27) | copy-start | bytes 196
  10.5 16.0 %copy-start.5 = (pred[1024,32]{0,1:T(8,128)(4,1)}, pred[1024,32]{0,1:T(8,128)(4,1)S(1)}, u32[]{:S(2)}) copy-start(pred[1024,32]{0,1:T(8,128)(4,1)S(1)} %iota_compare_fusion.3) | copy-start | bytes 98308
  10.6 15.9 %copy-start.6 = (pred[1024,16]{0,1:T(8,128)(4,1)}, pred[1024,16]{0,1:T(8,128)(4,1)S(1)}, u32[]{:S(2)}) copy-start(pred[1024,16]{0,1:T(8,128)(4,1)S(1)} %iota_compare_fusion.6) | copy-start | bytes 49156
  28.9 31.8 %copy-start.12 = (f32[48,16]{0,1:T(8,128)S(1)}, f32[48,16]{0,1:T(8,128)}, u32[]{:S(2)}) copy-start(f32[48,16]{0,1:T(8,128)} %param.31) | copy-start | bytes 9220
  28.9 31.9 %copy-start.4 = (f32[1,48,16,16]{1,3,2,0:T(8,128)S(1)}, f32[1,48,16,16]{1,3,2,0:T(8,128)}, u32[]{:S(2)}) copy-start(f32[1,48,16,16]{1,3,2,0:T(8,128)} %param.28) | copy-start | bytes 147460
  28.9 32.0 %copy-start.15 = (s32[2]{0:T(128)S(1)}, s32[2]{0:T(128)}, u32[]{:S(2)}) copy-start(s32[2]{0:T(128)} %constant.82.clone.1) | copy-start | bytes 28
  28.9 32.7 %copy-start.14 = (s32[2]{0:T(128)S(1)}, s32[2]{0:T(128)}, u32[]{:S(2)}) copy-start(s32[2]{0:T(128)} %constant.79.clone.1) | copy-start | bytes 28
  29.4 36.9 %collective-permute-start = (f32[8,384]{1,0:T(8,128)S(1)}, f32[8,384]{1,0:T(8,128)S(1)}, u32[]{:S(2)}, u32[]{:S(2)}) collective-permute-start(f32[8,384]{1,0:T(8,128)S(1)} %squeeze.57), channel_id=1, source_target_pairs={{0,508},{4,0},{8,4},{12,8},{16,12},{20,16},{24,20},{28,24},{32,28}... | collective-permute-start | bytes 36872 | tf_op jit(solution)/shard_map/ppermute | solution.py:67
  32.0 34.4 %collective-permute-start.1 = (f32[8,384]{1,0:T(8,128)S(1)}, f32[8,384]{1,0:T(8,128)S(1)}, u32[]{:S(2)}, u32[]{:S(2)}) collective-permute-start(f32[8,384]{1,0:T(8,128)S(1)} %squeeze.58), channel_id=1, source_target_pairs={{0,4},{4,8},{8,12},{12,16},{16,20},{20,24},{24,28},{28,32},{32,36}... | collective-permute-start | bytes 36872 | tf_op jit(solution)/shard_map/ppermute | solution.py:67
  36.5 30.1 %collective-permute-start.2 = (f32[8,384]{1,0:T(8,128)S(1)}, f32[8,384]{1,0:T(8,128)S(1)}, u32[]{:S(2)}, u32[]{:S(2)}) collective-permute-start(f32[8,384]{1,0:T(8,128)S(1)} %squeeze.59), channel_id=1, source_target_pairs={{0,480},{4,484},{8,488},{12,492},{16,496},{20,500},{24,504},{28,50... | collective-permute-start | bytes 36872 | tf_op jit(solution)/shard_map/ppermute | solution.py:67
  58.6 15.7 %copy-start.3 = (f32[1,4,8,48,16]{3,4,2,1,0:T(8,128)S(1)}, f32[1,4,8,48,16]{3,4,2,1,0:T(8,128)}, u32[]{:S(2)}) copy-start(f32[1,4,8,48,16]{3,4,2,1,0:T(8,128)} %param.26) | copy-start | bytes 294916
  58.8 15.4 %collective-permute-start.3 = (f32[8,384]{1,0:T(8,128)S(1)}, f32[8,384]{1,0:T(8,128)S(1)}, u32[]{:S(2)}, u32[]{:S(2)}) collective-permute-start(f32[8,384]{1,0:T(8,128)S(1)} %squeeze.60), channel_id=1, source_target_pairs={{0,32},{4,36},{8,40},{12,44},{16,48},{20,52},{24,56},{28,60},{32,6... | collective-permute-start | bytes 36872 | tf_op jit(solution)/shard_map/ppermute | solution.py:67
  77.0 14.0 %copy-start = (f32[24,16,1024]{2,1,0:T(8,128)S(1)}, f32[24,16,1024]{2,1,0:T(8,128)}, u32[]{:S(2)}) copy-start(f32[24,16,1024]{2,1,0:T(8,128)} %get-tuple-element.32) | copy-start | bytes 4718596
  77.0 14.0 %copy-start.2 = (f32[16,1024]{1,0:T(8,128)S(1)}, f32[16,1024]{1,0:T(8,128)}, u32[]{:S(2)}) copy-start(f32[16,1024]{1,0:T(8,128)} %fusion.23.fault_ref) | copy-start | bytes 196612
  91.1 1.9 %copy-start.9 = (f32[24,16]{1,0:T(8,128)S(1)}, f32[24,16]{1,0:T(8,128)}, u32[]{:S(2)}) copy-start(f32[24,16]{1,0:T(8,128)} %copy.60) | copy-start | bytes 4612
  91.1 1.9 %copy-start.10 = (f32[24,16]{1,0:T(8,128)S(1)}, f32[24,16]{1,0:T(8,128)}, u32[]{:S(2)}) copy-start(f32[24,16]{1,0:T(8,128)} %copy.61) | copy-start | bytes 4612
  91.1 20.8 %copy-start.1 = (f32[24,16,1024]{2,1,0:T(8,128)S(1)}, f32[24,16,1024]{2,1,0:T(8,128)}, u32[]{:S(2)}) copy-start(f32[24,16,1024]{2,1,0:T(8,128)} %get-tuple-element.35) | copy-start | bytes 4718596
  92.9 21.3 %copy-start.7 = (f32[384,16]{0,1:T(8,128)S(1)}, f32[384,16]{0,1:T(8,128)}, u32[]{:S(2)}) copy-start(f32[384,16]{0,1:T(8,128)} %squeeze.65) | copy-start | bytes 73732
  92.9 21.3 %copy-start.8 = (f32[384,16]{0,1:T(8,128)S(1)}, f32[384,16]{0,1:T(8,128)}, u32[]{:S(2)}) copy-start(f32[384,16]{0,1:T(8,128)} %squeeze.66) | copy-start | bytes 73732
  128.0 32.2 %collective-permute-start.4 = (f32[8,384]{1,0:T(8,128)S(1)}, f32[8,384]{1,0:T(8,128)S(1)}, u32[]{:S(2)}, u32[]{:S(2)}) collective-permute-start(f32[8,384]{1,0:T(8,128)S(1)} %squeeze.61), channel_id=1, source_target_pairs={{0,508},{4,0},{8,4},{12,8},{16,12},{20,16},{24,20},{28,24},{32,28}... | collective-permute-start | bytes 36872 | tf_op jit(solution)/shard_map/ppermute | solution.py:67
  139.4 20.9 %collective-permute-start.5 = (f32[8,384]{1,0:T(8,128)S(1)}, f32[8,384]{1,0:T(8,128)S(1)}, u32[]{:S(2)}, u32[]{:S(2)}) collective-permute-start(f32[8,384]{1,0:T(8,128)S(1)} %squeeze.62), channel_id=1, source_target_pairs={{0,4},{4,8},{8,12},{12,16},{16,20},{20,24},{24,28},{28,32},{32,36}... | collective-permute-start | bytes 36872 | tf_op jit(solution)/shard_map/ppermute | solution.py:67
  144.3 16.2 %collective-permute-start.6 = (f32[8,384]{1,0:T(8,128)S(1)}, f32[8,384]{1,0:T(8,128)S(1)}, u32[]{:S(2)}, u32[]{:S(2)}) collective-permute-start(f32[8,384]{1,0:T(8,128)S(1)} %squeeze.63), channel_id=1, source_target_pairs={{0,480},{4,484},{8,488},{12,492},{16,496},{20,500},{24,504},{28,50... | collective-permute-start | bytes 36872 | tf_op jit(solution)/shard_map/ppermute | solution.py:67
  157.7 15.3 %collective-permute-start.7 = (f32[8,384]{1,0:T(8,128)S(1)}, f32[8,384]{1,0:T(8,128)S(1)}, u32[]{:S(2)}, u32[]{:S(2)}) collective-permute-start(f32[8,384]{1,0:T(8,128)S(1)} %squeeze.64), channel_id=1, source_target_pairs={{0,32},{4,36},{8,40},{12,44},{16,48},{20,52},{24,56},{28,60},{32,6... | collective-permute-start | bytes 36872 | tf_op jit(solution)/shard_map/ppermute | solution.py:67

commit v4 on v3

--- a/solution.py
+++ b/solution.py
@@ -145,6 +145,12 @@
         samples = jnp.dot(
             adjoint_block.reshape(block_len * scen_rows, node_count), pick_table, precision=PRECISE
         )
+        fault_term = jnp.sum(
+            jnp.sum(adjoint_block * fault_table[None], axis=2)
+            * fault_voltage[block_start : block_start + block_len],
+            axis=0,
+        )
+        samples, fault_term = lax.optimization_barrier((samples, fault_term))
         series = (
             jnp.transpose(
                 samples[:, :port_total].reshape(block_len, scen_rows, 4, slot_count), (2, 3, 0, 1)
@@ -156,11 +162,6 @@
             samples[:, port_total:].reshape(block_len, scen_rows, conv_count)
             * conv_drive[0, block_start : block_start + block_len],
             axis=(0, 1),
-        )
-        fault_term = jnp.sum(
-            jnp.sum(adjoint_block * fault_table[None], axis=2)
-            * fault_voltage[block_start : block_start + block_len],
-            axis=0,
         )
         control_local = control_local + control_term
         fault_local = fault_local + fault_term

time: 175 us -> 164 us (0.937)
  the two profiles are of different devices: /device:TPU:25 before, /device:TPU:10 now
where the time goes in v4:
time: 164 us; the launch traced here: 163 us
  blocking collectives  76.7 us (47%)
  starting transfers between devices  32.4 us (20%)
  Pallas kernels  27.9 us (17%)
  local copies, waits for them, and re-layouts  9.82 us (6%)
  other arithmetic  8.37 us (5%)
  matrix products  6.8 us (4%)
    psum x3, blocking collectives, sum_both(): fault_value = lax.psum(fault_value, axis)  58.9 us
    ppermute x8, starting transfers between devices, passed_along(): return lax.ppermute(value, axis, pairs)  32.4 us
    pallas_call x2, Pallas kernels, block_scan(): pl.pallas_call(block_scan_kernel, out_shape=(jax.ShapeDtypeStruct(inflow....  27.9 us
    psum x1, blocking collectives, sum_both(): lax.psum((fault_slots.at[scen_index].set(fault_value), control_slots.at[h...  17.8 us
    dot_general x2, matrix products, body(): jnp.dot(picked, spread_table, precision=PRECISE)  3.96 us
    reduce_sum x2, other arithmetic, body(): jnp.sum(adjoint_block * fault_table[None], axis=2)  3.42 us
  transfers between devices with their start and end apart: 8, of which 0 were waited for; matrix products, arithmetic and copies ran while one was open for 4% of the time, Pallas kernels for 0%

profile of v4, /device:TPU:10, one launch (start us, length us, event | category | flops | bytes accessed | tf_op | source)
XLA Modules:
  0.0 163.3 jit_solution(3486290085774378703)
XLA Ops:
  0.7 2.8 %slice_bitcast_fusion = (bf16[24,16,1024]{2,1,0:T(8,128)(2,1)}, bf16[24,16,1024]{2,1,0:T(8,128)(2,1)}) fusion(bf16[48,1,16,1024]{3,2,0,1:T(8,128)(2,1)} %bitcast.81), kind=kLoop, calls=%fused_computation.2 | loop fusion | bytes 3145728 | tf_op jit(solution)/shard_map/squeeze | solution.py:137
  4.7 0.9 copy.45.current_ref
  5.6 0.7 fusion.23.fault_ref
  6.5 2.0 %fusion.13.inflow_ref = f32[24,16,1024]{2,1,0:T(8,128)} fusion(f32[24,16,32]{2,1,0:T(8,128)S(1)} %copy.44, f32[32]{0:T(128)S(1)} %broadcast_select_fusion.2, s32[32]{0:T(128)S(1)} %eq.71), kind=kOutput, calls=%fused_computation.21 | convolution fusion | flops 151040000 | bytes 1622272 | tf_op jit(solution)/shard_map/dot_general | solution.py:133
  8.5 14.0 %shard_map.165 = (f32[24,16,1024]{2,1,0:T(8,128)}, f32[16,1024]{1,0:T(8,128)}) custom-call(bf16[24,16,1024]{2,1,0:T(8,128)(2,1)} %get-tuple-element.46.grad_ref, f32[24,16,1024]{2,1,0:T(8,128)} %fusion.13.inflow_ref, f32[24,16,1]{2,1,0:T(8,128)} %copy.45.current_ref, f32[16,1024]{1,0:T(8,128)} %fusion.23.fault_ref, f32[1,1024]{1,0:T(1,128)} %companion_ref.3, ...), custom_call_target="tpu_custom_call" | custom-call | tf_op jit(solution)/shard_map/pallas_call | solution.py:55
  22.4 1.7 %multiply_reduce_fusion.1 = f32[24,16]{1,0:T(8,128)S(1)} fusion(f32[24,16,1024]{2,1,0:T(8,128)} %get-tuple-element.36, f32[16,1024]{1,0:T(8,128)S(1)} %copy-done.2), kind=kLoop, calls=%fused_computation.1 | loop fusion | flops 786048 | bytes 1639936 | tf_op jit(solution)/shard_map/reduce_sum | solution.py:149
  24.3 0.9 fusion.25
  25.7 6.8 %collective-permute-start.3 = (f32[8,384]{1,0:T(8,128)S(1)}, f32[8,384]{1,0:T(8,128)S(1)}, u32[]{:S(2)}, u32[]{:S(2)}) collective-permute-start(f32[8,384]{1,0:T(8,128)S(1)} %squeeze.60), channel_id=1, source_target_pairs={{0,32},{4,36},{8,40},{12,44},{16,48},{20,52},{24,56},{28,60},{32,6... | collective-permute-start | bytes 36872 | tf_op jit(solution)/shard_map/ppermute | solution.py:67
  32.6 3.8 %collective-permute-start.2 = (f32[8,384]{1,0:T(8,128)S(1)}, f32[8,384]{1,0:T(8,128)S(1)}, u32[]{:S(2)}, u32[]{:S(2)}) collective-permute-start(f32[8,384]{1,0:T(8,128)S(1)} %squeeze.59), channel_id=1, source_target_pairs={{0,480},{4,484},{8,488},{12,492},{16,496},{20,500},{24,504},{28,50... | collective-permute-start | bytes 36872 | tf_op jit(solution)/shard_map/ppermute | solution.py:67
  36.5 1.9 %collective-permute-start.1 = (f32[8,384]{1,0:T(8,128)S(1)}, f32[8,384]{1,0:T(8,128)S(1)}, u32[]{:S(2)}, u32[]{:S(2)}) collective-permute-start(f32[8,384]{1,0:T(8,128)S(1)} %squeeze.58), channel_id=1, source_target_pairs={{0,4},{4,8},{8,12},{12,16},{16,20},{20,24},{24,28},{28,32},{32,36}... | collective-permute-start | bytes 36872 | tf_op jit(solution)/shard_map/ppermute | solution.py:67
  38.6 3.6 %collective-permute-start = (f32[8,384]{1,0:T(8,128)S(1)}, f32[8,384]{1,0:T(8,128)S(1)}, u32[]{:S(2)}, u32[]{:S(2)}) collective-permute-start(f32[8,384]{1,0:T(8,128)S(1)} %squeeze.57), channel_id=1, source_target_pairs={{0,508},{4,0},{8,4},{12,8},{16,12},{20,16},{24,20},{28,24},{32,28}... | collective-permute-start | bytes 36872 | tf_op jit(solution)/shard_map/ppermute | solution.py:67
  42.3 0.7 and_reduce_fusion.1
  43.1 0.7 and_reduce_fusion
  43.8 0.9 copy.52.current_ref
  46.0 0.6 fusion
  46.7 2.0 %fusion.11.inflow_ref = f32[24,16,1024]{2,1,0:T(8,128)} fusion(f32[24,16,32]{2,1,0:T(8,128)S(1)} %copy.51, f32[32]{0:T(128)S(1)} %broadcast_select_fusion.2, s32[32]{0:T(128)S(1)} %eq.71), kind=kOutput, calls=%fused_computation.19 | convolution fusion | flops 151040000 | bytes 1622272 | tf_op jit(solution)/shard_map/dot_general | solution.py:133
  48.7 13.9 %shard_map.166 = (f32[24,16,1024]{2,1,0:T(8,128)}, f32[16,1024]{1,0:T(8,128)}) custom-call(bf16[24,16,1024]{2,1,0:T(8,128)(2,1)} %get-tuple-element.47.grad_ref, f32[24,16,1024]{2,1,0:T(8,128)} %fusion.11.inflow_ref, f32[24,16,1]{2,1,0:T(8,128)} %copy.52.current_ref, f32[16,1024]{1,0:T(8,128)} %fusion.23.fault_ref, f32[1,1024]{1,0:T(1,128)} %companion_ref.3, ...), custom_call_target="tpu_custom_call" | custom-call | tf_op jit(solution)/shard_map/pallas_call | solution.py:55
  62.6 1.7 %multiply_reduce_fusion = f32[24,16]{1,0:T(8,128)S(1)} fusion(f32[24,16,1024]{2,1,0:T(8,128)} %get-tuple-element.40, f32[16,1024]{1,0:T(8,128)S(1)} %copy-done.3), kind=kLoop, calls=%fused_computation | loop fusion | flops 786048 | bytes 1639936 | tf_op jit(solution)/shard_map/reduce_sum | solution.py:149
  64.5 0.9 fusion.24
  65.9 5.9 %collective-permute-start.7 = (f32[8,384]{1,0:T(8,128)S(1)}, f32[8,384]{1,0:T(8,128)S(1)}, u32[]{:S(2)}, u32[]{:S(2)}) collective-permute-start(f32[8,384]{1,0:T(8,128)S(1)} %squeeze.64), channel_id=1, source_target_pairs={{0,32},{4,36},{8,40},{12,44},{16,48},{20,52},{24,56},{28,60},{32,6... | collective-permute-start | bytes 36872 | tf_op jit(solution)/shard_map/ppermute | solution.py:67
  71.9 4.7 %collective-permute-start.6 = (f32[8,384]{1,0:T(8,128)S(1)}, f32[8,384]{1,0:T(8,128)S(1)}, u32[]{:S(2)}, u32[]{:S(2)}) collective-permute-start(f32[8,384]{1,0:T(8,128)S(1)} %squeeze.63), channel_id=1, source_target_pairs={{0,480},{4,484},{8,488},{12,492},{16,496},{20,500},{24,504},{28,50... | collective-permute-start | bytes 36872 | tf_op jit(solution)/shard_map/ppermute | solution.py:67
  76.7 1.9 %collective-permute-start.5 = (f32[8,384]{1,0:T(8,128)S(1)}, f32[8,384]{1,0:T(8,128)S(1)}, u32[]{:S(2)}, u32[]{:S(2)}) collective-permute-start(f32[8,384]{1,0:T(8,128)S(1)} %squeeze.62), channel_id=1, source_target_pairs={{0,4},{4,8},{8,12},{12,16},{16,20},{20,24},{24,28},{28,32},{32,36}... | collective-permute-start | bytes 36872 | tf_op jit(solution)/shard_map/ppermute | solution.py:67
  78.7 3.6 %collective-permute-start.4 = (f32[8,384]{1,0:T(8,128)S(1)}, f32[8,384]{1,0:T(8,128)S(1)}, u32[]{:S(2)}, u32[]{:S(2)}) collective-permute-start(f32[8,384]{1,0:T(8,128)S(1)} %squeeze.61), channel_id=1, source_target_pairs={{0,508},{4,0},{8,4},{12,8},{16,12},{20,16},{24,20},{28,24},{32,28}... | collective-permute-start | bytes 36872 | tf_op jit(solution)/shard_map/ppermute | solution.py:67
  82.4 2.5 %psum.36 = f32[16]{0:T(128)S(1)} all-reduce(f32[16]{0:T(128)S(1)} %add.84), channel_id=1, replica_groups=mesh['z_hi'=2,'x'=4,'y'=8,'core'=2,'scen'=4] {'core'}, use_global_device_ids=true, to_apply=%region_9.0 | all-reduce | flops 16 | bytes 128 | tf_op jit(solution)/shard_map/psum | solution.py:18
  84.9 20.5 %psum.37 = f32[16]{0:T(128)S(1)} all-reduce(f32[16]{0:T(128)S(1)} %psum.36), channel_id=1, replica_groups=mesh['z_hi'=2,'x'=4,'y'=8,'core'=2,'scen'=4] {'y'}, use_global_device_ids=true, to_apply=%region_10.0 | all-reduce | flops 16 | bytes 128 | tf_op jit(solution)/shard_map/psum | solution.py:18
  105.4 36.0 %psum.38 = f32[16]{0:T(128)S(1)} all-reduce(f32[16]{0:T(128)S(1)} %psum.37), channel_id=1, replica_groups=mesh['z_hi'=2,'x'=4,'y'=8,'core'=2,'scen'=4] {'x'}, use_global_device_ids=true, to_apply=%region_11.0 | all-reduce | flops 16 | bytes 128 | tf_op jit(solution)/shard_map/psum | solution.py:18
  141.5 0.7 fusion.26
  142.2 0.6 fusion.27
  142.8 17.8 %all-reduce = (f32[2,16]{1,0:T(2,128)S(1)}, f32[4,16]{1,0:T(4,128)S(1)}) all-reduce(f32[2,16]{1,0:T(2,128)S(1)} %scatter.6, f32[4,16]{1,0:T(4,128)S(1)} %scatter.9), channel_id=1, replica_groups=mesh['z_hi'=2,'x'=4,'y'=8,'core'=2,'scen'=4] {'z_hi','scen'}, use_global_device_ids=true, to_apply=%region_7.0 | all-reduce | flops 96 | bytes 768 | tf_op jit(solution)/shard_map/psum | solution.py:23
  160.7 0.5 constant_dynamic-slice_fusion
  161.2 0.5 dynamic-slice_bitcast_fusion
  162.4 0.9 maximum_bitcast_fusion
  (101 shorter events, 5.4 us)
Async XLA Ops:
  0.6 2.9 %copy-start.8 = (s32[1,4,8]{2,1,0:T(4,128)S(1)}, s32[1,4,8]{2,1,0:T(4,128)}, u32[]{:S(2)}) copy-start(s32[1,4,8]{2,1,0:T(4,128)} %param.24) | copy-start | bytes 388
  0.6 3.0 %copy-start.4 = (f32[1,4,8,48,16]{3,4,2,1,0:T(8,128)S(1)}, f32[1,4,8,48,16]{3,4,2,1,0:T(8,128)}, u32[]{:S(2)}) copy-start(f32[1,4,8,48,16]{3,4,2,1,0:T(8,128)} %param.26) | copy-start | bytes 294916
  0.7 3.7 %copy-start.12 = (s32[1,4]{1,0:T(1,128)S(1)}, s32[1,4]{1,0:T(1,128)}, u32[]{:S(2)}) copy-start(s32[1,4]{1,0:T(1,128)} %param.23) | copy-start | bytes 52
  0.7 3.8 %copy-start.9 = (f32[1,4,8]{2,1,0:T(4,128)S(1)}, f32[1,4,8]{2,1,0:T(4,128)}, u32[]{:S(2)}) copy-start(f32[1,4,8]{2,1,0:T(4,128)} %param.25) | copy-start | bytes 388
  0.7 3.9 %copy-start.10 = (s32[1,4,8]{2,1,0:T(4,128)S(1)}, s32[1,4,8]{2,1,0:T(4,128)}, u32[]{:S(2)}) copy-start(s32[1,4,8]{2,1,0:T(4,128)} %param.22) | copy-start | bytes 388
  0.7 4.0 %copy-start.6 = (f32[48,16]{0,1:T(8,128)S(1)}, f32[48,16]{0,1:T(8,128)}, u32[]{:S(2)}) copy-start(f32[48,16]{0,1:T(8,128)} %param.30) | copy-start | bytes 9220
  0.7 4.9 %copy-start.15 = (s32[16]{0:T(128)S(1)}, s32[16]{0:T(128)}, u32[]{:S(2)}) copy-start(s32[16]{0:T(128)} %param.29) | copy-start | bytes 196
  0.7 5.6 %copy-start.11 = (s32[1,16]{1,0:T(1,128)S(1)}, s32[1,16]{1,0:T(1,128)}, u32[]{:S(2)}) copy-start(s32[1,16]{1,0:T(1,128)} %param.27) | copy-start | bytes 196
  8.5 14.0 %copy-start.2 = (f32[16,1024]{1,0:T(8,128)S(1)}, f32[16,1024]{1,0:T(8,128)}, u32[]{:S(2)}) copy-start(f32[16,1024]{1,0:T(8,128)} %fusion.23.fault_ref) | copy-start | bytes 196612
  22.4 1.7 %copy-start.7 = (f32[48,16]{0,1:T(8,128)S(1)}, f32[48,16]{0,1:T(8,128)}, u32[]{:S(2)}) copy-start(f32[48,16]{0,1:T(8,128)} %param.31) | copy-start | bytes 9220
  22.4 1.9 %copy-start = (f32[24,16,1024]{2,1,0:T(8,128)S(1)}, f32[24,16,1024]{2,1,0:T(8,128)}, u32[]{:S(2)}) copy-start(f32[24,16,1024]{2,1,0:T(8,128)} %get-tuple-element.36) | copy-start | bytes 4718596
  25.2 17.0 %copy-start.5 = (f32[1,48,16,16]{1,3,2,0:T(8,128)S(1)}, f32[1,48,16,16]{1,3,2,0:T(8,128)}, u32[]{:S(2)}) copy-start(f32[1,48,16,16]{1,3,2,0:T(8,128)} %param.28) | copy-start | bytes 147460
  25.2 17.1 %copy-start.14 = (s32[2]{0:T(128)S(1)}, s32[2]{0:T(128)}, u32[]{:S(2)}) copy-start(s32[2]{0:T(128)} %constant.79.clone.1) | copy-start | bytes 28
  25.3 17.8 %copy-start.13 = (s32[2]{0:T(128)S(1)}, s32[2]{0:T(128)}, u32[]{:S(2)}) copy-start(s32[2]{0:T(128)} %constant.82.clone.1) | copy-start | bytes 28
  25.7 19.5 %collective-permute-start.3 = (f32[8,384]{1,0:T(8,128)S(1)}, f32[8,384]{1,0:T(8,128)S(1)}, u32[]{:S(2)}, u32[]{:S(2)}) collective-permute-start(f32[8,384]{1,0:T(8,128)S(1)} %squeeze.60), channel_id=1, source_target_pairs={{0,32},{4,36},{8,40},{12,44},{16,48},{20,52},{24,56},{28,60},{32,6... | collective-permute-start | bytes 36872 | tf_op jit(solution)/shard_map/ppermute | solution.py:67
  32.6 12.8 %collective-permute-start.2 = (f32[8,384]{1,0:T(8,128)S(1)}, f32[8,384]{1,0:T(8,128)S(1)}, u32[]{:S(2)}, u32[]{:S(2)}) collective-permute-start(f32[8,384]{1,0:T(8,128)S(1)} %squeeze.59), channel_id=1, source_target_pairs={{0,480},{4,484},{8,488},{12,492},{16,496},{20,500},{24,504},{28,50... | collective-permute-start | bytes 36872 | tf_op jit(solution)/shard_map/ppermute | solution.py:67
  36.5 9.0 %collective-permute-start.1 = (f32[8,384]{1,0:T(8,128)S(1)}, f32[8,384]{1,0:T(8,128)S(1)}, u32[]{:S(2)}, u32[]{:S(2)}) collective-permute-start(f32[8,384]{1,0:T(8,128)S(1)} %squeeze.58), channel_id=1, source_target_pairs={{0,4},{4,8},{8,12},{12,16},{16,20},{20,24},{24,28},{28,32},{32,36}... | collective-permute-start | bytes 36872 | tf_op jit(solution)/shard_map/ppermute | solution.py:67
  38.6 7.2 %collective-permute-start = (f32[8,384]{1,0:T(8,128)S(1)}, f32[8,384]{1,0:T(8,128)S(1)}, u32[]{:S(2)}, u32[]{:S(2)}) collective-permute-start(f32[8,384]{1,0:T(8,128)S(1)} %squeeze.57), channel_id=1, source_target_pairs={{0,508},{4,0},{8,4},{12,8},{16,12},{20,16},{24,20},{28,24},{32,28}... | collective-permute-start | bytes 36872 | tf_op jit(solution)/shard_map/ppermute | solution.py:67
  48.7 13.9 %copy-start.3 = (f32[16,1024]{1,0:T(8,128)S(1)}, f32[16,1024]{1,0:T(8,128)}, u32[]{:S(2)}) copy-start(f32[16,1024]{1,0:T(8,128)} %fusion.23.fault_ref) | copy-start | bytes 196612
  62.6 1.9 %copy-start.1 = (f32[24,16,1024]{2,1,0:T(8,128)S(1)}, f32[24,16,1024]{2,1,0:T(8,128)}, u32[]{:S(2)}) copy-start(f32[24,16,1024]{2,1,0:T(8,128)} %get-tuple-element.40) | copy-start | bytes 4718596
  65.9 95.8 %collective-permute-start.7 = (f32[8,384]{1,0:T(8,128)S(1)}, f32[8,384]{1,0:T(8,128)S(1)}, u32[]{:S(2)}, u32[]{:S(2)}) collective-permute-start(f32[8,384]{1,0:T(8,128)S(1)} %squeeze.64), channel_id=1, source_target_pairs={{0,32},{4,36},{8,40},{12,44},{16,48},{20,52},{24,56},{28,60},{32,6... | collective-permute-start | bytes 36872 | tf_op jit(solution)/shard_map/ppermute | solution.py:67
  71.9 90.0 %collective-permute-start.6 = (f32[8,384]{1,0:T(8,128)S(1)}, f32[8,384]{1,0:T(8,128)S(1)}, u32[]{:S(2)}, u32[]{:S(2)}) collective-permute-start(f32[8,384]{1,0:T(8,128)S(1)} %squeeze.63), channel_id=1, source_target_pairs={{0,480},{4,484},{8,488},{12,492},{16,496},{20,500},{24,504},{28,50... | collective-permute-start | bytes 36872 | tf_op jit(solution)/shard_map/ppermute | solution.py:67
  76.7 85.3 %collective-permute-start.5 = (f32[8,384]{1,0:T(8,128)S(1)}, f32[8,384]{1,0:T(8,128)S(1)}, u32[]{:S(2)}, u32[]{:S(2)}) collective-permute-start(f32[8,384]{1,0:T(8,128)S(1)} %squeeze.62), channel_id=1, source_target_pairs={{0,4},{4,8},{8,12},{12,16},{16,20},{20,24},{24,28},{28,32},{32,36}... | collective-permute-start | bytes 36872 | tf_op jit(solution)/shard_map/ppermute | solution.py:67
  78.7 83.5 %collective-permute-start.4 = (f32[8,384]{1,0:T(8,128)S(1)}, f32[8,384]{1,0:T(8,128)S(1)}, u32[]{:S(2)}, u32[]{:S(2)}) collective-permute-start(f32[8,384]{1,0:T(8,128)S(1)} %squeeze.61), channel_id=1, source_target_pairs={{0,508},{4,0},{8,4},{12,8},{16,12},{20,16},{24,20},{28,24},{32,28}... | collective-permute-start | bytes 36872 | tf_op jit(solution)/shard_map/ppermute | solution.py:67

commit v5 on v3

--- a/solution.py
+++ b/solution.py
@@ -3,6 +3,7 @@
 import numpy as np
 from jax.sharding import Mesh
 from jax.experimental import pallas as pl
+from jax.experimental.pallas import tpu as pltpu
 from jax import lax
 from jax.sharding import PartitionSpec as P
 
@@ -28,37 +29,67 @@
 
 
 def block_scan_kernel(
-    grad_ref, inflow_ref, current_ref, fault_ref, companion_ref, start_ref, weights_ref, out_ref, last_ref
+    grad_ref,
+    picked_ref,
+    spread_ref,
+    current_ref,
+    fault_ref,
+    companion_ref,
+    start_ref,
+    weights_ref,
+    pick_ref,
+    voltage_ref,
+    last_ref,
+    samples_ref,
+    fault_out_ref,
+    inflow_ref,
+    adjoint_ref,
 ):
-    steps = grad_ref.shape[0]
+    steps, scen_rows, node_count = grad_ref.shape
     companion = companion_ref[...]
     fault_table = fault_ref[...]
+    inflow_ref[...] = jnp.dot(
+        picked_ref[...], spread_ref[...], precision=PRECISE, preferred_element_type=jnp.float32
+    )
 
     def one_step(index, adjoint_prev):
         step = steps - 1 - index
+        rows = pl.ds(pl.multiple_of(step * scen_rows, scen_rows), scen_rows)
         right_side = (
             grad_ref[step].astype(jnp.float32)
             + companion * adjoint_prev
-            + inflow_ref[step]
+            + inflow_ref[rows]
             + current_ref[step] * fault_table
         )
         adjoint = jnp.dot(
             right_side.astype(jnp.bfloat16), weights_ref[...], preferred_element_type=jnp.float32
         )
-        out_ref[step] = adjoint
+        adjoint_ref[rows] = adjoint
         return adjoint
 
     last_ref[...] = lax.fori_loop(0, steps, one_step, start_ref[...])
-
-
-def block_scan(grad, inflow, current, fault_table, companion, start, weights):
+    adjoint_block = adjoint_ref[...]
+    samples_ref[...] = jnp.dot(
+        adjoint_block, pick_ref[...], precision=PRECISE, preferred_element_type=jnp.float32
+    )
+    at_fault = jnp.sum(adjoint_block.reshape(steps, scen_rows, node_count) * fault_table[None], axis=2)
+    fault_out_ref[...] = jnp.sum(at_fault * voltage_ref[...], axis=0, keepdims=True)
+
+
+def block_scan(grad, picked, spread, current, fault_table, companion, start, weights, pick, voltage):
+    steps, scen_rows, node_count = grad.shape
     return pl.pallas_call(
         block_scan_kernel,
         out_shape=(
-            jax.ShapeDtypeStruct(inflow.shape, jnp.float32),
             jax.ShapeDtypeStruct(start.shape, jnp.float32),
+            jax.ShapeDtypeStruct((steps * scen_rows, pick.shape[1]), jnp.float32),
+            jax.ShapeDtypeStruct((1, scen_rows), jnp.float32),
         ),
-    )(grad, inflow, current[:, :, None], fault_table, companion, start, weights)
+        scratch_shapes=[
+            pltpu.VMEM((steps * scen_rows, node_count), jnp.float32),
+            pltpu.VMEM((steps * scen_rows, node_count), jnp.float32),
+        ],
+    )(grad, picked, spread, current[:, :, None], fault_table, companion, start, weights, pick, voltage)
 
 
 def passed_along(value, axis, steps):
@@ -130,21 +161,19 @@
             )
             * line_scale[None, :]
         )
-        inflow = jnp.dot(picked, spread_table, precision=PRECISE).reshape(
-            block_len, scen_rows, node_count
-        )
-        adjoint_block, adjoint_next = block_scan(
+        adjoint_next, samples, fault_term = block_scan(
             objective_grad[block_start : block_start + block_len, 0],
-            inflow,
+            picked,
+            spread_table,
             fault_current[block_start : block_start + block_len],
             fault_table,
             companion,
             adjoint_next,
             weights,
-        )
-        samples = jnp.dot(
-            adjoint_block.reshape(block_len * scen_rows, node_count), pick_table, precision=PRECISE
-        )
+            pick_table,
+            fault_voltage[block_start : block_start + block_len],
+        )
+        samples, fault_term = lax.optimization_barrier((samples, fault_term[0]))
         series = (
             jnp.transpose(
                 samples[:, :port_total].reshape(block_len, scen_rows, 4, slot_count), (2, 3, 0, 1)
@@ -156,11 +185,6 @@
             samples[:, port_total:].reshape(block_len, scen_rows, conv_count)
             * conv_drive[0, block_start : block_start + block_len],
             axis=(0, 1),
-        )
-        fault_term = jnp.sum(
-            jnp.sum(adjoint_block * fault_table[None], axis=2)
-            * fault_voltage[block_start : block_start + block_len],
-            axis=0,
         )
         control_local = control_local + control_term
         fault_local = fault_local + fault_term

time: 175 us -> 165 us (0.943)
  the two profiles are of different devices: /device:TPU:25 before, /device:TPU:10 now
where the time goes in v5:
time: 165 us; the launch traced here: 164 us
  blocking collectives  76.7 us (46%)
  starting transfers between devices  32.4 us (20%)
  Pallas kernels  32.1 us (19%)
  local copies, waits for them, and re-layouts  14.5 us (9%)
  other arithmetic  6.41 us (4%)
    psum x3, blocking collectives, sum_both(): fault_value = lax.psum(fault_value, axis)  58.9 us
    ppermute x8, starting transfers between devices, passed_along(): return lax.ppermute(value, axis, pairs)  32.4 us
    pallas_call x2, Pallas kernels, block_scan(): pl.pallas_call(block_scan_kernel, out_shape=(jax.ShapeDtypeStruct(start.s...  32.1 us
    psum x1, blocking collectives, sum_both(): lax.psum((fault_slots.at[scen_index].set(fault_value), control_slots.at[h...  17.8 us
  transfers between devices with their start and end apart: 8, of which 0 were waited for; matrix products, arithmetic and copies ran while one was open for 5% of the time, Pallas kernels for 0%

profile of v5, /device:TPU:10, one launch (start us, length us, event | category | flops | bytes accessed | tf_op | source)
XLA Modules:
  0.0 164.4 jit_solution(583882633296794751)
XLA Ops:
  0.7 2.8 %slice_bitcast_fusion = (bf16[24,16,1024]{2,1,0:T(8,128)(2,1)}, bf16[24,16,1024]{2,1,0:T(8,128)(2,1)}) fusion(bf16[48,1,16,1024]{3,2,0,1:T(8,128)(2,1)} %bitcast.82), kind=kLoop, calls=%fused_computation.2 | loop fusion | bytes 3145728 | tf_op jit(solution)/shard_map/squeeze | solution.py:165
  5.5 0.8 copy.110.spread_ref
  6.4 0.9 copy.111.current_ref
  7.2 0.7 fusion.13.fault_ref
  8.0 0.7 copy.130.voltage_ref
  8.7 0.7 broadcast_multiply_fusion.1.picked_ref
  9.4 16.0 %shard_map.165 = (f32[16,1024]{1,0:T(8,128)}, f32[384,48]{1,0:T(8,128)}, f32[1,16]{1,0:T(1,128)}) custom-call(bf16[24,16,1024]{2,1,0:T(8,128)(2,1)} %get-tuple-element.50.grad_ref, f32[384,32]{1,0:T(8,128)} %broadcast_multiply_fusion.1.picked_ref, f32[32,1024]{1,0:T(8,128)} %copy.110.spread_ref, f32[24,16,1]{2,1,0:T(8,128)} %copy.111.current_ref, ...), custom_call_target="tpu_custom_call" | custom-call | tf_op jit(solution)/shard_map/pallas_call | solution.py:81
  25.5 1.1 copy.112
  26.9 6.8 %collective-permute-start.3 = (f32[8,384]{1,0:T(8,128)S(1)}, f32[8,384]{1,0:T(8,128)S(1)}, u32[]{:S(2)}, u32[]{:S(2)}) collective-permute-start(f32[8,384]{1,0:T(8,128)S(1)} %squeeze.67), channel_id=1, source_target_pairs={{0,32},{4,36},{8,40},{12,44},{16,48},{20,52},{24,56},{28,60},{32,6... | collective-permute-start | bytes 36872 | tf_op jit(solution)/shard_map/ppermute | solution.py:98
  33.9 3.8 %collective-permute-start.2 = (f32[8,384]{1,0:T(8,128)S(1)}, f32[8,384]{1,0:T(8,128)S(1)}, u32[]{:S(2)}, u32[]{:S(2)}) collective-permute-start(f32[8,384]{1,0:T(8,128)S(1)} %squeeze.66), channel_id=1, source_target_pairs={{0,480},{4,484},{8,488},{12,492},{16,496},{20,500},{24,504},{28,50... | collective-permute-start | bytes 36872 | tf_op jit(solution)/shard_map/ppermute | solution.py:98
  37.8 1.9 %collective-permute-start.1 = (f32[8,384]{1,0:T(8,128)S(1)}, f32[8,384]{1,0:T(8,128)S(1)}, u32[]{:S(2)}, u32[]{:S(2)}) collective-permute-start(f32[8,384]{1,0:T(8,128)S(1)} %squeeze.65), channel_id=1, source_target_pairs={{0,4},{4,8},{8,12},{12,16},{16,20},{20,24},{24,28},{28,32},{32,36}... | collective-permute-start | bytes 36872 | tf_op jit(solution)/shard_map/ppermute | solution.py:98
  39.8 3.6 %collective-permute-start = (f32[8,384]{1,0:T(8,128)S(1)}, f32[8,384]{1,0:T(8,128)S(1)}, u32[]{:S(2)}, u32[]{:S(2)}) collective-permute-start(f32[8,384]{1,0:T(8,128)S(1)} %squeeze.64), channel_id=1, source_target_pairs={{0,508},{4,0},{8,4},{12,8},{16,12},{20,16},{24,20},{28,24},{32,28}... | collective-permute-start | bytes 36872 | tf_op jit(solution)/shard_map/ppermute | solution.py:98
  43.6 0.7 and_reduce_fusion.1
  44.3 0.7 and_reduce_fusion
  45.1 0.9 copy.122.current_ref
  45.9 0.7 copy.131.voltage_ref
  47.6 0.6 convolution_bitcast_fusion
  48.7 0.7 broadcast_multiply_fusion.picked_ref
  49.4 16.0 %shard_map.166 = (f32[16,1024]{1,0:T(8,128)}, f32[384,48]{1,0:T(8,128)}, f32[1,16]{1,0:T(1,128)}) custom-call(bf16[24,16,1024]{2,1,0:T(8,128)(2,1)} %get-tuple-element.51.grad_ref, f32[384,32]{1,0:T(8,128)} %broadcast_multiply_fusion.picked_ref, f32[32,1024]{1,0:T(8,128)} %copy.110.spread_ref, f32[24,16,1]{2,1,0:T(8,128)} %copy.122.current_ref, ...), custom_call_target="tpu_custom_call" | custom-call | tf_op jit(solution)/shard_map/pallas_call | solution.py:81
  65.4 1.1 copy.123
  66.9 5.9 %collective-permute-start.7 = (f32[8,384]{1,0:T(8,128)S(1)}, f32[8,384]{1,0:T(8,128)S(1)}, u32[]{:S(2)}, u32[]{:S(2)}) collective-permute-start(f32[8,384]{1,0:T(8,128)S(1)} %squeeze.72), channel_id=1, source_target_pairs={{0,32},{4,36},{8,40},{12,44},{16,48},{20,52},{24,56},{28,60},{32,6... | collective-permute-start | bytes 36872 | tf_op jit(solution)/shard_map/ppermute | solution.py:98
  73.0 4.7 %collective-permute-start.6 = (f32[8,384]{1,0:T(8,128)S(1)}, f32[8,384]{1,0:T(8,128)S(1)}, u32[]{:S(2)}, u32[]{:S(2)}) collective-permute-start(f32[8,384]{1,0:T(8,128)S(1)} %squeeze.71), channel_id=1, source_target_pairs={{0,480},{4,484},{8,488},{12,492},{16,496},{20,500},{24,504},{28,50... | collective-permute-start | bytes 36872 | tf_op jit(solution)/shard_map/ppermute | solution.py:98
  77.8 1.9 %collective-permute-start.5 = (f32[8,384]{1,0:T(8,128)S(1)}, f32[8,384]{1,0:T(8,128)S(1)}, u32[]{:S(2)}, u32[]{:S(2)}) collective-permute-start(f32[8,384]{1,0:T(8,128)S(1)} %squeeze.70), channel_id=1, source_target_pairs={{0,4},{4,8},{8,12},{12,16},{16,20},{20,24},{24,28},{28,32},{32,36}... | collective-permute-start | bytes 36872 | tf_op jit(solution)/shard_map/ppermute | solution.py:98
  79.8 3.6 %collective-permute-start.4 = (f32[8,384]{1,0:T(8,128)S(1)}, f32[8,384]{1,0:T(8,128)S(1)}, u32[]{:S(2)}, u32[]{:S(2)}) collective-permute-start(f32[8,384]{1,0:T(8,128)S(1)} %squeeze.69), channel_id=1, source_target_pairs={{0,508},{4,0},{8,4},{12,8},{16,12},{20,16},{24,20},{28,24},{32,28}... | collective-permute-start | bytes 36872 | tf_op jit(solution)/shard_map/ppermute | solution.py:98
  83.5 2.5 %psum.36 = f32[16]{0:T(128)S(1)} all-reduce(f32[16]{0:T(128)S(1)} %add.84), channel_id=1, replica_groups=mesh['z_hi'=2,'x'=4,'y'=8,'core'=2,'scen'=4] {'core'}, use_global_device_ids=true, to_apply=%region_5.0 | all-reduce | flops 16 | bytes 128 | tf_op jit(solution)/shard_map/psum | solution.py:19
  86.0 20.5 %psum.37 = f32[16]{0:T(128)S(1)} all-reduce(f32[16]{0:T(128)S(1)} %psum.36), channel_id=1, replica_groups=mesh['z_hi'=2,'x'=4,'y'=8,'core'=2,'scen'=4] {'y'}, use_global_device_ids=true, to_apply=%region_6.0 | all-reduce | flops 16 | bytes 128 | tf_op jit(solution)/shard_map/psum | solution.py:19
  106.5 36.0 %psum.38 = f32[16]{0:T(128)S(1)} all-reduce(f32[16]{0:T(128)S(1)} %psum.37), channel_id=1, replica_groups=mesh['z_hi'=2,'x'=4,'y'=8,'core'=2,'scen'=4] {'x'}, use_global_device_ids=true, to_apply=%region_7.0 | all-reduce | flops 16 | bytes 128 | tf_op jit(solution)/shard_map/psum | solution.py:19
  142.7 0.6 fusion.14
  143.3 0.6 fusion.15
  144.0 17.8 %all-reduce = (f32[2,16]{1,0:T(2,128)S(1)}, f32[4,16]{1,0:T(4,128)S(1)}) all-reduce(f32[2,16]{1,0:T(2,128)S(1)} %scatter.6, f32[4,16]{1,0:T(4,128)S(1)} %scatter.9), channel_id=1, replica_groups=mesh['z_hi'=2,'x'=4,'y'=8,'core'=2,'scen'=4] {'z_hi','scen'}, use_global_device_ids=true, to_apply=%region_3.0 | all-reduce | flops 96 | bytes 768 | tf_op jit(solution)/shard_map/psum | solution.py:24
  161.8 0.5 constant_dynamic-slice_fusion
  163.6 0.9 maximum_bitcast_fusion
  (104 shorter events, 6.4 us)
Async XLA Ops:
  0.6 2.8 %copy-start.7 = (s32[1,4,8]{2,1,0:T(4,128)S(1)}, s32[1,4,8]{2,1,0:T(4,128)}, u32[]{:S(2)}) copy-start(s32[1,4,8]{2,1,0:T(4,128)} %param.24) | copy-start | bytes 388
  0.6 2.9 %copy-start.1 = (f32[1,4,8,48,16]{3,4,2,1,0:T(8,128)S(1)}, f32[1,4,8,48,16]{3,4,2,1,0:T(8,128)}, u32[]{:S(2)}) copy-start(f32[1,4,8,48,16]{3,4,2,1,0:T(8,128)} %param.26) | copy-start | bytes 294916
  3.4 1.1 copy-start.11
  3.4 1.3 copy-start.8
  3.4 1.4 copy-start.10
  3.4 1.5 copy-start.9
  4.4 1.9 %copy-start.5 = (f32[48,16]{0,1:T(8,128)S(1)}, f32[48,16]{0,1:T(8,128)}, u32[]{:S(2)}) copy-start(f32[48,16]{0,1:T(8,128)} %param.30) | copy-start | bytes 9220
  4.4 2.8 %copy-start.14 = (s32[16]{0:T(128)S(1)}, s32[16]{0:T(128)}, u32[]{:S(2)}) copy-start(s32[16]{0:T(128)} %param.29) | copy-start | bytes 196
  4.5 3.4 %copy-start.6 = (f32[48,16]{0,1:T(8,128)S(1)}, f32[48,16]{0,1:T(8,128)}, u32[]{:S(2)}) copy-start(f32[48,16]{0,1:T(8,128)} %param.31) | copy-start | bytes 9220
  5.4 4.0 %copy-start = (f32[1024,48]{1,0:T(8,128)}, f32[1024,48]{1,0:T(8,128)S(1)}, u32[]{:S(2)}) copy-start(f32[1024,48]{1,0:T(8,128)S(1)} %convert_element_type.15.pick_ref) | copy-start | bytes 589828
  25.4 18.0 %copy-start.4 = (f32[1,48,16,16]{1,3,2,0:T(8,128)S(1)}, f32[1,48,16,16]{1,3,2,0:T(8,128)}, u32[]{:S(2)}) copy-start(f32[1,48,16,16]{1,3,2,0:T(8,128)} %param.28) | copy-start | bytes 147460
  25.4 18.1 %copy-start.13 = (s32[2]{0:T(128)S(1)}, s32[2]{0:T(128)}, u32[]{:S(2)}) copy-start(s32[2]{0:T(128)} %constant.79.clone.1) | copy-start | bytes 28
  25.5 18.9 %copy-start.12 = (s32[2]{0:T(128)S(1)}, s32[2]{0:T(128)}, u32[]{:S(2)}) copy-start(s32[2]{0:T(128)} %constant.82.clone.1) | copy-start | bytes 28
  26.9 19.9 %collective-permute-start.3 = (f32[8,384]{1,0:T(8,128)S(1)}, f32[8,384]{1,0:T(8,128)S(1)}, u32[]{:S(2)}, u32[]{:S(2)}) collective-permute-start(f32[8,384]{1,0:T(8,128)S(1)} %squeeze.67), channel_id=1, source_target_pairs={{0,32},{4,36},{8,40},{12,44},{16,48},{20,52},{24,56},{28,60},{32,6... | collective-permute-start | bytes 36872 | tf_op jit(solution)/shard_map/ppermute | solution.py:98
  33.9 13.2 %collective-permute-start.2 = (f32[8,384]{1,0:T(8,128)S(1)}, f32[8,384]{1,0:T(8,128)S(1)}, u32[]{:S(2)}, u32[]{:S(2)}) collective-permute-start(f32[8,384]{1,0:T(8,128)S(1)} %squeeze.66), channel_id=1, source_target_pairs={{0,480},{4,484},{8,488},{12,492},{16,496},{20,500},{24,504},{28,50... | collective-permute-start | bytes 36872 | tf_op jit(solution)/shard_map/ppermute | solution.py:98
  37.8 9.4 %collective-permute-start.1 = (f32[8,384]{1,0:T(8,128)S(1)}, f32[8,384]{1,0:T(8,128)S(1)}, u32[]{:S(2)}, u32[]{:S(2)}) collective-permute-start(f32[8,384]{1,0:T(8,128)S(1)} %squeeze.65), channel_id=1, source_target_pairs={{0,4},{4,8},{8,12},{12,16},{16,20},{20,24},{24,28},{28,32},{32,36}... | collective-permute-start | bytes 36872 | tf_op jit(solution)/shard_map/ppermute | solution.py:98
  39.8 7.6 %collective-permute-start = (f32[8,384]{1,0:T(8,128)S(1)}, f32[8,384]{1,0:T(8,128)S(1)}, u32[]{:S(2)}, u32[]{:S(2)}) collective-permute-start(f32[8,384]{1,0:T(8,128)S(1)} %squeeze.64), channel_id=1, source_target_pairs={{0,508},{4,0},{8,4},{12,8},{16,12},{20,16},{24,20},{28,24},{32,28}... | collective-permute-start | bytes 36872 | tf_op jit(solution)/shard_map/ppermute | solution.py:98
  65.4 18.1 %copy-start.15 = (f32[1,16]{1,0:T(1,128)S(1)}, f32[1,16]{1,0:T(1,128)}, u32[]{:S(2)}) copy-start(f32[1,16]{1,0:T(1,128)} %get-tuple-element.39) | copy-start | bytes 196
  65.4 18.1 %copy-start.16 = (f32[1,16]{1,0:T(1,128)S(1)}, f32[1,16]{1,0:T(1,128)}, u32[]{:S(2)}) copy-start(f32[1,16]{1,0:T(1,128)} %get-tuple-element.44) | copy-start | bytes 196
  65.4 77.0 %copy-start.2 = (f32[384,48]{1,0:T(8,128)S(1)}, f32[384,48]{1,0:T(8,128)}, u32[]{:S(2)}) copy-start(f32[384,48]{1,0:T(8,128)} %get-tuple-element.40) | copy-start | bytes 221188
  65.4 77.0 %copy-start.3 = (f32[384,48]{1,0:T(8,128)S(1)}, f32[384,48]{1,0:T(8,128)}, u32[]{:S(2)}) copy-start(f32[384,48]{1,0:T(8,128)} %get-tuple-element.45) | copy-start | bytes 221188
  66.9 95.9 %collective-permute-start.7 = (f32[8,384]{1,0:T(8,128)S(1)}, f32[8,384]{1,0:T(8,128)S(1)}, u32[]{:S(2)}, u32[]{:S(2)}) collective-permute-start(f32[8,384]{1,0:T(8,128)S(1)} %squeeze.72), channel_id=1, source_target_pairs={{0,32},{4,36},{8,40},{12,44},{16,48},{20,52},{24,56},{28,60},{32,6... | collective-permute-start | bytes 36872 | tf_op jit(solution)/shard_map/ppermute | solution.py:98
  73.0 90.0 %collective-permute-start.6 = (f32[8,384]{1,0:T(8,128)S(1)}, f32[8,384]{1,0:T(8,128)S(1)}, u32[]{:S(2)}, u32[]{:S(2)}) collective-permute-start(f32[8,384]{1,0:T(8,128)S(1)} %squeeze.71), channel_id=1, source_target_pairs={{0,480},{4,484},{8,488},{12,492},{16,496},{20,500},{24,504},{28,50... | collective-permute-start | bytes 36872 | tf_op jit(solution)/shard_map/ppermute | solution.py:98
  77.8 85.4 %collective-permute-start.5 = (f32[8,384]{1,0:T(8,128)S(1)}, f32[8,384]{1,0:T(8,128)S(1)}, u32[]{:S(2)}, u32[]{:S(2)}) collective-permute-start(f32[8,384]{1,0:T(8,128)S(1)} %squeeze.70), channel_id=1, source_target_pairs={{0,4},{4,8},{8,12},{12,16},{16,20},{20,24},{24,28},{28,32},{32,36}... | collective-permute-start | bytes 36872 | tf_op jit(solution)/shard_map/ppermute | solution.py:98
  79.8 83.6 %collective-permute-start.4 = (f32[8,384]{1,0:T(8,128)S(1)}, f32[8,384]{1,0:T(8,128)S(1)}, u32[]{:S(2)}, u32[]{:S(2)}) collective-permute-start(f32[8,384]{1,0:T(8,128)S(1)} %squeeze.69), channel_id=1, source_target_pairs={{0,508},{4,0},{8,4},{12,8},{16,12},{20,16},{24,20},{28,24},{32,28}... | collective-permute-start | bytes 36872 | tf_op jit(solution)/shard_map/ppermute | solution.py:98

commit v6 on v5

--- a/solution.py
+++ b/solution.py
@@ -1,3 +1,5 @@
+import functools
+
 import jax
 import jax.numpy as jnp
 import numpy as np
@@ -29,11 +31,10 @@
 
 
 def block_scan_kernel(
+    block_start,
     grad_ref,
     picked_ref,
     spread_ref,
-    current_ref,
-    fault_ref,
     companion_ref,
     start_ref,
     weights_ref,
@@ -47,7 +48,6 @@
 ):
     steps, scen_rows, node_count = grad_ref.shape
     companion = companion_ref[...]
-    fault_table = fault_ref[...]
     inflow_ref[...] = jnp.dot(
         picked_ref[...], spread_ref[...], precision=PRECISE, preferred_element_type=jnp.float32
     )
@@ -59,7 +59,6 @@
             grad_ref[step].astype(jnp.float32)
             + companion * adjoint_prev
             + inflow_ref[rows]
-            + current_ref[step] * fault_table
         )
         adjoint = jnp.dot(
             right_side.astype(jnp.bfloat16), weights_ref[...], preferred_element_type=jnp.float32
@@ -72,14 +71,16 @@
     samples_ref[...] = jnp.dot(
         adjoint_block, pick_ref[...], precision=PRECISE, preferred_element_type=jnp.float32
     )
+    fault_table = spread_ref[pl.ds(spread_ref.shape[0] - scen_rows, scen_rows), :]
     at_fault = jnp.sum(adjoint_block.reshape(steps, scen_rows, node_count) * fault_table[None], axis=2)
-    fault_out_ref[...] = jnp.sum(at_fault * voltage_ref[...], axis=0, keepdims=True)
-
-
-def block_scan(grad, picked, spread, current, fault_table, companion, start, weights, pick, voltage):
+    voltage = voltage_ref[pl.ds(block_start, steps), :]
+    fault_out_ref[...] = jnp.sum(at_fault * voltage, axis=0, keepdims=True)
+
+
+def block_scan(block_start, grad, picked, spread, companion, start, weights, pick, voltage):
     steps, scen_rows, node_count = grad.shape
     return pl.pallas_call(
-        block_scan_kernel,
+        functools.partial(block_scan_kernel, block_start),
         out_shape=(
             jax.ShapeDtypeStruct(start.shape, jnp.float32),
             jax.ShapeDtypeStruct((steps * scen_rows, pick.shape[1]), jnp.float32),
@@ -89,7 +90,7 @@
             pltpu.VMEM((steps * scen_rows, node_count), jnp.float32),
             pltpu.VMEM((steps * scen_rows, node_count), jnp.float32),
         ],
-    )(grad, picked, spread, current[:, :, None], fault_table, companion, start, weights, pick, voltage)
+    )(grad, picked, spread, companion, start, weights, pick, voltage)
 
 
 def passed_along(value, axis, steps):
@@ -138,9 +139,18 @@
         ],
         axis=1,
     ).astype(jnp.float32)
-    spread_table = jnp.transpose(pick_table[:, :port_total])
     line_scale = (line_admittance[0] * live_mask).reshape(port_total)
     fault_table = (node_iota[None, :] == (fault_bus - sub_index * node_count)[:, None]).astype(
+        jnp.float32
+    )
+    spread_table = jnp.concatenate(
+        [
+            (port_node[0].reshape(port_total)[:, None] == node_iota[None, :]).astype(jnp.float32),
+            fault_table,
+        ],
+        axis=0,
+    )
+    scen_eye = (lax.iota(jnp.int32, scen_rows)[:, None] == lax.iota(jnp.int32, scen_rows)[None, :]).astype(
         jnp.float32
     )
     window = later_history[0]
@@ -155,23 +165,28 @@
         block_start = block_id * block_len
         target = block_rows[None, None, :] + line_delay[0][:, :, None] - block_len
         time_table = (target[..., None] == time_iota).astype(jnp.float32)
-        picked = (
-            jnp.einsum("ecji,ecis->jsec", time_table, window, precision=PRECISE).reshape(
-                block_len * scen_rows, port_total
-            )
-            * line_scale[None, :]
+        picked = jnp.concatenate(
+            [
+                jnp.einsum("ecji,ecis->jsec", time_table, window, precision=PRECISE).reshape(
+                    block_len * scen_rows, port_total
+                )
+                * line_scale[None, :],
+                (fault_current[block_start : block_start + block_len, :, None] * scen_eye[None]).reshape(
+                    block_len * scen_rows, scen_rows
+                ),
+            ],
+            axis=1,
         )
         adjoint_next, samples, fault_term = block_scan(
+            block_start,
             objective_grad[block_start : block_start + block_len, 0],
             picked,
             spread_table,
-            fault_current[block_start : block_start + block_len],
-            fault_table,
             companion,
             adjoint_next,
             weights,
             pick_table,
-            fault_voltage[block_start : block_start + block_len],
+            fault_voltage,
         )
         samples, fault_term = lax.optimization_barrier((samples, fault_term[0]))
         series = (

time: 165 us -> 162 us (0.982)
  Pallas kernels: 32.1 us -> 29.9 us
    pallas_call x2, Pallas kernels: 32.1 us -> 29.9 us  [block_scan(): pl.pallas_call(functools.partial(block_scan_kernel, block_start), out_sha...]
    broadcast_in_dim x3 -> x0, local copies, waits for them, and re-layouts: 1.78 us -> none  [block_scan(): current[:, :, None]]
  transfers between devices with their start and end apart: 8 -> 8, of which waited for: 0 -> 0; matrix products, arithmetic and copies ran while one was open for 5% -> 4% of each run, Pallas kernels for 0% -> 0%
where the time goes in v6:
time: 162 us; the launch traced here: 161 us
  blocking collectives  76.8 us (47%)
  starting transfers between devices  32.4 us (20%)
  Pallas kernels  29.9 us (18%)
  local copies, waits for them, and re-layouts  13.7 us (8%)
  other arithmetic  6.16 us (4%)
    psum x3, blocking collectives, sum_both(): fault_value = lax.psum(fault_value, axis)  58.9 us
    ppermute x8, starting transfers between devices, passed_along(): return lax.ppermute(value, axis, pairs)  32.4 us
    pallas_call x2, Pallas kernels, block_scan(): pl.pallas_call(functools.partial(block_scan_kernel, block_start), out_sha...  29.9 us
    psum x1, blocking collectives, sum_both(): lax.psum((fault_slots.at[scen_index].set(fault_value), control_slots.at[h...  17.8 us
  transfers between devices with their start and end apart: 8, of which 0 were waited for; matrix products, arithmetic and copies ran while one was open for 4% of the time, Pallas kernels for 0%

profile of v6, /device:TPU:10, one launch (start us, length us, event | category | flops | bytes accessed | tf_op | source)
XLA Modules:
  0.0 161.2 jit_solution(11398301134548084171)
XLA Ops:
  0.6 0.8 eq.105
  1.6 2.8 %slice_bitcast_fusion = (bf16[24,16,1024]{2,1,0:T(8,128)(2,1)}, bf16[24,16,1024]{2,1,0:T(8,128)(2,1)}) fusion(bf16[48,1,16,1024]{3,2,0,1:T(8,128)(2,1)} %bitcast.78), kind=kLoop, calls=%fused_computation.2 | loop fusion | bytes 3145728 | tf_op jit(solution)/shard_map/squeeze | solution.py:182
  5.0 0.5 convolution_bitcast_fusion.1
  6.3 0.8 copy.98.picked_ref
  7.6 0.8 convert_element_type.24.pick_ref
  8.4 0.7 copy.99.voltage_ref
  9.1 0.7 add_convert_fusion.spread_ref
  9.8 15.0 %shard_map.165 = (f32[16,1024]{1,0:T(8,128)}, f32[384,48]{1,0:T(8,128)}, f32[1,16]{1,0:T(1,128)}) custom-call(bf16[24,16,1024]{2,1,0:T(8,128)(2,1)} %get-tuple-element.50.grad_ref, f32[384,48]{1,0:T(8,128)} %copy.98.picked_ref, f32[48,1024]{1,0:T(8,128)} %add_convert_fusion.spread_ref, f32[1,1024]{1,0:T(1,128)} %companion_ref.3, f32[16,1024]{1,0:T(8,128)} %bitcast.82, ...), custom_call_target="tpu_custom_call" | custom-call | tf_op jit(solution)/shard_map/pallas_call | solution.py:82
  24.8 1.1 copy.100
  26.2 6.8 %collective-permute-start.3 = (f32[8,384]{1,0:T(8,128)S(1)}, f32[8,384]{1,0:T(8,128)S(1)}, u32[]{:S(2)}, u32[]{:S(2)}) collective-permute-start(f32[8,384]{1,0:T(8,128)S(1)} %squeeze.67), channel_id=1, source_target_pairs={{0,32},{4,36},{8,40},{12,44},{16,48},{20,52},{24,56},{28,60},{32,6... | collective-permute-start | bytes 36872 | tf_op jit(solution)/shard_map/ppermute | solution.py:99
  33.2 3.8 %collective-permute-start.2 = (f32[8,384]{1,0:T(8,128)S(1)}, f32[8,384]{1,0:T(8,128)S(1)}, u32[]{:S(2)}, u32[]{:S(2)}) collective-permute-start(f32[8,384]{1,0:T(8,128)S(1)} %squeeze.66), channel_id=1, source_target_pairs={{0,480},{4,484},{8,488},{12,492},{16,496},{20,500},{24,504},{28,50... | collective-permute-start | bytes 36872 | tf_op jit(solution)/shard_map/ppermute | solution.py:99
  37.1 1.9 %collective-permute-start.1 = (f32[8,384]{1,0:T(8,128)S(1)}, f32[8,384]{1,0:T(8,128)S(1)}, u32[]{:S(2)}, u32[]{:S(2)}) collective-permute-start(f32[8,384]{1,0:T(8,128)S(1)} %squeeze.65), channel_id=1, source_target_pairs={{0,4},{4,8},{8,12},{12,16},{16,20},{20,24},{24,28},{28,32},{32,36}... | collective-permute-start | bytes 36872 | tf_op jit(solution)/shard_map/ppermute | solution.py:99
  39.1 3.6 %collective-permute-start = (f32[8,384]{1,0:T(8,128)S(1)}, f32[8,384]{1,0:T(8,128)S(1)}, u32[]{:S(2)}, u32[]{:S(2)}) collective-permute-start(f32[8,384]{1,0:T(8,128)S(1)} %squeeze.64), channel_id=1, source_target_pairs={{0,508},{4,0},{8,4},{12,8},{16,12},{20,16},{24,20},{28,24},{32,28}... | collective-permute-start | bytes 36872 | tf_op jit(solution)/shard_map/ppermute | solution.py:99
  42.9 0.7 and_reduce_fusion.1
  43.6 0.7 and_reduce_fusion
  45.4 0.6 convolution_bitcast_fusion
  46.4 0.8 copy.107.picked_ref
  47.2 15.0 %shard_map.166 = (f32[16,1024]{1,0:T(8,128)}, f32[384,48]{1,0:T(8,128)}, f32[1,16]{1,0:T(1,128)}) custom-call(bf16[24,16,1024]{2,1,0:T(8,128)(2,1)} %get-tuple-element.51.grad_ref, f32[384,48]{1,0:T(8,128)} %copy.107.picked_ref, f32[48,1024]{1,0:T(8,128)} %add_convert_fusion.spread_ref, f32[1,1024]{1,0:T(1,128)} %companion_ref.3, ...), custom_call_target="tpu_custom_call" | custom-call | tf_op jit(solution)/shard_map/pallas_call | solution.py:82
  62.2 1.1 copy.109
  63.7 5.9 %collective-permute-start.7 = (f32[8,384]{1,0:T(8,128)S(1)}, f32[8,384]{1,0:T(8,128)S(1)}, u32[]{:S(2)}, u32[]{:S(2)}) collective-permute-start(f32[8,384]{1,0:T(8,128)S(1)} %squeeze.72), channel_id=1, source_target_pairs={{0,32},{4,36},{8,40},{12,44},{16,48},{20,52},{24,56},{28,60},{32,6... | collective-permute-start | bytes 36872 | tf_op jit(solution)/shard_map/ppermute | solution.py:99
  69.8 4.7 %collective-permute-start.6 = (f32[8,384]{1,0:T(8,128)S(1)}, f32[8,384]{1,0:T(8,128)S(1)}, u32[]{:S(2)}, u32[]{:S(2)}) collective-permute-start(f32[8,384]{1,0:T(8,128)S(1)} %squeeze.71), channel_id=1, source_target_pairs={{0,480},{4,484},{8,488},{12,492},{16,496},{20,500},{24,504},{28,50... | collective-permute-start | bytes 36872 | tf_op jit(solution)/shard_map/ppermute | solution.py:99
  74.6 1.9 %collective-permute-start.5 = (f32[8,384]{1,0:T(8,128)S(1)}, f32[8,384]{1,0:T(8,128)S(1)}, u32[]{:S(2)}, u32[]{:S(2)}) collective-permute-start(f32[8,384]{1,0:T(8,128)S(1)} %squeeze.70), channel_id=1, source_target_pairs={{0,4},{4,8},{8,12},{12,16},{16,20},{20,24},{24,28},{28,32},{32,36}... | collective-permute-start | bytes 36872 | tf_op jit(solution)/shard_map/ppermute | solution.py:99
  76.6 3.6 %collective-permute-start.4 = (f32[8,384]{1,0:T(8,128)S(1)}, f32[8,384]{1,0:T(8,128)S(1)}, u32[]{:S(2)}, u32[]{:S(2)}) collective-permute-start(f32[8,384]{1,0:T(8,128)S(1)} %squeeze.69), channel_id=1, source_target_pairs={{0,508},{4,0},{8,4},{12,8},{16,12},{20,16},{24,20},{28,24},{32,28}... | collective-permute-start | bytes 36872 | tf_op jit(solution)/shard_map/ppermute | solution.py:99
  80.3 2.5 %psum.36 = f32[16]{0:T(128)S(1)} all-reduce(f32[16]{0:T(128)S(1)} %add.84), channel_id=1, replica_groups=mesh['z_hi'=2,'x'=4,'y'=8,'core'=2,'scen'=4] {'core'}, use_global_device_ids=true, to_apply=%region_5.0 | all-reduce | flops 16 | bytes 128 | tf_op jit(solution)/shard_map/psum | solution.py:21
  82.7 20.5 %psum.37 = f32[16]{0:T(128)S(1)} all-reduce(f32[16]{0:T(128)S(1)} %psum.36), channel_id=1, replica_groups=mesh['z_hi'=2,'x'=4,'y'=8,'core'=2,'scen'=4] {'y'}, use_global_device_ids=true, to_apply=%region_6.0 | all-reduce | flops 16 | bytes 128 | tf_op jit(solution)/shard_map/psum | solution.py:21
  103.2 36.0 %psum.38 = f32[16]{0:T(128)S(1)} all-reduce(f32[16]{0:T(128)S(1)} %psum.37), channel_id=1, replica_groups=mesh['z_hi'=2,'x'=4,'y'=8,'core'=2,'scen'=4] {'x'}, use_global_device_ids=true, to_apply=%region_7.0 | all-reduce | flops 16 | bytes 128 | tf_op jit(solution)/shard_map/psum | solution.py:21
  139.4 0.6 fusion.14
  140.1 0.6 fusion.15
  140.8 17.8 %all-reduce = (f32[2,16]{1,0:T(2,128)S(1)}, f32[4,16]{1,0:T(4,128)S(1)}) all-reduce(f32[2,16]{1,0:T(2,128)S(1)} %scatter.6, f32[4,16]{1,0:T(4,128)S(1)} %scatter.9), channel_id=1, replica_groups=mesh['z_hi'=2,'x'=4,'y'=8,'core'=2,'scen'=4] {'z_hi','scen'}, use_global_device_ids=true, to_apply=%region_3.0 | all-reduce | flops 96 | bytes 768 | tf_op jit(solution)/shard_map/psum | solution.py:26
  158.6 0.5 constant_dynamic-slice_fusion
  159.1 0.5 dynamic-slice_bitcast_fusion
  160.4 0.9 maximum_bitcast_fusion
  (106 shorter events, 5.7 us)
Async XLA Ops:
  1.6 3.0 %copy-start.4 = (f32[48,16]{0,1:T(8,128)S(1)}, f32[48,16]{0,1:T(8,128)}, u32[]{:S(2)}) copy-start(f32[48,16]{0,1:T(8,128)} %param.30) | copy-start | bytes 9220
  1.6 3.3 %copy-start.6 = (s32[1,4,8]{2,1,0:T(4,128)S(1)}, s32[1,4,8]{2,1,0:T(4,128)}, u32[]{:S(2)}) copy-start(s32[1,4,8]{2,1,0:T(4,128)} %param.24) | copy-start | bytes 388
  1.6 3.4 %copy-start = (f32[1,4,8,48,16]{3,4,2,1,0:T(8,128)S(1)}, f32[1,4,8,48,16]{3,4,2,1,0:T(8,128)}, u32[]{:S(2)}) copy-start(f32[1,4,8,48,16]{3,4,2,1,0:T(8,128)} %param.26) | copy-start | bytes 294916
  4.4 1.5 copy-start.9
  4.4 1.7 %copy-start.7 = (f32[1,4,8]{2,1,0:T(4,128)S(1)}, f32[1,4,8]{2,1,0:T(4,128)}, u32[]{:S(2)}) copy-start(f32[1,4,8]{2,1,0:T(4,128)} %param.25) | copy-start | bytes 388
  4.4 2.7 %copy-start.12 = (s32[16]{0:T(128)S(1)}, s32[16]{0:T(128)}, u32[]{:S(2)}) copy-start(s32[16]{0:T(128)} %param.29) | copy-start | bytes 196
  4.4 2.8 %copy-start.8 = (s32[1,16]{1,0:T(1,128)S(1)}, s32[1,16]{1,0:T(1,128)}, u32[]{:S(2)}) copy-start(s32[1,16]{1,0:T(1,128)} %param.27) | copy-start | bytes 196
  5.0 3.4 %copy-start.5 = (f32[48,16]{0,1:T(8,128)S(1)}, f32[48,16]{0,1:T(8,128)}, u32[]{:S(2)}) copy-start(f32[48,16]{0,1:T(8,128)} %param.31) | copy-start | bytes 9220
  24.7 18.0 %copy-start.3 = (f32[1,48,16,16]{1,3,2,0:T(8,128)S(1)}, f32[1,48,16,16]{1,3,2,0:T(8,128)}, u32[]{:S(2)}) copy-start(f32[1,48,16,16]{1,3,2,0:T(8,128)} %param.28) | copy-start | bytes 147460
  24.7 18.1 %copy-start.11 = (s32[2]{0:T(128)S(1)}, s32[2]{0:T(128)}, u32[]{:S(2)}) copy-start(s32[2]{0:T(128)} %constant.79.clone.1) | copy-start | bytes 28
  24.7 18.9 %copy-start.10 = (s32[2]{0:T(128)S(1)}, s32[2]{0:T(128)}, u32[]{:S(2)}) copy-start(s32[2]{0:T(128)} %constant.82.clone.1) | copy-start | bytes 28
  26.2 18.4 %collective-permute-start.3 = (f32[8,384]{1,0:T(8,128)S(1)}, f32[8,384]{1,0:T(8,128)S(1)}, u32[]{:S(2)}, u32[]{:S(2)}) collective-permute-start(f32[8,384]{1,0:T(8,128)S(1)} %squeeze.67), channel_id=1, source_target_pairs={{0,32},{4,36},{8,40},{12,44},{16,48},{20,52},{24,56},{28,60},{32,6... | collective-permute-start | bytes 36872 | tf_op jit(solution)/shard_map/ppermute | solution.py:99
  33.2 11.7 %collective-permute-start.2 = (f32[8,384]{1,0:T(8,128)S(1)}, f32[8,384]{1,0:T(8,128)S(1)}, u32[]{:S(2)}, u32[]{:S(2)}) collective-permute-start(f32[8,384]{1,0:T(8,128)S(1)} %squeeze.66), channel_id=1, source_target_pairs={{0,480},{4,484},{8,488},{12,492},{16,496},{20,500},{24,504},{28,50... | collective-permute-start | bytes 36872 | tf_op jit(solution)/shard_map/ppermute | solution.py:99
  37.1 7.9 %collective-permute-start.1 = (f32[8,384]{1,0:T(8,128)S(1)}, f32[8,384]{1,0:T(8,128)S(1)}, u32[]{:S(2)}, u32[]{:S(2)}) collective-permute-start(f32[8,384]{1,0:T(8,128)S(1)} %squeeze.65), channel_id=1, source_target_pairs={{0,4},{4,8},{8,12},{12,16},{16,20},{20,24},{24,28},{28,32},{32,36}... | collective-permute-start | bytes 36872 | tf_op jit(solution)/shard_map/ppermute | solution.py:99
  39.1 6.1 %collective-permute-start = (f32[8,384]{1,0:T(8,128)S(1)}, f32[8,384]{1,0:T(8,128)S(1)}, u32[]{:S(2)}, u32[]{:S(2)}) collective-permute-start(f32[8,384]{1,0:T(8,128)S(1)} %squeeze.64), channel_id=1, source_target_pairs={{0,508},{4,0},{8,4},{12,8},{16,12},{20,16},{24,20},{28,24},{32,28}... | collective-permute-start | bytes 36872 | tf_op jit(solution)/shard_map/ppermute | solution.py:99
  62.2 18.1 %copy-start.13 = (f32[1,16]{1,0:T(1,128)S(1)}, f32[1,16]{1,0:T(1,128)}, u32[]{:S(2)}) copy-start(f32[1,16]{1,0:T(1,128)} %get-tuple-element.39) | copy-start | bytes 196
  62.2 18.1 %copy-start.14 = (f32[1,16]{1,0:T(1,128)S(1)}, f32[1,16]{1,0:T(1,128)}, u32[]{:S(2)}) copy-start(f32[1,16]{1,0:T(1,128)} %get-tuple-element.44) | copy-start | bytes 196
  62.2 77.0 %copy-start.1 = (f32[384,48]{1,0:T(8,128)S(1)}, f32[384,48]{1,0:T(8,128)}, u32[]{:S(2)}) copy-start(f32[384,48]{1,0:T(8,128)} %get-tuple-element.40) | copy-start | bytes 221188
  62.2 77.0 %copy-start.2 = (f32[384,48]{1,0:T(8,128)S(1)}, f32[384,48]{1,0:T(8,128)}, u32[]{:S(2)}) copy-start(f32[384,48]{1,0:T(8,128)} %get-tuple-element.45) | copy-start | bytes 221188
  63.7 95.9 %collective-permute-start.7 = (f32[8,384]{1,0:T(8,128)S(1)}, f32[8,384]{1,0:T(8,128)S(1)}, u32[]{:S(2)}, u32[]{:S(2)}) collective-permute-start(f32[8,384]{1,0:T(8,128)S(1)} %squeeze.72), channel_id=1, source_target_pairs={{0,32},{4,36},{8,40},{12,44},{16,48},{20,52},{24,56},{28,60},{32,6... | collective-permute-start | bytes 36872 | tf_op jit(solution)/shard_map/ppermute | solution.py:99
  69.8 90.0 %collective-permute-start.6 = (f32[8,384]{1,0:T(8,128)S(1)}, f32[8,384]{1,0:T(8,128)S(1)}, u32[]{:S(2)}, u32[]{:S(2)}) collective-permute-start(f32[8,384]{1,0:T(8,128)S(1)} %squeeze.71), channel_id=1, source_target_pairs={{0,480},{4,484},{8,488},{12,492},{16,496},{20,500},{24,504},{28,50... | collective-permute-start | bytes 36872 | tf_op jit(solution)/shard_map/ppermute | solution.py:99
  74.6 85.4 %collective-permute-start.5 = (f32[8,384]{1,0:T(8,128)S(1)}, f32[8,384]{1,0:T(8,128)S(1)}, u32[]{:S(2)}, u32[]{:S(2)}) collective-permute-start(f32[8,384]{1,0:T(8,128)S(1)} %squeeze.70), channel_id=1, source_target_pairs={{0,4},{4,8},{8,12},{12,16},{16,20},{20,24},{24,28},{28,32},{32,36}... | collective-permute-start | bytes 36872 | tf_op jit(solution)/shard_map/ppermute | solution.py:99
  76.6 83.6 %collective-permute-start.4 = (f32[8,384]{1,0:T(8,128)S(1)}, f32[8,384]{1,0:T(8,128)S(1)}, u32[]{:S(2)}, u32[]{:S(2)}) collective-permute-start(f32[8,384]{1,0:T(8,128)S(1)} %squeeze.69), channel_id=1, source_target_pairs={{0,508},{4,0},{8,4},{12,8},{16,12},{20,16},{24,20},{28,24},{32,28}... | collective-permute-start | bytes 36872 | tf_op jit(solution)/shard_map/ppermute | solution.py:99

commit v7 on v6

--- a/solution.py
+++ b/solution.py
@@ -1,5 +1,3 @@
-import functools
-
 import jax
 import jax.numpy as jnp
 import numpy as np
@@ -19,47 +17,34 @@
 def sum_both(fault_value, control_value):
     for axis in reversed(SUB[1:]):
         fault_value = lax.psum(fault_value, axis)
-    scen_index = lax.axis_index("scen")
-    high_index = lax.axis_index(SUB[0])
-    fault_slots = jnp.zeros((lax.axis_size("scen"),) + fault_value.shape, jnp.float32)
-    control_slots = jnp.zeros((lax.axis_size(SUB[0]),) + control_value.shape, jnp.float32)
+    fault_mask = (lax.iota(jnp.int32, lax.axis_size("scen")) == lax.axis_index("scen")).astype(
+        jnp.float32
+    )[:, None]
+    control_mask = (lax.iota(jnp.int32, lax.axis_size(SUB[0])) == lax.axis_index(SUB[0])).astype(
+        jnp.float32
+    )[:, None]
     fault_slots, control_slots = lax.psum(
-        (fault_slots.at[scen_index].set(fault_value), control_slots.at[high_index].set(control_value)),
-        (SUB[0], "scen"),
-    )
-    return fault_slots[scen_index], control_slots[high_index]
+        (fault_mask * fault_value[None], control_mask * control_value[None]), (SUB[0], "scen")
+    )
+    return jnp.sum(fault_slots * fault_mask, axis=0), jnp.sum(control_slots * control_mask, axis=0)
 
 
 def block_scan_kernel(
-    block_start,
-    grad_ref,
-    picked_ref,
-    spread_ref,
-    companion_ref,
-    start_ref,
-    weights_ref,
-    pick_ref,
-    voltage_ref,
-    last_ref,
-    samples_ref,
-    fault_out_ref,
-    inflow_ref,
-    adjoint_ref,
+    grad_ref, picked_ref, table_ref, companion_ref, start_ref, weights_ref, last_ref, samples_ref, inflow_ref, adjoint_ref
 ):
     steps, scen_rows, node_count = grad_ref.shape
     companion = companion_ref[...]
     inflow_ref[...] = jnp.dot(
-        picked_ref[...], spread_ref[...], precision=PRECISE, preferred_element_type=jnp.float32
+        picked_ref[...],
+        table_ref[pl.ds(0, picked_ref.shape[1]), :],
+        precision=PRECISE,
+        preferred_element_type=jnp.float32,
     )
 
     def one_step(index, adjoint_prev):
         step = steps - 1 - index
         rows = pl.ds(pl.multiple_of(step * scen_rows, scen_rows), scen_rows)
-        right_side = (
-            grad_ref[step].astype(jnp.float32)
-            + companion * adjoint_prev
-            + inflow_ref[rows]
-        )
+        right_side = grad_ref[step].astype(jnp.float32) + companion * adjoint_prev + inflow_ref[rows]
         adjoint = jnp.dot(
             right_side.astype(jnp.bfloat16), weights_ref[...], preferred_element_type=jnp.float32
         )
@@ -67,30 +52,28 @@
         return adjoint
 
     last_ref[...] = lax.fori_loop(0, steps, one_step, start_ref[...])
-    adjoint_block = adjoint_ref[...]
-    samples_ref[...] = jnp.dot(
-        adjoint_block, pick_ref[...], precision=PRECISE, preferred_element_type=jnp.float32
-    )
-    fault_table = spread_ref[pl.ds(spread_ref.shape[0] - scen_rows, scen_rows), :]
-    at_fault = jnp.sum(adjoint_block.reshape(steps, scen_rows, node_count) * fault_table[None], axis=2)
-    voltage = voltage_ref[pl.ds(block_start, steps), :]
-    fault_out_ref[...] = jnp.sum(at_fault * voltage, axis=0, keepdims=True)
-
-
-def block_scan(block_start, grad, picked, spread, companion, start, weights, pick, voltage):
+    samples_ref[...] = lax.dot_general(
+        table_ref[...],
+        adjoint_ref[...],
+        (((1,), (1,)), ((), ())),
+        precision=PRECISE,
+        preferred_element_type=jnp.float32,
+    )
+
+
+def block_scan(grad, picked, table, companion, start, weights):
     steps, scen_rows, node_count = grad.shape
     return pl.pallas_call(
-        functools.partial(block_scan_kernel, block_start),
+        block_scan_kernel,
         out_shape=(
             jax.ShapeDtypeStruct(start.shape, jnp.float32),
-            jax.ShapeDtypeStruct((steps * scen_rows, pick.shape[1]), jnp.float32),
-            jax.ShapeDtypeStruct((1, scen_rows), jnp.float32),
+            jax.ShapeDtypeStruct((table.shape[0], steps * scen_rows), jnp.float32),
         ),
         scratch_shapes=[
             pltpu.VMEM((steps * scen_rows, node_count), jnp.float32),
             pltpu.VMEM((steps * scen_rows, node_count), jnp.float32),
         ],
-    )(grad, picked, spread, companion, start, weights, pick, voltage)
+    )(grad, picked, table, companion, start, weights)
 
 
 def passed_along(value, axis, steps):
@@ -132,21 +115,15 @@
         jnp.float32
     )
     node_iota = lax.iota(jnp.int32, node_count)
-    pick_table = jnp.concatenate(
-        [
-            node_iota[:, None] == port_node[0].reshape(port_total)[None, :],
-            node_iota[:, None] == conv_node[0][None, :],
-        ],
-        axis=1,
-    ).astype(jnp.float32)
     line_scale = (line_admittance[0] * live_mask).reshape(port_total)
     fault_table = (node_iota[None, :] == (fault_bus - sub_index * node_count)[:, None]).astype(
         jnp.float32
     )
-    spread_table = jnp.concatenate(
+    node_table = jnp.concatenate(
         [
             (port_node[0].reshape(port_total)[:, None] == node_iota[None, :]).astype(jnp.float32),
             fault_table,
+            (conv_node[0][:, None] == node_iota[None, :]).astype(jnp.float32),
         ],
         axis=0,
     )
@@ -177,29 +154,28 @@
             ],
             axis=1,
         )
-        adjoint_next, samples, fault_term = block_scan(
-            block_start,
+        adjoint_next, samples = block_scan(
             objective_grad[block_start : block_start + block_len, 0],
             picked,
-            spread_table,
+            node_table,
             companion,
             adjoint_next,
             weights,
-            pick_table,
-            fault_voltage,
-        )
-        samples, fault_term = lax.optimization_barrier((samples, fault_term[0]))
-        series = (
-            jnp.transpose(
-                samples[:, :port_total].reshape(block_len, scen_rows, 4, slot_count), (2, 3, 0, 1)
-            )
-            * live_mask[:, :, None, None]
-        )
-        outbound = series.reshape(4, slot_count, block_len * scen_rows)
+        )
+        samples = lax.optimization_barrier(samples)
+        outbound = samples[:port_total].reshape(4, slot_count, block_len * scen_rows) * live_mask[
+            :, :, None
+        ]
+        at_fault = jnp.sum(
+            samples[port_total : port_total + scen_rows].reshape(scen_rows, block_len, scen_rows)
+            * scen_eye[:, None, :],
+            axis=0,
+        )
+        fault_term = jnp.sum(at_fault * fault_voltage[block_start : block_start + block_len], axis=0)
+        at_conv = samples[port_total + scen_rows :].reshape(conv_count, block_len, scen_rows)
         control_term = jnp.sum(
-            samples[:, port_total:].reshape(block_len, scen_rows, conv_count)
-            * conv_drive[0, block_start : block_start + block_len],
-            axis=(0, 1),
+            at_conv * jnp.transpose(conv_drive[0, block_start : block_start + block_len], (2, 0, 1)),
+            axis=(1, 2),
         )
         control_local = control_local + control_term
         fault_local = fault_local + fault_term
@@ -208,6 +184,9 @@
                 passed_along(outbound[opposite[direction]], SUB, -offsets[direction])
                 for direction in range(4)
             ]
+        )
+        received, fault_local, control_local = lax.optimization_barrier(
+            (received, fault_local, control_local)
         )
         window = jnp.concatenate(
             [received.reshape(4, slot_count, block_len, scen_rows), window[:, :, :block_len]],

time: 162 us -> 166 us (1.025)
  the two profiles are of different devices: /device:TPU:10 before, /device:TPU:2 now
where the time goes in v7:
time: 166 us; the launch traced here: 165 us
  blocking collectives  51.3 us (31%)
  starting transfers between devices  45.5 us (27%)
  Pallas kernels  29.9 us (18%)
  waiting for transfers between devices  18.5 us (11%)
  other arithmetic  8.56 us (5%)
  local copies, waits for them, and re-layouts  8.4 us (5%)
  matrix products  2 us (1%)
    ppermute x8, starting transfers between devices, passed_along(): return lax.ppermute(value, axis, pairs)  45.5 us
    psum x3, blocking collectives, sum_both(): fault_value = lax.psum(fault_value, axis)  35.8 us
    pallas_call x2, Pallas kernels, block_scan(): pl.pallas_call(block_scan_kernel, out_shape=(jax.ShapeDtypeStruct(start.s...  29.9 us
    ppermute x8, waiting for transfers between devices, passed_along(): return lax.ppermute(value, axis, pairs)  18.5 us
    psum x1, blocking collectives, sum_both(): lax.psum((fault_mask * fault_value[None], control_mask * control_value[No...  15.5 us
  transfers between devices with their start and end apart: 8, of which 2 were waited for; matrix products, arithmetic and copies ran while one was open for 1% of the time, Pallas kernels for 0%

profile of v7, /device:TPU:2, one launch (start us, length us, event | category | flops | bytes accessed | tf_op | source)
XLA Modules:
  0.0 165.2 jit_solution(8800798747467766591)
XLA Ops:
  0.7 0.9 eq.128
  1.9 0.8 fusion.19
  3.0 0.7 fusion.14
  3.8 0.8 squeeze.51
  4.6 0.8 add_add_fusion
  5.4 1.4 convolution_bitcast_fusion.1
  7.3 0.8 copy.75.picked_ref
  8.1 1.3 slice_bitcast_fusion
  9.5 0.7 add_convert_fusion.table_ref
  10.2 15.0 %shard_map.165 = (f32[16,1024]{1,0:T(8,128)}, f32[64,384]{1,0:T(8,128)}) custom-call(bf16[24,16,1024]{2,1,0:T(8,128)(2,1)} %get-tuple-element.30.grad_ref, f32[384,48]{1,0:T(8,128)} %copy.75.picked_ref, f32[64,1024]{1,0:T(8,128)} %add_convert_fusion.table_ref, f32[1,1024]{1,0:T(1,128)} %companion_ref.3, f32[16,1024]{1,0:T(8,128)} %bitcast.81, ...), custom_call_target="tpu_custom_call" | custom-call | tf_op jit(solution)/shard_map/pallas_call | solution.py:66
  25.2 0.9 fusion.8
  26.1 4.8 %collective-permute-start = (f32[8,384]{1,0:T(8,128)S(1)}, f32[8,384]{1,0:T(8,128)S(1)}, u32[]{:S(2)}, u32[]{:S(2)}) collective-permute-start(f32[8,384]{1,0:T(8,128)S(1)} %get-tuple-element.42), channel_id=1, source_target_pairs={{0,508},{4,0},{8,4},{12,8},{16,12},{20,16},{24,20},{28,24},{32,28}... | collective-permute-start | bytes 36872 | tf_op jit(solution)/shard_map/ppermute | solution.py:82
  30.9 1.9 %collective-permute-start.1 = (f32[8,384]{1,0:T(8,128)S(1)}, f32[8,384]{1,0:T(8,128)S(1)}, u32[]{:S(2)}, u32[]{:S(2)}) collective-permute-start(f32[8,384]{1,0:T(8,128)S(1)} %get-tuple-element.45), channel_id=1, source_target_pairs={{0,4},{4,8},{8,12},{12,16},{16,20},{20,24},{24,28},{28,32},{32,36}... | collective-permute-start | bytes 36872 | tf_op jit(solution)/shard_map/ppermute | solution.py:82
  32.8 5.3 %collective-permute-start.2 = (f32[8,384]{1,0:T(8,128)S(1)}, f32[8,384]{1,0:T(8,128)S(1)}, u32[]{:S(2)}, u32[]{:S(2)}) collective-permute-start(f32[8,384]{1,0:T(8,128)S(1)} %get-tuple-element.44), channel_id=1, source_target_pairs={{0,480},{4,484},{8,488},{12,492},{16,496},{20,500},{24,504},{28,50... | collective-permute-start | bytes 36872 | tf_op jit(solution)/shard_map/ppermute | solution.py:82
  38.1 4.4 %collective-permute-start.3 = (f32[8,384]{1,0:T(8,128)S(1)}, f32[8,384]{1,0:T(8,128)S(1)}, u32[]{:S(2)}, u32[]{:S(2)}) collective-permute-start(f32[8,384]{1,0:T(8,128)S(1)} %get-tuple-element.43), channel_id=1, source_target_pairs={{0,32},{4,36},{8,40},{12,44},{16,48},{20,52},{24,56},{28,60},{32,6... | collective-permute-start | bytes 36872 | tf_op jit(solution)/shard_map/ppermute | solution.py:82
  42.7 0.8 fusion.17
  44.6 10.3 %collective-permute-done.3 = f32[8,384]{1,0:T(8,128)S(1)} collective-permute-done((f32[8,384]{1,0:T(8,128)S(1)}, f32[8,384]{1,0:T(8,128)S(1)}, u32[]{:S(2)}, u32[]{:S(2)}) %collective-permute-start.3) | collective-permute-done | bytes 12320 | tf_op jit(solution)/shard_map/ppermute | solution.py:82
  56.2 0.8 copy.81.picked_ref
  57.0 14.9 %shard_map.166 = (f32[16,1024]{1,0:T(8,128)}, f32[64,384]{1,0:T(8,128)}) custom-call(bf16[24,16,1024]{2,1,0:T(8,128)(2,1)} %get-tuple-element.31.grad_ref, f32[384,48]{1,0:T(8,128)} %copy.81.picked_ref, f32[64,1024]{1,0:T(8,128)} %add_convert_fusion.table_ref, f32[1,1024]{1,0:T(1,128)} %companion_ref.3, f32[16,1024]{1,0:T(8,128)} %get-tuple-element.16.start_ref, ...), custom_call_target="tpu_custom_call" | custom-call | tf_op jit(solution)/shard_map/pallas_call | solution.py:66
  72.0 0.8 fusion.16
  72.8 0.9 fusion.7
  73.8 10.6 %collective-permute-start.4 = (f32[8,384]{1,0:T(8,128)S(1)}, f32[8,384]{1,0:T(8,128)S(1)}, u32[]{:S(2)}, u32[]{:S(2)}) collective-permute-start(f32[8,384]{1,0:T(8,128)S(1)} %get-tuple-element.38), channel_id=1, source_target_pairs={{0,508},{4,0},{8,4},{12,8},{16,12},{20,16},{24,20},{28,24},{32,28}... | collective-permute-start | bytes 36872 | tf_op jit(solution)/shard_map/ppermute | solution.py:82
  84.5 1.9 %collective-permute-start.5 = (f32[8,384]{1,0:T(8,128)S(1)}, f32[8,384]{1,0:T(8,128)S(1)}, u32[]{:S(2)}, u32[]{:S(2)}) collective-permute-start(f32[8,384]{1,0:T(8,128)S(1)} %get-tuple-element.41), channel_id=1, source_target_pairs={{0,4},{4,8},{8,12},{12,16},{16,20},{20,24},{24,28},{28,32},{32,36}... | collective-permute-start | bytes 36872 | tf_op jit(solution)/shard_map/ppermute | solution.py:82
  86.4 14.6 %collective-permute-start.6 = (f32[8,384]{1,0:T(8,128)S(1)}, f32[8,384]{1,0:T(8,128)S(1)}, u32[]{:S(2)}, u32[]{:S(2)}) collective-permute-start(f32[8,384]{1,0:T(8,128)S(1)} %get-tuple-element.40), channel_id=1, source_target_pairs={{0,480},{4,484},{8,488},{12,492},{16,496},{20,500},{24,504},{28,50... | collective-permute-start | bytes 36872 | tf_op jit(solution)/shard_map/ppermute | solution.py:82
  101.0 1.9 %collective-permute-start.7 = (f32[8,384]{1,0:T(8,128)S(1)}, f32[8,384]{1,0:T(8,128)S(1)}, u32[]{:S(2)}, u32[]{:S(2)}) collective-permute-start(f32[8,384]{1,0:T(8,128)S(1)} %get-tuple-element.39), channel_id=1, source_target_pairs={{0,32},{4,36},{8,40},{12,44},{16,48},{20,52},{24,56},{28,60},{32,6... | collective-permute-start | bytes 36872 | tf_op jit(solution)/shard_map/ppermute | solution.py:82
  103.2 8.2 %collective-permute-done.7 = f32[8,384]{1,0:T(8,128)S(1)} collective-permute-done((f32[8,384]{1,0:T(8,128)S(1)}, f32[8,384]{1,0:T(8,128)S(1)}, u32[]{:S(2)}, u32[]{:S(2)}) %collective-permute-start.7) | collective-permute-done | bytes 12320 | tf_op jit(solution)/shard_map/ppermute | solution.py:82
  111.4 2.4 %psum.36 = f32[16]{0:T(128)S(1)} all-reduce(f32[16]{0:T(128)S(1)} %add.63), channel_id=1, replica_groups=mesh['z_hi'=2,'x'=4,'y'=8,'core'=2,'scen'=4] {'core'}, use_global_device_ids=true, to_apply=%region_8.0 | all-reduce | flops 16 | bytes 128 | tf_op jit(solution)/shard_map/psum | solution.py:19
  113.8 14.1 %psum.37 = f32[16]{0:T(128)S(1)} all-reduce(f32[16]{0:T(128)S(1)} %psum.36), channel_id=1, replica_groups=mesh['z_hi'=2,'x'=4,'y'=8,'core'=2,'scen'=4] {'y'}, use_global_device_ids=true, to_apply=%region_9.0 | all-reduce | flops 16 | bytes 128 | tf_op jit(solution)/shard_map/psum | solution.py:19
  128.0 19.2 %psum.38 = f32[16]{0:T(128)S(1)} all-reduce(f32[16]{0:T(128)S(1)} %psum.37), channel_id=1, replica_groups=mesh['z_hi'=2,'x'=4,'y'=8,'core'=2,'scen'=4] {'x'}, use_global_device_ids=true, to_apply=%region_10.0 | all-reduce | flops 16 | bytes 128 | tf_op jit(solution)/shard_map/psum | solution.py:19
  147.3 15.5 %all-reduce = (f32[2,16]{1,0:T(2,128)S(1)}, f32[4,16]{1,0:T(4,128)S(1)}) all-reduce(f32[2,16]{1,0:T(2,128)S(1)} %broadcast_multiply_fusion.5, f32[4,16]{1,0:T(4,128)S(1)} %broadcast_multiply_fusion.4), channel_id=1, replica_groups=mesh['z_hi'=2,'x'=4,'y'=8,'core'=2,'scen'=4] {'z_hi','scen'}, use_global_device_ids=true, to_apply=%region_6.0 | all-reduce | flops 96 | bytes 768 | tf_op jit(solution)/shard_map/psum | solution.py:26
  162.8 0.6 multiply_reduce_fusion.2
  164.3 0.9 maximum_bitcast_fusion
  (72 shorter events, 5.2 us)
Async XLA Ops:
  0.6 7.4 %copy-start = (bf16[48,1,16,1024]{3,2,1,0:T(8,128)(2,1)S(1)}, bf16[48,1,16,1024]{3,2,1,0:T(8,128)(2,1)}, u32[]{:S(2)}) copy-start(bf16[48,1,16,1024]{3,2,1,0:T(8,128)(2,1)} %param.15) | copy-start | bytes 4718596
  8.1 1.3 copy-start.5
  8.1 1.3 copy-start.4
  10.2 33.4 %copy-start.2 = (f32[1,48,16,16]{1,3,2,0:T(8,128)S(1)}, f32[1,48,16,16]{1,3,2,0:T(8,128)}, u32[]{:S(2)}) copy-start(f32[1,48,16,16]{1,3,2,0:T(8,128)} %param.24) | copy-start | bytes 147460
  25.2 18.8 %copy-start.3 = (f32[48,16]{0,1:T(8,128)S(1)}, f32[48,16]{0,1:T(8,128)}, u32[]{:S(2)}) copy-start(f32[48,16]{0,1:T(8,128)} %param.27) | copy-start | bytes 9220
  26.1 18.5 %collective-permute-start = (f32[8,384]{1,0:T(8,128)S(1)}, f32[8,384]{1,0:T(8,128)S(1)}, u32[]{:S(2)}, u32[]{:S(2)}) collective-permute-start(f32[8,384]{1,0:T(8,128)S(1)} %get-tuple-element.42), channel_id=1, source_target_pairs={{0,508},{4,0},{8,4},{12,8},{16,12},{20,16},{24,20},{28,24},{32,28}... | collective-permute-start | bytes 36872 | tf_op jit(solution)/shard_map/ppermute | solution.py:82
  30.9 13.7 %collective-permute-start.1 = (f32[8,384]{1,0:T(8,128)S(1)}, f32[8,384]{1,0:T(8,128)S(1)}, u32[]{:S(2)}, u32[]{:S(2)}) collective-permute-start(f32[8,384]{1,0:T(8,128)S(1)} %get-tuple-element.45), channel_id=1, source_target_pairs={{0,4},{4,8},{8,12},{12,16},{16,20},{20,24},{24,28},{28,32},{32,36}... | collective-permute-start | bytes 36872 | tf_op jit(solution)/shard_map/ppermute | solution.py:82
  32.8 11.7 %collective-permute-start.2 = (f32[8,384]{1,0:T(8,128)S(1)}, f32[8,384]{1,0:T(8,128)S(1)}, u32[]{:S(2)}, u32[]{:S(2)}) collective-permute-start(f32[8,384]{1,0:T(8,128)S(1)} %get-tuple-element.44), channel_id=1, source_target_pairs={{0,480},{4,484},{8,488},{12,492},{16,496},{20,500},{24,504},{28,50... | collective-permute-start | bytes 36872 | tf_op jit(solution)/shard_map/ppermute | solution.py:82
  38.1 16.7 %collective-permute-start.3 = (f32[8,384]{1,0:T(8,128)S(1)}, f32[8,384]{1,0:T(8,128)S(1)}, u32[]{:S(2)}, u32[]{:S(2)}) collective-permute-start(f32[8,384]{1,0:T(8,128)S(1)} %get-tuple-element.43), channel_id=1, source_target_pairs={{0,32},{4,36},{8,40},{12,44},{16,48},{20,52},{24,56},{28,60},{32,6... | collective-permute-start | bytes 36872 | tf_op jit(solution)/shard_map/ppermute | solution.py:82
  43.5 11.7 %copy-start.1 = (f32[1,4,8,48,16]{3,4,2,1,0:T(8,128)S(1)}, f32[1,4,8,48,16]{3,4,2,1,0:T(8,128)}, u32[]{:S(2)}) copy-start(f32[1,4,8,48,16]{3,4,2,1,0:T(8,128)} %param.22) | copy-start | bytes 294916
  73.8 29.3 %collective-permute-start.4 = (f32[8,384]{1,0:T(8,128)S(1)}, f32[8,384]{1,0:T(8,128)S(1)}, u32[]{:S(2)}, u32[]{:S(2)}) collective-permute-start(f32[8,384]{1,0:T(8,128)S(1)} %get-tuple-element.38), channel_id=1, source_target_pairs={{0,508},{4,0},{8,4},{12,8},{16,12},{20,16},{24,20},{28,24},{32,28}... | collective-permute-start | bytes 36872 | tf_op jit(solution)/shard_map/ppermute | solution.py:82
  84.5 18.7 %collective-permute-start.5 = (f32[8,384]{1,0:T(8,128)S(1)}, f32[8,384]{1,0:T(8,128)S(1)}, u32[]{:S(2)}, u32[]{:S(2)}) collective-permute-start(f32[8,384]{1,0:T(8,128)S(1)} %get-tuple-element.41), channel_id=1, source_target_pairs={{0,4},{4,8},{8,12},{12,16},{16,20},{20,24},{24,28},{28,32},{32,36}... | collective-permute-start | bytes 36872 | tf_op jit(solution)/shard_map/ppermute | solution.py:82
  86.4 16.8 %collective-permute-start.6 = (f32[8,384]{1,0:T(8,128)S(1)}, f32[8,384]{1,0:T(8,128)S(1)}, u32[]{:S(2)}, u32[]{:S(2)}) collective-permute-start(f32[8,384]{1,0:T(8,128)S(1)} %get-tuple-element.40), channel_id=1, source_target_pairs={{0,480},{4,484},{8,488},{12,492},{16,496},{20,500},{24,504},{28,50... | collective-permute-start | bytes 36872 | tf_op jit(solution)/shard_map/ppermute | solution.py:82
  101.0 10.4 %collective-permute-start.7 = (f32[8,384]{1,0:T(8,128)S(1)}, f32[8,384]{1,0:T(8,128)S(1)}, u32[]{:S(2)}, u32[]{:S(2)}) collective-permute-start(f32[8,384]{1,0:T(8,128)S(1)} %get-tuple-element.39), channel_id=1, source_target_pairs={{0,32},{4,36},{8,40},{12,44},{16,48},{20,52},{24,56},{28,60},{32,6... | collective-permute-start | bytes 36872 | tf_op jit(solution)/shard_map/ppermute | solution.py:82

commit v8 on v6

--- a/solution.py
+++ b/solution.py
@@ -19,15 +19,16 @@
 def sum_both(fault_value, control_value):
     for axis in reversed(SUB[1:]):
         fault_value = lax.psum(fault_value, axis)
-    scen_index = lax.axis_index("scen")
-    high_index = lax.axis_index(SUB[0])
-    fault_slots = jnp.zeros((lax.axis_size("scen"),) + fault_value.shape, jnp.float32)
-    control_slots = jnp.zeros((lax.axis_size(SUB[0]),) + control_value.shape, jnp.float32)
+    fault_mask = (lax.iota(jnp.int32, lax.axis_size("scen")) == lax.axis_index("scen")).astype(
+        jnp.float32
+    )[:, None]
+    control_mask = (lax.iota(jnp.int32, lax.axis_size(SUB[0])) == lax.axis_index(SUB[0])).astype(
+        jnp.float32
+    )[:, None]
     fault_slots, control_slots = lax.psum(
-        (fault_slots.at[scen_index].set(fault_value), control_slots.at[high_index].set(control_value)),
-        (SUB[0], "scen"),
-    )
-    return fault_slots[scen_index], control_slots[high_index]
+        (fault_mask * fault_value[None], control_mask * control_value[None]), (SUB[0], "scen")
+    )
+    return jnp.sum(fault_slots * fault_mask, axis=0), jnp.sum(control_slots * control_mask, axis=0)
 
 
 def block_scan_kernel(

time: 162 us -> 160 us (0.988)
    another operation x4 -> x0, other arithmetic: 2.69 us -> none
  transfers between devices with their start and end apart: 8 -> 8, of which waited for: 0 -> 1; matrix products, arithmetic and copies ran while one was open for 4% -> 2% of each run, Pallas kernels for 0% -> 0%
where the time goes in v8:
time: 160 us; the launch traced here: 159 us
  blocking collectives  76.7 us (48%)
  starting transfers between devices  32.4 us (20%)
  Pallas kernels  29.9 us (19%)
  local copies, waits for them, and re-layouts  12.5 us (8%)
  other arithmetic  4.8 us (3%)
    psum x3, blocking collectives, sum_both(): fault_value = lax.psum(fault_value, axis)  58.9 us
    ppermute x8, starting transfers between devices, passed_along(): return lax.ppermute(value, axis, pairs)  32.4 us
    pallas_call x2, Pallas kernels, block_scan(): pl.pallas_call(functools.partial(block_scan_kernel, block_start), out_sha...  29.9 us
    psum x1, blocking collectives, sum_both(): lax.psum((fault_mask * fault_value[None], control_mask * control_value[No...  17.8 us
  transfers between devices with their start and end apart: 8, of which 1 were waited for; matrix products, arithmetic and copies ran while one was open for 2% of the time, Pallas kernels for 0%

profile of v8, /device:TPU:10, one launch (start us, length us, event | category | flops | bytes accessed | tf_op | source)
XLA Modules:
  0.0 159.1 jit_solution(3118561059597304182)
XLA Ops:
  0.6 0.8 eq.125
  1.6 2.8 %slice_bitcast_fusion = (bf16[24,16,1024]{2,1,0:T(8,128)(2,1)}, bf16[24,16,1024]{2,1,0:T(8,128)(2,1)}) fusion(bf16[48,1,16,1024]{3,2,0,1:T(8,128)(2,1)} %bitcast.71), kind=kLoop, calls=%fused_computation.2 | loop fusion | bytes 3145728 | tf_op jit(solution)/shard_map/squeeze | solution.py:183
  5.0 0.5 convolution_bitcast_fusion.1
  5.5 0.2 copy.118
  6.3 0.8 copy.121.picked_ref
  7.3 0.3 copy.120
  7.6 0.8 convert_element_type.38.pick_ref
  8.4 0.7 copy.122.voltage_ref
  9.1 0.7 add_convert_fusion.spread_ref
  9.8 15.0 %shard_map.165 = (f32[16,1024]{1,0:T(8,128)}, f32[384,48]{1,0:T(8,128)}, f32[1,16]{1,0:T(1,128)}) custom-call(bf16[24,16,1024]{2,1,0:T(8,128)(2,1)} %get-tuple-element.26.grad_ref, f32[384,48]{1,0:T(8,128)} %copy.121.picked_ref, f32[48,1024]{1,0:T(8,128)} %add_convert_fusion.spread_ref, f32[1,1024]{1,0:T(1,128)} %companion_ref.3, f32[16,1024]{1,0:T(8,128)} %bitcast.75, ...), custom_call_target="tpu_custom_call" | custom-call | tf_op jit(solution)/shard_map/pallas_call | solution.py:83
  24.8 1.1 copy.123
  26.2 6.8 %collective-permute-start.3 = (f32[8,384]{1,0:T(8,128)S(1)}, f32[8,384]{1,0:T(8,128)S(1)}, u32[]{:S(2)}, u32[]{:S(2)}) collective-permute-start(f32[8,384]{1,0:T(8,128)S(1)} %squeeze.64), channel_id=1, source_target_pairs={{0,32},{4,36},{8,40},{12,44},{16,48},{20,52},{24,56},{28,60},{32,6... | collective-permute-start | bytes 36872 | tf_op jit(solution)/shard_map/ppermute | solution.py:100
  33.2 3.8 %collective-permute-start.2 = (f32[8,384]{1,0:T(8,128)S(1)}, f32[8,384]{1,0:T(8,128)S(1)}, u32[]{:S(2)}, u32[]{:S(2)}) collective-permute-start(f32[8,384]{1,0:T(8,128)S(1)} %squeeze.63), channel_id=1, source_target_pairs={{0,480},{4,484},{8,488},{12,492},{16,496},{20,500},{24,504},{28,50... | collective-permute-start | bytes 36872 | tf_op jit(solution)/shard_map/ppermute | solution.py:100
  37.1 1.9 %collective-permute-start.1 = (f32[8,384]{1,0:T(8,128)S(1)}, f32[8,384]{1,0:T(8,128)S(1)}, u32[]{:S(2)}, u32[]{:S(2)}) collective-permute-start(f32[8,384]{1,0:T(8,128)S(1)} %squeeze.62), channel_id=1, source_target_pairs={{0,4},{4,8},{8,12},{12,16},{16,20},{20,24},{24,28},{28,32},{32,36}... | collective-permute-start | bytes 36872 | tf_op jit(solution)/shard_map/ppermute | solution.py:100
  39.1 3.6 %collective-permute-start = (f32[8,384]{1,0:T(8,128)S(1)}, f32[8,384]{1,0:T(8,128)S(1)}, u32[]{:S(2)}, u32[]{:S(2)}) collective-permute-start(f32[8,384]{1,0:T(8,128)S(1)} %squeeze.61), channel_id=1, source_target_pairs={{0,508},{4,0},{8,4},{12,8},{16,12},{20,16},{24,20},{28,24},{32,28}... | collective-permute-start | bytes 36872 | tf_op jit(solution)/shard_map/ppermute | solution.py:100
  43.8 0.4 collective-permute-done
  44.3 0.6 convolution_bitcast_fusion
  44.9 0.2 copy.128
  45.3 0.8 copy.130.picked_ref
  46.1 15.0 %shard_map.166 = (f32[16,1024]{1,0:T(8,128)}, f32[384,48]{1,0:T(8,128)}, f32[1,16]{1,0:T(1,128)}) custom-call(bf16[24,16,1024]{2,1,0:T(8,128)(2,1)} %get-tuple-element.27.grad_ref, f32[384,48]{1,0:T(8,128)} %copy.130.picked_ref, f32[48,1024]{1,0:T(8,128)} %add_convert_fusion.spread_ref, f32[1,1024]{1,0:T(1,128)} %companion_ref.3, ...), custom_call_target="tpu_custom_call" | custom-call | tf_op jit(solution)/shard_map/pallas_call | solution.py:83
  61.1 1.1 copy.132
  62.6 5.9 %collective-permute-start.7 = (f32[8,384]{1,0:T(8,128)S(1)}, f32[8,384]{1,0:T(8,128)S(1)}, u32[]{:S(2)}, u32[]{:S(2)}) collective-permute-start(f32[8,384]{1,0:T(8,128)S(1)} %squeeze.69), channel_id=1, source_target_pairs={{0,32},{4,36},{8,40},{12,44},{16,48},{20,52},{24,56},{28,60},{32,6... | collective-permute-start | bytes 36872 | tf_op jit(solution)/shard_map/ppermute | solution.py:100
  68.7 4.7 %collective-permute-start.6 = (f32[8,384]{1,0:T(8,128)S(1)}, f32[8,384]{1,0:T(8,128)S(1)}, u32[]{:S(2)}, u32[]{:S(2)}) collective-permute-start(f32[8,384]{1,0:T(8,128)S(1)} %squeeze.68), channel_id=1, source_target_pairs={{0,480},{4,484},{8,488},{12,492},{16,496},{20,500},{24,504},{28,50... | collective-permute-start | bytes 36872 | tf_op jit(solution)/shard_map/ppermute | solution.py:100
  73.5 3.0 %collective-permute-start.5 = (f32[8,384]{1,0:T(8,128)S(1)}, f32[8,384]{1,0:T(8,128)S(1)}, u32[]{:S(2)}, u32[]{:S(2)}) collective-permute-start(f32[8,384]{1,0:T(8,128)S(1)} %squeeze.67), channel_id=1, source_target_pairs={{0,4},{4,8},{8,12},{12,16},{16,20},{20,24},{24,28},{28,32},{32,36}... | collective-permute-start | bytes 36872 | tf_op jit(solution)/shard_map/ppermute | solution.py:100
  76.6 2.6 %collective-permute-start.4 = (f32[8,384]{1,0:T(8,128)S(1)}, f32[8,384]{1,0:T(8,128)S(1)}, u32[]{:S(2)}, u32[]{:S(2)}) collective-permute-start(f32[8,384]{1,0:T(8,128)S(1)} %squeeze.66), channel_id=1, source_target_pairs={{0,508},{4,0},{8,4},{12,8},{16,12},{20,16},{24,20},{28,24},{32,28}... | collective-permute-start | bytes 36872 | tf_op jit(solution)/shard_map/ppermute | solution.py:100
  79.2 2.5 %psum.36 = f32[16]{0:T(128)S(1)} all-reduce(f32[16]{0:T(128)S(1)} %add.68), channel_id=1, replica_groups=mesh['z_hi'=2,'x'=4,'y'=8,'core'=2,'scen'=4] {'core'}, use_global_device_ids=true, to_apply=%region_4.0 | all-reduce | flops 16 | bytes 128 | tf_op jit(solution)/shard_map/psum | solution.py:21
  81.7 20.5 %psum.37 = f32[16]{0:T(128)S(1)} all-reduce(f32[16]{0:T(128)S(1)} %psum.36), channel_id=1, replica_groups=mesh['z_hi'=2,'x'=4,'y'=8,'core'=2,'scen'=4] {'y'}, use_global_device_ids=true, to_apply=%region_5.0 | all-reduce | flops 16 | bytes 128 | tf_op jit(solution)/shard_map/psum | solution.py:21
  102.1 36.0 %psum.38 = f32[16]{0:T(128)S(1)} all-reduce(f32[16]{0:T(128)S(1)} %psum.37), channel_id=1, replica_groups=mesh['z_hi'=2,'x'=4,'y'=8,'core'=2,'scen'=4] {'x'}, use_global_device_ids=true, to_apply=%region_6.0 | all-reduce | flops 16 | bytes 128 | tf_op jit(solution)/shard_map/psum | solution.py:21
  138.5 17.8 %all-reduce = (f32[2,16]{1,0:T(2,128)S(1)}, f32[4,16]{1,0:T(4,128)S(1)}) all-reduce(f32[2,16]{1,0:T(2,128)S(1)} %broadcast_multiply_fusion.5, f32[4,16]{1,0:T(4,128)S(1)} %broadcast_multiply_fusion.4), channel_id=1, replica_groups=mesh['z_hi'=2,'x'=4,'y'=8,'core'=2,'scen'=4] {'z_hi','scen'}, use_global_device_ids=true, to_apply=%region_2.0 | all-reduce | flops 96 | bytes 768 | tf_op jit(solution)/shard_map/psum | solution.py:28
  156.3 0.6 multiply_reduce_fusion
  156.9 0.6 multiply_reduce_fusion.1
  158.2 0.9 maximum_bitcast_fusion
  (99 shorter events, 5.2 us)
Async XLA Ops:
  1.6 3.0 %copy-start.4 = (f32[48,16]{0,1:T(8,128)S(1)}, f32[48,16]{0,1:T(8,128)}, u32[]{:S(2)}) copy-start(f32[48,16]{0,1:T(8,128)} %param.26) | copy-start | bytes 9220
  1.6 3.3 %copy-start.6 = (s32[1,4,8]{2,1,0:T(4,128)S(1)}, s32[1,4,8]{2,1,0:T(4,128)}, u32[]{:S(2)}) copy-start(s32[1,4,8]{2,1,0:T(4,128)} %param.20) | copy-start | bytes 388
  1.6 3.4 %copy-start = (f32[1,4,8,48,16]{3,4,2,1,0:T(8,128)S(1)}, f32[1,4,8,48,16]{3,4,2,1,0:T(8,128)}, u32[]{:S(2)}) copy-start(f32[1,4,8,48,16]{3,4,2,1,0:T(8,128)} %param.22) | copy-start | bytes 294916
  4.4 1.5 copy-start.9
  4.4 1.7 %copy-start.7 = (f32[1,4,8]{2,1,0:T(4,128)S(1)}, f32[1,4,8]{2,1,0:T(4,128)}, u32[]{:S(2)}) copy-start(f32[1,4,8]{2,1,0:T(4,128)} %param.21) | copy-start | bytes 388
  4.4 2.7 %copy-start.10 = (s32[16]{0:T(128)S(1)}, s32[16]{0:T(128)}, u32[]{:S(2)}) copy-start(s32[16]{0:T(128)} %param.25) | copy-start | bytes 196
  4.4 2.8 %copy-start.8 = (s32[1,16]{1,0:T(1,128)S(1)}, s32[1,16]{1,0:T(1,128)}, u32[]{:S(2)}) copy-start(s32[1,16]{1,0:T(1,128)} %param.23) | copy-start | bytes 196
  5.0 3.4 %copy-start.5 = (f32[48,16]{0,1:T(8,128)S(1)}, f32[48,16]{0,1:T(8,128)}, u32[]{:S(2)}) copy-start(f32[48,16]{0,1:T(8,128)} %param.27) | copy-start | bytes 9220
  24.7 18.0 %copy-start.3 = (f32[1,48,16,16]{1,3,2,0:T(8,128)S(1)}, f32[1,48,16,16]{1,3,2,0:T(8,128)}, u32[]{:S(2)}) copy-start(f32[1,48,16,16]{1,3,2,0:T(8,128)} %param.24) | copy-start | bytes 147460
  26.2 17.0 %collective-permute-start.3 = (f32[8,384]{1,0:T(8,128)S(1)}, f32[8,384]{1,0:T(8,128)S(1)}, u32[]{:S(2)}, u32[]{:S(2)}) collective-permute-start(f32[8,384]{1,0:T(8,128)S(1)} %squeeze.64), channel_id=1, source_target_pairs={{0,32},{4,36},{8,40},{12,44},{16,48},{20,52},{24,56},{28,60},{32,6... | collective-permute-start | bytes 36872 | tf_op jit(solution)/shard_map/ppermute | solution.py:100
  33.2 10.2 %collective-permute-start.2 = (f32[8,384]{1,0:T(8,128)S(1)}, f32[8,384]{1,0:T(8,128)S(1)}, u32[]{:S(2)}, u32[]{:S(2)}) collective-permute-start(f32[8,384]{1,0:T(8,128)S(1)} %squeeze.63), channel_id=1, source_target_pairs={{0,480},{4,484},{8,488},{12,492},{16,496},{20,500},{24,504},{28,50... | collective-permute-start | bytes 36872 | tf_op jit(solution)/shard_map/ppermute | solution.py:100
  37.1 6.5 %collective-permute-start.1 = (f32[8,384]{1,0:T(8,128)S(1)}, f32[8,384]{1,0:T(8,128)S(1)}, u32[]{:S(2)}, u32[]{:S(2)}) collective-permute-start(f32[8,384]{1,0:T(8,128)S(1)} %squeeze.62), channel_id=1, source_target_pairs={{0,4},{4,8},{8,12},{12,16},{16,20},{20,24},{24,28},{28,32},{32,36}... | collective-permute-start | bytes 36872 | tf_op jit(solution)/shard_map/ppermute | solution.py:100
  39.1 5.0 %collective-permute-start = (f32[8,384]{1,0:T(8,128)S(1)}, f32[8,384]{1,0:T(8,128)S(1)}, u32[]{:S(2)}, u32[]{:S(2)}) collective-permute-start(f32[8,384]{1,0:T(8,128)S(1)} %squeeze.61), channel_id=1, source_target_pairs={{0,508},{4,0},{8,4},{12,8},{16,12},{20,16},{24,20},{28,24},{32,28}... | collective-permute-start | bytes 36872 | tf_op jit(solution)/shard_map/ppermute | solution.py:100
  61.1 18.1 %copy-start.11 = (f32[1,16]{1,0:T(1,128)S(1)}, f32[1,16]{1,0:T(1,128)}, u32[]{:S(2)}) copy-start(f32[1,16]{1,0:T(1,128)} %get-tuple-element.15) | copy-start | bytes 196
  61.1 18.1 %copy-start.12 = (f32[1,16]{1,0:T(1,128)S(1)}, f32[1,16]{1,0:T(1,128)}, u32[]{:S(2)}) copy-start(f32[1,16]{1,0:T(1,128)} %get-tuple-element.20) | copy-start | bytes 196
  61.1 77.0 %copy-start.1 = (f32[384,48]{1,0:T(8,128)S(1)}, f32[384,48]{1,0:T(8,128)}, u32[]{:S(2)}) copy-start(f32[384,48]{1,0:T(8,128)} %get-tuple-element.16) | copy-start | bytes 221188
  61.1 77.0 %copy-start.2 = (f32[384,48]{1,0:T(8,128)S(1)}, f32[384,48]{1,0:T(8,128)}, u32[]{:S(2)}) copy-start(f32[384,48]{1,0:T(8,128)} %get-tuple-element.21) | copy-start | bytes 221188
  62.6 94.8 %collective-permute-start.7 = (f32[8,384]{1,0:T(8,128)S(1)}, f32[8,384]{1,0:T(8,128)S(1)}, u32[]{:S(2)}, u32[]{:S(2)}) collective-permute-start(f32[8,384]{1,0:T(8,128)S(1)} %squeeze.69), channel_id=1, source_target_pairs={{0,32},{4,36},{8,40},{12,44},{16,48},{20,52},{24,56},{28,60},{32,6... | collective-permute-start | bytes 36872 | tf_op jit(solution)/shard_map/ppermute | solution.py:100
  68.7 89.0 %collective-permute-start.6 = (f32[8,384]{1,0:T(8,128)S(1)}, f32[8,384]{1,0:T(8,128)S(1)}, u32[]{:S(2)}, u32[]{:S(2)}) collective-permute-start(f32[8,384]{1,0:T(8,128)S(1)} %squeeze.68), channel_id=1, source_target_pairs={{0,480},{4,484},{8,488},{12,492},{16,496},{20,500},{24,504},{28,50... | collective-permute-start | bytes 36872 | tf_op jit(solution)/shard_map/ppermute | solution.py:100
  73.5 84.4 %collective-permute-start.5 = (f32[8,384]{1,0:T(8,128)S(1)}, f32[8,384]{1,0:T(8,128)S(1)}, u32[]{:S(2)}, u32[]{:S(2)}) collective-permute-start(f32[8,384]{1,0:T(8,128)S(1)} %squeeze.67), channel_id=1, source_target_pairs={{0,4},{4,8},{8,12},{12,16},{16,20},{20,24},{24,28},{28,32},{32,36}... | collective-permute-start | bytes 36872 | tf_op jit(solution)/shard_map/ppermute | solution.py:100
  76.6 81.4 %collective-permute-start.4 = (f32[8,384]{1,0:T(8,128)S(1)}, f32[8,384]{1,0:T(8,128)S(1)}, u32[]{:S(2)}, u32[]{:S(2)}) collective-permute-start(f32[8,384]{1,0:T(8,128)S(1)} %squeeze.66), channel_id=1, source_target_pairs={{0,508},{4,0},{8,4},{12,8},{16,12},{20,16},{24,20},{28,24},{32,28}... | collective-permute-start | bytes 36872 | tf_op jit(solution)/shard_map/ppermute | solution.py:100

commit v9 on v8

--- a/solution.py
+++ b/solution.py
@@ -78,10 +78,28 @@
     fault_out_ref[...] = jnp.sum(at_fault * voltage, axis=0, keepdims=True)
 
 
-def block_scan(block_start, grad, picked, spread, companion, start, weights, pick, voltage):
-    steps, scen_rows, node_count = grad.shape
+def whole(array):
+    return pl.BlockSpec(array.shape, lambda index: (0,) * array.ndim)
+
+
+def block_scan(block_start, steps, grad, picked, spread, companion, start, weights, pick, voltage):
+    _, _, scen_rows, node_count = grad.shape
+    block_id = block_start // steps
+    operands = (grad, picked, spread, companion, start, weights, pick, voltage)
     return pl.pallas_call(
         functools.partial(block_scan_kernel, block_start),
+        grid=(1,),
+        in_specs=[
+            pl.BlockSpec(
+                (steps, None, scen_rows, node_count), lambda index: (block_id, 0, 0, 0)
+            )
+        ]
+        + [whole(array) for array in operands[1:]],
+        out_specs=(
+            whole(start),
+            pl.BlockSpec((steps * scen_rows, pick.shape[1]), lambda index: (0, 0)),
+            pl.BlockSpec((1, scen_rows), lambda index: (0, 0)),
+        ),
         out_shape=(
             jax.ShapeDtypeStruct(start.shape, jnp.float32),
             jax.ShapeDtypeStruct((steps * scen_rows, pick.shape[1]), jnp.float32),
@@ -91,7 +109,7 @@
             pltpu.VMEM((steps * scen_rows, node_count), jnp.float32),
             pltpu.VMEM((steps * scen_rows, node_count), jnp.float32),
         ],
-    )(grad, picked, spread, companion, start, weights, pick, voltage)
+    )(*operands)
 
 
 def passed_along(value, axis, steps):
@@ -180,7 +198,8 @@
         )
         adjoint_next, samples, fault_term = block_scan(
             block_start,
-            objective_grad[block_start : block_start + block_len, 0],
+            block_len,
+            objective_grad,
             picked,
             spread_table,
             companion,

time: 160 us -> 159 us (level)
  local copies, waits for them, and re-layouts: 12.5 us -> 10.5 us
    squeeze x1 -> x0, local copies, waits for them, and re-layouts: 2.77 us -> none  [body(): objective_grad[block_start:block_start + block_len, 0]]
where the time goes in v9:
time: 159 us
  blocking collectives  76.7 us (48%)
  starting transfers between devices  32.4 us (20%)
  Pallas kernels  29.9 us (19%)
  local copies, waits for them, and re-layouts  10.5 us (7%)
  other arithmetic  5.48 us (3%)
  matrix products  2 us (1%)
    psum x3, blocking collectives, sum_both(): fault_value = lax.psum(fault_value, axis)  58.9 us
    ppermute x8, starting transfers between devices, passed_along(): return lax.ppermute(value, axis, pairs)  32.4 us
    pallas_call x2, Pallas kernels, block_scan(): pl.pallas_call(functools.partial(block_scan_kernel, block_start), grid=(1...  29.9 us
    psum x1, blocking collectives, sum_both(): lax.psum((fault_mask * fault_value[None], control_mask * control_value[No...  17.8 us
  transfers between devices with their start and end apart: 8, of which 1 were waited for; matrix products, arithmetic and copies ran while one was open for 2% of the time, Pallas kernels for 0%

profile of v9, /device:TPU:10, one launch (start us, length us, event | category | flops | bytes accessed | tf_op | source)
XLA Modules:
  0.0 158.7 jit_solution(10403889556879460830)
XLA Ops:
  0.7 0.8 eq.125
  1.8 0.8 fusion.20
  3.0 0.8 add_add_fusion
  3.7 1.4 convolution_bitcast_fusion.1
  5.9 0.8 copy.109.picked_ref
  6.9 0.3 copy.108
  7.2 0.8 convert_element_type.38.pick_ref
  8.0 0.7 copy.110.voltage_ref
  8.7 0.7 add_convert_fusion.spread_ref
  9.4 15.0 %shard_map.165 = (f32[16,1024]{1,0:T(8,128)}, f32[384,48]{1,0:T(8,128)}, f32[1,16]{1,0:T(1,128)}) custom-call(bf16[48,1,16,1024]{3,2,1,0:T(8,128)(2,1)} %grad_ref.3, f32[384,48]{1,0:T(8,128)} %copy.109.picked_ref, f32[48,1024]{1,0:T(8,128)} %add_convert_fusion.spread_ref, f32[1,1024]{1,0:T(1,128)} %companion_ref.3, f32[16,1024]{1,0:T(8,128)} %bitcast.68, ...), custom_call_target="tpu_custom_call" | custom-call | tf_op jit(solution)/shard_map/pallas_call | solution.py:89
  24.3 1.1 copy.111
  25.8 6.8 %collective-permute-start.3 = (f32[8,384]{1,0:T(8,128)S(1)}, f32[8,384]{1,0:T(8,128)S(1)}, u32[]{:S(2)}, u32[]{:S(2)}) collective-permute-start(f32[8,384]{1,0:T(8,128)S(1)} %squeeze.56), channel_id=1, source_target_pairs={{0,32},{4,36},{8,40},{12,44},{16,48},{20,52},{24,56},{28,60},{32,6... | collective-permute-start | bytes 36872 | tf_op jit(solution)/shard_map/ppermute | solution.py:118
  32.8 3.8 %collective-permute-start.2 = (f32[8,384]{1,0:T(8,128)S(1)}, f32[8,384]{1,0:T(8,128)S(1)}, u32[]{:S(2)}, u32[]{:S(2)}) collective-permute-start(f32[8,384]{1,0:T(8,128)S(1)} %squeeze.55), channel_id=1, source_target_pairs={{0,480},{4,484},{8,488},{12,492},{16,496},{20,500},{24,504},{28,50... | collective-permute-start | bytes 36872 | tf_op jit(solution)/shard_map/ppermute | solution.py:118
  36.7 1.9 %collective-permute-start.1 = (f32[8,384]{1,0:T(8,128)S(1)}, f32[8,384]{1,0:T(8,128)S(1)}, u32[]{:S(2)}, u32[]{:S(2)}) collective-permute-start(f32[8,384]{1,0:T(8,128)S(1)} %squeeze.54), channel_id=1, source_target_pairs={{0,4},{4,8},{8,12},{12,16},{16,20},{20,24},{24,28},{28,32},{32,36}... | collective-permute-start | bytes 36872 | tf_op jit(solution)/shard_map/ppermute | solution.py:118
  38.7 3.6 %collective-permute-start = (f32[8,384]{1,0:T(8,128)S(1)}, f32[8,384]{1,0:T(8,128)S(1)}, u32[]{:S(2)}, u32[]{:S(2)}) collective-permute-start(f32[8,384]{1,0:T(8,128)S(1)} %squeeze.53), channel_id=1, source_target_pairs={{0,508},{4,0},{8,4},{12,8},{16,12},{20,16},{24,20},{28,24},{32,28}... | collective-permute-start | bytes 36872 | tf_op jit(solution)/shard_map/ppermute | solution.py:118
  43.4 0.4 collective-permute-done
  43.9 0.6 convolution_bitcast_fusion
  44.5 0.2 copy.116
  44.9 0.8 copy.118.picked_ref
  45.8 15.0 %shard_map.166 = (f32[16,1024]{1,0:T(8,128)}, f32[384,48]{1,0:T(8,128)}, f32[1,16]{1,0:T(1,128)}) custom-call(bf16[48,1,16,1024]{3,2,1,0:T(8,128)(2,1)} %grad_ref.3, f32[384,48]{1,0:T(8,128)} %copy.118.picked_ref, f32[48,1024]{1,0:T(8,128)} %add_convert_fusion.spread_ref, f32[1,1024]{1,0:T(1,128)} %companion_ref.3, f32[16,1024]{1,0:T(8,128)} %get-tuple-element.17.start_ref, ...), custom_call_target="tpu_custom_call" | custom-call | tf_op jit(solution)/shard_map/pallas_call | solution.py:89
  60.7 1.1 copy.120
  62.2 5.9 %collective-permute-start.7 = (f32[8,384]{1,0:T(8,128)S(1)}, f32[8,384]{1,0:T(8,128)S(1)}, u32[]{:S(2)}, u32[]{:S(2)}) collective-permute-start(f32[8,384]{1,0:T(8,128)S(1)} %squeeze.61), channel_id=1, source_target_pairs={{0,32},{4,36},{8,40},{12,44},{16,48},{20,52},{24,56},{28,60},{32,6... | collective-permute-start | bytes 36872 | tf_op jit(solution)/shard_map/ppermute | solution.py:118
  68.3 4.7 %collective-permute-start.6 = (f32[8,384]{1,0:T(8,128)S(1)}, f32[8,384]{1,0:T(8,128)S(1)}, u32[]{:S(2)}, u32[]{:S(2)}) collective-permute-start(f32[8,384]{1,0:T(8,128)S(1)} %squeeze.60), channel_id=1, source_target_pairs={{0,480},{4,484},{8,488},{12,492},{16,496},{20,500},{24,504},{28,50... | collective-permute-start | bytes 36872 | tf_op jit(solution)/shard_map/ppermute | solution.py:118
  73.1 3.0 %collective-permute-start.5 = (f32[8,384]{1,0:T(8,128)S(1)}, f32[8,384]{1,0:T(8,128)S(1)}, u32[]{:S(2)}, u32[]{:S(2)}) collective-permute-start(f32[8,384]{1,0:T(8,128)S(1)} %squeeze.59), channel_id=1, source_target_pairs={{0,4},{4,8},{8,12},{12,16},{16,20},{20,24},{24,28},{28,32},{32,36}... | collective-permute-start | bytes 36872 | tf_op jit(solution)/shard_map/ppermute | solution.py:118
  76.2 2.6 %collective-permute-start.4 = (f32[8,384]{1,0:T(8,128)S(1)}, f32[8,384]{1,0:T(8,128)S(1)}, u32[]{:S(2)}, u32[]{:S(2)}) collective-permute-start(f32[8,384]{1,0:T(8,128)S(1)} %squeeze.58), channel_id=1, source_target_pairs={{0,508},{4,0},{8,4},{12,8},{16,12},{20,16},{24,20},{28,24},{32,28}... | collective-permute-start | bytes 36872 | tf_op jit(solution)/shard_map/ppermute | solution.py:118
  78.8 2.5 %psum.36 = f32[16]{0:T(128)S(1)} all-reduce(f32[16]{0:T(128)S(1)} %add.68), channel_id=1, replica_groups=mesh['z_hi'=2,'x'=4,'y'=8,'core'=2,'scen'=4] {'core'}, use_global_device_ids=true, to_apply=%region_4.0 | all-reduce | flops 16 | bytes 128 | tf_op jit(solution)/shard_map/psum | solution.py:21
  81.3 20.5 %psum.37 = f32[16]{0:T(128)S(1)} all-reduce(f32[16]{0:T(128)S(1)} %psum.36), channel_id=1, replica_groups=mesh['z_hi'=2,'x'=4,'y'=8,'core'=2,'scen'=4] {'y'}, use_global_device_ids=true, to_apply=%region_5.0 | all-reduce | flops 16 | bytes 128 | tf_op jit(solution)/shard_map/psum | solution.py:21
  101.8 36.0 %psum.38 = f32[16]{0:T(128)S(1)} all-reduce(f32[16]{0:T(128)S(1)} %psum.37), channel_id=1, replica_groups=mesh['z_hi'=2,'x'=4,'y'=8,'core'=2,'scen'=4] {'x'}, use_global_device_ids=true, to_apply=%region_6.0 | all-reduce | flops 16 | bytes 128 | tf_op jit(solution)/shard_map/psum | solution.py:21
  138.1 17.8 %all-reduce = (f32[2,16]{1,0:T(2,128)S(1)}, f32[4,16]{1,0:T(4,128)S(1)}) all-reduce(f32[2,16]{1,0:T(2,128)S(1)} %broadcast_multiply_fusion.5, f32[4,16]{1,0:T(4,128)S(1)} %broadcast_multiply_fusion.4), channel_id=1, replica_groups=mesh['z_hi'=2,'x'=4,'y'=8,'core'=2,'scen'=4] {'z_hi','scen'}, use_global_device_ids=true, to_apply=%region_2.0 | all-reduce | flops 96 | bytes 768 | tf_op jit(solution)/shard_map/psum | solution.py:28
  155.9 0.6 multiply_reduce_fusion
  156.5 0.6 multiply_reduce_fusion.1
  157.8 0.9 maximum_bitcast_fusion
  (94 shorter events, 5.2 us)
Async XLA Ops:
  0.6 4.9 %copy-start.7 = (s32[1,4]{1,0:T(1,128)S(1)}, s32[1,4]{1,0:T(1,128)}, u32[]{:S(2)}) copy-start(s32[1,4]{1,0:T(1,128)} %param.19) | copy-start | bytes 52
  0.6 5.1 %copy-start.5 = (f32[1,4,8]{2,1,0:T(4,128)S(1)}, f32[1,4,8]{2,1,0:T(4,128)}, u32[]{:S(2)}) copy-start(f32[1,4,8]{2,1,0:T(4,128)} %param.21) | copy-start | bytes 388
  0.7 6.1 %copy-start.8 = (s32[16]{0:T(128)S(1)}, s32[16]{0:T(128)}, u32[]{:S(2)}) copy-start(s32[16]{0:T(128)} %param.25) | copy-start | bytes 196
  0.7 6.1 %copy-start.6 = (s32[1,16]{1,0:T(1,128)S(1)}, s32[1,16]{1,0:T(1,128)}, u32[]{:S(2)}) copy-start(s32[1,16]{1,0:T(1,128)} %param.23) | copy-start | bytes 196
  0.7 7.3 %copy-start.4 = (f32[48,16]{0,1:T(8,128)S(1)}, f32[48,16]{0,1:T(8,128)}, u32[]{:S(2)}) copy-start(f32[48,16]{0,1:T(8,128)} %param.27) | copy-start | bytes 9220
  24.3 18.0 %copy-start.3 = (f32[1,48,16,16]{1,3,2,0:T(8,128)S(1)}, f32[1,48,16,16]{1,3,2,0:T(8,128)}, u32[]{:S(2)}) copy-start(f32[1,48,16,16]{1,3,2,0:T(8,128)} %param.24) | copy-start | bytes 147460
  25.6 18.3 %copy-start = (f32[1,4,8,48,16]{3,4,2,1,0:T(8,128)S(1)}, f32[1,4,8,48,16]{3,4,2,1,0:T(8,128)}, u32[]{:S(2)}) copy-start(f32[1,4,8,48,16]{3,4,2,1,0:T(8,128)} %param.22) | copy-start | bytes 294916
  25.8 17.0 %collective-permute-start.3 = (f32[8,384]{1,0:T(8,128)S(1)}, f32[8,384]{1,0:T(8,128)S(1)}, u32[]{:S(2)}, u32[]{:S(2)}) collective-permute-start(f32[8,384]{1,0:T(8,128)S(1)} %squeeze.56), channel_id=1, source_target_pairs={{0,32},{4,36},{8,40},{12,44},{16,48},{20,52},{24,56},{28,60},{32,6... | collective-permute-start | bytes 36872 | tf_op jit(solution)/shard_map/ppermute | solution.py:118
  32.8 10.2 %collective-permute-start.2 = (f32[8,384]{1,0:T(8,128)S(1)}, f32[8,384]{1,0:T(8,128)S(1)}, u32[]{:S(2)}, u32[]{:S(2)}) collective-permute-start(f32[8,384]{1,0:T(8,128)S(1)} %squeeze.55), channel_id=1, source_target_pairs={{0,480},{4,484},{8,488},{12,492},{16,496},{20,500},{24,504},{28,50... | collective-permute-start | bytes 36872 | tf_op jit(solution)/shard_map/ppermute | solution.py:118
  36.7 6.5 %collective-permute-start.1 = (f32[8,384]{1,0:T(8,128)S(1)}, f32[8,384]{1,0:T(8,128)S(1)}, u32[]{:S(2)}, u32[]{:S(2)}) collective-permute-start(f32[8,384]{1,0:T(8,128)S(1)} %squeeze.54), channel_id=1, source_target_pairs={{0,4},{4,8},{8,12},{12,16},{16,20},{20,24},{24,28},{28,32},{32,36}... | collective-permute-start | bytes 36872 | tf_op jit(solution)/shard_map/ppermute | solution.py:118
  38.7 5.0 %collective-permute-start = (f32[8,384]{1,0:T(8,128)S(1)}, f32[8,384]{1,0:T(8,128)S(1)}, u32[]{:S(2)}, u32[]{:S(2)}) collective-permute-start(f32[8,384]{1,0:T(8,128)S(1)} %squeeze.53), channel_id=1, source_target_pairs={{0,508},{4,0},{8,4},{12,8},{16,12},{20,16},{24,20},{28,24},{32,28}... | collective-permute-start | bytes 36872 | tf_op jit(solution)/shard_map/ppermute | solution.py:118
  60.7 18.1 %copy-start.9 = (f32[1,16]{1,0:T(1,128)S(1)}, f32[1,16]{1,0:T(1,128)}, u32[]{:S(2)}) copy-start(f32[1,16]{1,0:T(1,128)} %get-tuple-element.15) | copy-start | bytes 196
  60.7 18.1 %copy-start.10 = (f32[1,16]{1,0:T(1,128)S(1)}, f32[1,16]{1,0:T(1,128)}, u32[]{:S(2)}) copy-start(f32[1,16]{1,0:T(1,128)} %get-tuple-element.20) | copy-start | bytes 196
  60.7 77.0 %copy-start.1 = (f32[384,48]{1,0:T(8,128)S(1)}, f32[384,48]{1,0:T(8,128)}, u32[]{:S(2)}) copy-start(f32[384,48]{1,0:T(8,128)} %get-tuple-element.16) | copy-start | bytes 221188
  60.7 77.0 %copy-start.2 = (f32[384,48]{1,0:T(8,128)S(1)}, f32[384,48]{1,0:T(8,128)}, u32[]{:S(2)}) copy-start(f32[384,48]{1,0:T(8,128)} %get-tuple-element.21) | copy-start | bytes 221188
  62.2 94.8 %collective-permute-start.7 = (f32[8,384]{1,0:T(8,128)S(1)}, f32[8,384]{1,0:T(8,128)S(1)}, u32[]{:S(2)}, u32[]{:S(2)}) collective-permute-start(f32[8,384]{1,0:T(8,128)S(1)} %squeeze.61), channel_id=1, source_target_pairs={{0,32},{4,36},{8,40},{12,44},{16,48},{20,52},{24,56},{28,60},{32,6... | collective-permute-start | bytes 36872 | tf_op jit(solution)/shard_map/ppermute | solution.py:118
  68.3 89.0 %collective-permute-start.6 = (f32[8,384]{1,0:T(8,128)S(1)}, f32[8,384]{1,0:T(8,128)S(1)}, u32[]{:S(2)}, u32[]{:S(2)}) collective-permute-start(f32[8,384]{1,0:T(8,128)S(1)} %squeeze.60), channel_id=1, source_target_pairs={{0,480},{4,484},{8,488},{12,492},{16,496},{20,500},{24,504},{28,50... | collective-permute-start | bytes 36872 | tf_op jit(solution)/shard_map/ppermute | solution.py:118
  73.1 84.4 %collective-permute-start.5 = (f32[8,384]{1,0:T(8,128)S(1)}, f32[8,384]{1,0:T(8,128)S(1)}, u32[]{:S(2)}, u32[]{:S(2)}) collective-permute-start(f32[8,384]{1,0:T(8,128)S(1)} %squeeze.59), channel_id=1, source_target_pairs={{0,4},{4,8},{8,12},{12,16},{16,20},{20,24},{24,28},{28,32},{32,36}... | collective-permute-start | bytes 36872 | tf_op jit(solution)/shard_map/ppermute | solution.py:118
  76.2 81.4 %collective-permute-start.4 = (f32[8,384]{1,0:T(8,128)S(1)}, f32[8,384]{1,0:T(8,128)S(1)}, u32[]{:S(2)}, u32[]{:S(2)}) collective-permute-start(f32[8,384]{1,0:T(8,128)S(1)} %squeeze.58), channel_id=1, source_target_pairs={{0,508},{4,0},{8,4},{12,8},{16,12},{20,16},{24,20},{28,24},{32,28}... | collective-permute-start | bytes 36872 | tf_op jit(solution)/shard_map/ppermute | solution.py:118

commit v10 on v9

--- a/solution.py
+++ b/solution.py
@@ -67,7 +67,7 @@
         adjoint_ref[rows] = adjoint
         return adjoint
 
-    last_ref[...] = lax.fori_loop(0, steps, one_step, start_ref[...])
+    last_ref[...] = lax.fori_loop(0, steps, one_step, start_ref[...], unroll=True)
     adjoint_block = adjoint_ref[...]
     samples_ref[...] = jnp.dot(
         adjoint_block, pick_ref[...], precision=PRECISE, preferred_element_type=jnp.float32

time: 159 us -> 159 us (level)
  no operation moved by 1% of the time
where the time goes in v10:
time: 159 us; the launch traced here: 158 us
  blocking collectives  76.7 us (48%)
  starting transfers between devices  32.6 us (21%)
  Pallas kernels  29.1 us (18%)
  local copies, waits for them, and re-layouts  10.5 us (7%)
  other arithmetic  5.48 us (3%)
  matrix products  2 us (1%)
    psum x3, blocking collectives, sum_both(): fault_value = lax.psum(fault_value, axis)  58.9 us
    ppermute x8, starting transfers between devices, passed_along(): return lax.ppermute(value, axis, pairs)  32.6 us
    pallas_call x2, Pallas kernels, block_scan(): pl.pallas_call(functools.partial(block_scan_kernel, block_start), grid=(1...  29.1 us
    psum x1, blocking collectives, sum_both(): lax.psum((fault_mask * fault_value[None], control_mask * control_value[No...  17.8 us
  transfers between devices with their start and end apart: 8, of which 1 were waited for; matrix products, arithmetic and copies ran while one was open for 2% of the time, Pallas kernels for 0%

profile of v10, /device:TPU:10, one launch (start us, length us, event | category | flops | bytes accessed | tf_op | source)
XLA Modules:
  0.0 158.0 jit_solution(3041000451377564556)
XLA Ops:
  0.7 0.8 eq.125
  1.8 0.8 fusion.20
  3.0 0.8 add_add_fusion
  3.7 1.4 convolution_bitcast_fusion.1
  5.9 0.8 copy.109.picked_ref
  6.9 0.3 copy.108
  7.2 0.8 convert_element_type.38.pick_ref
  8.0 0.7 copy.110.voltage_ref
  8.7 0.7 add_convert_fusion.spread_ref
  9.4 14.5 %shard_map.165 = (f32[16,1024]{1,0:T(8,128)}, f32[384,48]{1,0:T(8,128)}, f32[1,16]{1,0:T(1,128)}) custom-call(bf16[48,1,16,1024]{3,2,1,0:T(8,128)(2,1)} %grad_ref.3, f32[384,48]{1,0:T(8,128)} %copy.109.picked_ref, f32[48,1024]{1,0:T(8,128)} %add_convert_fusion.spread_ref, f32[1,1024]{1,0:T(1,128)} %companion_ref.3, f32[16,1024]{1,0:T(8,128)} %bitcast.68, ...), custom_call_target="tpu_custom_call" | custom-call | tf_op jit(solution)/shard_map/pallas_call | solution.py:89
  23.9 1.1 copy.111
  25.4 6.8 %collective-permute-start.3 = (f32[8,384]{1,0:T(8,128)S(1)}, f32[8,384]{1,0:T(8,128)S(1)}, u32[]{:S(2)}, u32[]{:S(2)}) collective-permute-start(f32[8,384]{1,0:T(8,128)S(1)} %squeeze.56), channel_id=1, source_target_pairs={{0,32},{4,36},{8,40},{12,44},{16,48},{20,52},{24,56},{28,60},{32,6... | collective-permute-start | bytes 36872 | tf_op jit(solution)/shard_map/ppermute | solution.py:118
  32.4 4.0 %collective-permute-start.2 = (f32[8,384]{1,0:T(8,128)S(1)}, f32[8,384]{1,0:T(8,128)S(1)}, u32[]{:S(2)}, u32[]{:S(2)}) collective-permute-start(f32[8,384]{1,0:T(8,128)S(1)} %squeeze.55), channel_id=1, source_target_pairs={{0,480},{4,484},{8,488},{12,492},{16,496},{20,500},{24,504},{28,50... | collective-permute-start | bytes 36872 | tf_op jit(solution)/shard_map/ppermute | solution.py:118
  36.5 1.9 %collective-permute-start.1 = (f32[8,384]{1,0:T(8,128)S(1)}, f32[8,384]{1,0:T(8,128)S(1)}, u32[]{:S(2)}, u32[]{:S(2)}) collective-permute-start(f32[8,384]{1,0:T(8,128)S(1)} %squeeze.54), channel_id=1, source_target_pairs={{0,4},{4,8},{8,12},{12,16},{16,20},{20,24},{24,28},{28,32},{32,36}... | collective-permute-start | bytes 36872 | tf_op jit(solution)/shard_map/ppermute | solution.py:118
  38.5 3.6 %collective-permute-start = (f32[8,384]{1,0:T(8,128)S(1)}, f32[8,384]{1,0:T(8,128)S(1)}, u32[]{:S(2)}, u32[]{:S(2)}) collective-permute-start(f32[8,384]{1,0:T(8,128)S(1)} %squeeze.53), channel_id=1, source_target_pairs={{0,508},{4,0},{8,4},{12,8},{16,12},{20,16},{24,20},{28,24},{32,28}... | collective-permute-start | bytes 36872 | tf_op jit(solution)/shard_map/ppermute | solution.py:118
  43.1 0.4 collective-permute-done
  43.7 0.6 convolution_bitcast_fusion
  44.3 0.2 copy.116
  44.7 0.8 copy.118.picked_ref
  45.5 14.5 %shard_map.166 = (f32[16,1024]{1,0:T(8,128)}, f32[384,48]{1,0:T(8,128)}, f32[1,16]{1,0:T(1,128)}) custom-call(bf16[48,1,16,1024]{3,2,1,0:T(8,128)(2,1)} %grad_ref.3, f32[384,48]{1,0:T(8,128)} %copy.118.picked_ref, f32[48,1024]{1,0:T(8,128)} %add_convert_fusion.spread_ref, f32[1,1024]{1,0:T(1,128)} %companion_ref.3, f32[16,1024]{1,0:T(8,128)} %get-tuple-element.17.start_ref, ...), custom_call_target="tpu_custom_call" | custom-call | tf_op jit(solution)/shard_map/pallas_call | solution.py:89
  60.1 1.1 copy.120
  61.6 5.9 %collective-permute-start.7 = (f32[8,384]{1,0:T(8,128)S(1)}, f32[8,384]{1,0:T(8,128)S(1)}, u32[]{:S(2)}, u32[]{:S(2)}) collective-permute-start(f32[8,384]{1,0:T(8,128)S(1)} %squeeze.61), channel_id=1, source_target_pairs={{0,32},{4,36},{8,40},{12,44},{16,48},{20,52},{24,56},{28,60},{32,6... | collective-permute-start | bytes 36872 | tf_op jit(solution)/shard_map/ppermute | solution.py:118
  67.6 4.7 %collective-permute-start.6 = (f32[8,384]{1,0:T(8,128)S(1)}, f32[8,384]{1,0:T(8,128)S(1)}, u32[]{:S(2)}, u32[]{:S(2)}) collective-permute-start(f32[8,384]{1,0:T(8,128)S(1)} %squeeze.60), channel_id=1, source_target_pairs={{0,480},{4,484},{8,488},{12,492},{16,496},{20,500},{24,504},{28,50... | collective-permute-start | bytes 36872 | tf_op jit(solution)/shard_map/ppermute | solution.py:118
  72.5 3.0 %collective-permute-start.5 = (f32[8,384]{1,0:T(8,128)S(1)}, f32[8,384]{1,0:T(8,128)S(1)}, u32[]{:S(2)}, u32[]{:S(2)}) collective-permute-start(f32[8,384]{1,0:T(8,128)S(1)} %squeeze.59), channel_id=1, source_target_pairs={{0,4},{4,8},{8,12},{12,16},{16,20},{20,24},{24,28},{28,32},{32,36}... | collective-permute-start | bytes 36872 | tf_op jit(solution)/shard_map/ppermute | solution.py:118
  75.6 2.6 %collective-permute-start.4 = (f32[8,384]{1,0:T(8,128)S(1)}, f32[8,384]{1,0:T(8,128)S(1)}, u32[]{:S(2)}, u32[]{:S(2)}) collective-permute-start(f32[8,384]{1,0:T(8,128)S(1)} %squeeze.58), channel_id=1, source_target_pairs={{0,508},{4,0},{8,4},{12,8},{16,12},{20,16},{24,20},{28,24},{32,28}... | collective-permute-start | bytes 36872 | tf_op jit(solution)/shard_map/ppermute | solution.py:118
  78.2 2.5 %psum.36 = f32[16]{0:T(128)S(1)} all-reduce(f32[16]{0:T(128)S(1)} %add.68), channel_id=1, replica_groups=mesh['z_hi'=2,'x'=4,'y'=8,'core'=2,'scen'=4] {'core'}, use_global_device_ids=true, to_apply=%region_4.0 | all-reduce | flops 16 | bytes 128 | tf_op jit(solution)/shard_map/psum | solution.py:21
  80.6 20.5 %psum.37 = f32[16]{0:T(128)S(1)} all-reduce(f32[16]{0:T(128)S(1)} %psum.36), channel_id=1, replica_groups=mesh['z_hi'=2,'x'=4,'y'=8,'core'=2,'scen'=4] {'y'}, use_global_device_ids=true, to_apply=%region_5.0 | all-reduce | flops 16 | bytes 128 | tf_op jit(solution)/shard_map/psum | solution.py:21
  101.1 36.0 %psum.38 = f32[16]{0:T(128)S(1)} all-reduce(f32[16]{0:T(128)S(1)} %psum.37), channel_id=1, replica_groups=mesh['z_hi'=2,'x'=4,'y'=8,'core'=2,'scen'=4] {'x'}, use_global_device_ids=true, to_apply=%region_6.0 | all-reduce | flops 16 | bytes 128 | tf_op jit(solution)/shard_map/psum | solution.py:21
  137.4 17.8 %all-reduce = (f32[2,16]{1,0:T(2,128)S(1)}, f32[4,16]{1,0:T(4,128)S(1)}) all-reduce(f32[2,16]{1,0:T(2,128)S(1)} %broadcast_multiply_fusion.5, f32[4,16]{1,0:T(4,128)S(1)} %broadcast_multiply_fusion.4), channel_id=1, replica_groups=mesh['z_hi'=2,'x'=4,'y'=8,'core'=2,'scen'=4] {'z_hi','scen'}, use_global_device_ids=true, to_apply=%region_2.0 | all-reduce | flops 96 | bytes 768 | tf_op jit(solution)/shard_map/psum | solution.py:28
  155.2 0.6 multiply_reduce_fusion
  155.8 0.6 multiply_reduce_fusion.1
  157.2 0.9 maximum_bitcast_fusion
  (94 shorter events, 5.2 us)
Async XLA Ops:
  0.6 4.9 %copy-start.7 = (s32[1,4]{1,0:T(1,128)S(1)}, s32[1,4]{1,0:T(1,128)}, u32[]{:S(2)}) copy-start(s32[1,4]{1,0:T(1,128)} %param.19) | copy-start | bytes 52
  0.6 5.1 %copy-start.5 = (f32[1,4,8]{2,1,0:T(4,128)S(1)}, f32[1,4,8]{2,1,0:T(4,128)}, u32[]{:S(2)}) copy-start(f32[1,4,8]{2,1,0:T(4,128)} %param.21) | copy-start | bytes 388
  0.7 6.1 %copy-start.8 = (s32[16]{0:T(128)S(1)}, s32[16]{0:T(128)}, u32[]{:S(2)}) copy-start(s32[16]{0:T(128)} %param.25) | copy-start | bytes 196
  0.7 6.1 %copy-start.6 = (s32[1,16]{1,0:T(1,128)S(1)}, s32[1,16]{1,0:T(1,128)}, u32[]{:S(2)}) copy-start(s32[1,16]{1,0:T(1,128)} %param.23) | copy-start | bytes 196
  0.7 7.3 %copy-start.4 = (f32[48,16]{0,1:T(8,128)S(1)}, f32[48,16]{0,1:T(8,128)}, u32[]{:S(2)}) copy-start(f32[48,16]{0,1:T(8,128)} %param.27) | copy-start | bytes 9220
  23.9 18.2 %copy-start.3 = (f32[1,48,16,16]{1,3,2,0:T(8,128)S(1)}, f32[1,48,16,16]{1,3,2,0:T(8,128)}, u32[]{:S(2)}) copy-start(f32[1,48,16,16]{1,3,2,0:T(8,128)} %param.24) | copy-start | bytes 147460
  25.2 18.5 %copy-start = (f32[1,4,8,48,16]{3,4,2,1,0:T(8,128)S(1)}, f32[1,4,8,48,16]{3,4,2,1,0:T(8,128)}, u32[]{:S(2)}) copy-start(f32[1,4,8,48,16]{3,4,2,1,0:T(8,128)} %param.22) | copy-start | bytes 294916
  25.4 17.1 %collective-permute-start.3 = (f32[8,384]{1,0:T(8,128)S(1)}, f32[8,384]{1,0:T(8,128)S(1)}, u32[]{:S(2)}, u32[]{:S(2)}) collective-permute-start(f32[8,384]{1,0:T(8,128)S(1)} %squeeze.56), channel_id=1, source_target_pairs={{0,32},{4,36},{8,40},{12,44},{16,48},{20,52},{24,56},{28,60},{32,6... | collective-permute-start | bytes 36872 | tf_op jit(solution)/shard_map/ppermute | solution.py:118
  32.4 10.4 %collective-permute-start.2 = (f32[8,384]{1,0:T(8,128)S(1)}, f32[8,384]{1,0:T(8,128)S(1)}, u32[]{:S(2)}, u32[]{:S(2)}) collective-permute-start(f32[8,384]{1,0:T(8,128)S(1)} %squeeze.55), channel_id=1, source_target_pairs={{0,480},{4,484},{8,488},{12,492},{16,496},{20,500},{24,504},{28,50... | collective-permute-start | bytes 36872 | tf_op jit(solution)/shard_map/ppermute | solution.py:118
  36.5 6.5 %collective-permute-start.1 = (f32[8,384]{1,0:T(8,128)S(1)}, f32[8,384]{1,0:T(8,128)S(1)}, u32[]{:S(2)}, u32[]{:S(2)}) collective-permute-start(f32[8,384]{1,0:T(8,128)S(1)} %squeeze.54), channel_id=1, source_target_pairs={{0,4},{4,8},{8,12},{12,16},{16,20},{20,24},{24,28},{28,32},{32,36}... | collective-permute-start | bytes 36872 | tf_op jit(solution)/shard_map/ppermute | solution.py:118
  38.5 5.0 %collective-permute-start = (f32[8,384]{1,0:T(8,128)S(1)}, f32[8,384]{1,0:T(8,128)S(1)}, u32[]{:S(2)}, u32[]{:S(2)}) collective-permute-start(f32[8,384]{1,0:T(8,128)S(1)} %squeeze.53), channel_id=1, source_target_pairs={{0,508},{4,0},{8,4},{12,8},{16,12},{20,16},{24,20},{28,24},{32,28}... | collective-permute-start | bytes 36872 | tf_op jit(solution)/shard_map/ppermute | solution.py:118
  60.1 18.1 %copy-start.9 = (f32[1,16]{1,0:T(1,128)S(1)}, f32[1,16]{1,0:T(1,128)}, u32[]{:S(2)}) copy-start(f32[1,16]{1,0:T(1,128)} %get-tuple-element.15) | copy-start | bytes 196
  60.1 18.1 %copy-start.10 = (f32[1,16]{1,0:T(1,128)S(1)}, f32[1,16]{1,0:T(1,128)}, u32[]{:S(2)}) copy-start(f32[1,16]{1,0:T(1,128)} %get-tuple-element.20) | copy-start | bytes 196
  60.1 77.0 %copy-start.1 = (f32[384,48]{1,0:T(8,128)S(1)}, f32[384,48]{1,0:T(8,128)}, u32[]{:S(2)}) copy-start(f32[384,48]{1,0:T(8,128)} %get-tuple-element.16) | copy-start | bytes 221188
  60.1 77.0 %copy-start.2 = (f32[384,48]{1,0:T(8,128)S(1)}, f32[384,48]{1,0:T(8,128)}, u32[]{:S(2)}) copy-start(f32[384,48]{1,0:T(8,128)} %get-tuple-element.21) | copy-start | bytes 221188
  61.6 94.8 %collective-permute-start.7 = (f32[8,384]{1,0:T(8,128)S(1)}, f32[8,384]{1,0:T(8,128)S(1)}, u32[]{:S(2)}, u32[]{:S(2)}) collective-permute-start(f32[8,384]{1,0:T(8,128)S(1)} %squeeze.61), channel_id=1, source_target_pairs={{0,32},{4,36},{8,40},{12,44},{16,48},{20,52},{24,56},{28,60},{32,6... | collective-permute-start | bytes 36872 | tf_op jit(solution)/shard_map/ppermute | solution.py:118
  67.6 89.0 %collective-permute-start.6 = (f32[8,384]{1,0:T(8,128)S(1)}, f32[8,384]{1,0:T(8,128)S(1)}, u32[]{:S(2)}, u32[]{:S(2)}) collective-permute-start(f32[8,384]{1,0:T(8,128)S(1)} %squeeze.60), channel_id=1, source_target_pairs={{0,480},{4,484},{8,488},{12,492},{16,496},{20,500},{24,504},{28,50... | collective-permute-start | bytes 36872 | tf_op jit(solution)/shard_map/ppermute | solution.py:118
  72.5 84.3 %collective-permute-start.5 = (f32[8,384]{1,0:T(8,128)S(1)}, f32[8,384]{1,0:T(8,128)S(1)}, u32[]{:S(2)}, u32[]{:S(2)}) collective-permute-start(f32[8,384]{1,0:T(8,128)S(1)} %squeeze.59), channel_id=1, source_target_pairs={{0,4},{4,8},{8,12},{12,16},{16,20},{20,24},{24,28},{28,32},{32,36}... | collective-permute-start | bytes 36872 | tf_op jit(solution)/shard_map/ppermute | solution.py:118
  75.6 81.4 %collective-permute-start.4 = (f32[8,384]{1,0:T(8,128)S(1)}, f32[8,384]{1,0:T(8,128)S(1)}, u32[]{:S(2)}, u32[]{:S(2)}) collective-permute-start(f32[8,384]{1,0:T(8,128)S(1)} %squeeze.58), channel_id=1, source_target_pairs={{0,508},{4,0},{8,4},{12,8},{16,12},{20,16},{24,20},{28,24},{32,28}... | collective-permute-start | bytes 36872 | tf_op jit(solution)/shard_map/ppermute | solution.py:118

commit v11 on v10

--- a/solution.py
+++ b/solution.py
@@ -50,7 +50,7 @@
     steps, scen_rows, node_count = grad_ref.shape
     companion = companion_ref[...]
     inflow_ref[...] = jnp.dot(
-        picked_ref[...], spread_ref[...], precision=PRECISE, preferred_element_type=jnp.float32
+        picked_ref[...], spread_ref[...], precision=lax.Precision.HIGH, preferred_element_type=jnp.float32
     )
 
     def one_step(index, adjoint_prev):
@@ -70,7 +70,7 @@
     last_ref[...] = lax.fori_loop(0, steps, one_step, start_ref[...], unroll=True)
     adjoint_block = adjoint_ref[...]
     samples_ref[...] = jnp.dot(
-        adjoint_block, pick_ref[...], precision=PRECISE, preferred_element_type=jnp.float32
+        adjoint_block, pick_ref[...], precision=lax.Precision.HIGH, preferred_element_type=jnp.float32
     )
     fault_table = spread_ref[pl.ds(spread_ref.shape[0] - scen_rows, scen_rows), :]
     at_fault = jnp.sum(adjoint_block.reshape(steps, scen_rows, node_count) * fault_table[None], axis=2)

time: 159 us -> 154 us (0.969)
  Pallas kernels: 29.1 us -> 24.2 us
    pallas_call x2, Pallas kernels: 29.1 us -> 24.2 us  [block_scan(): pl.pallas_call(functools.partial(block_scan_kernel, block_start), grid=(1...]
where the time goes in v11:
time: 154 us; the launch traced here: 153 us
  blocking collectives  76.7 us (50%)
  starting transfers between devices  32.6 us (21%)
  Pallas kernels  24.2 us (16%)
  local copies, waits for them, and re-layouts  10.5 us (7%)
  other arithmetic  5.48 us (4%)
  matrix products  2 us (1%)
    psum x3, blocking collectives, sum_both(): fault_value = lax.psum(fault_value, axis)  58.9 us
    ppermute x8, starting transfers between devices, passed_along(): return lax.ppermute(value, axis, pairs)  32.6 us
    pallas_call x2, Pallas kernels, block_scan(): pl.pallas_call(functools.partial(block_scan_kernel, block_start), grid=(1...  24.2 us
    psum x1, blocking collectives, sum_both(): lax.psum((fault_mask * fault_value[None], control_mask * control_value[No...  17.8 us
  transfers between devices with their start and end apart: 8, of which 1 were waited for; matrix products, arithmetic and copies ran while one was open for 2% of the time, Pallas kernels for 0%

profile of v11, /device:TPU:10, one launch (start us, length us, event | category | flops | bytes accessed | tf_op | source)
XLA Modules:
  0.0 153.0 jit_solution(3165043066551758684)
XLA Ops:
  0.7 0.8 eq.125
  1.8 0.8 fusion.20
  3.0 0.8 add_add_fusion
  3.7 1.4 convolution_bitcast_fusion.1
  5.9 0.8 copy.109.picked_ref
  6.9 0.3 copy.108
  7.2 0.8 convert_element_type.38.pick_ref
  8.0 0.7 copy.110.voltage_ref
  8.7 0.7 add_convert_fusion.spread_ref
  9.4 12.1 %shard_map.165 = (f32[16,1024]{1,0:T(8,128)}, f32[384,48]{1,0:T(8,128)}, f32[1,16]{1,0:T(1,128)}) custom-call(bf16[48,1,16,1024]{3,2,1,0:T(8,128)(2,1)} %grad_ref.3, f32[384,48]{1,0:T(8,128)} %copy.109.picked_ref, f32[48,1024]{1,0:T(8,128)} %add_convert_fusion.spread_ref, f32[1,1024]{1,0:T(1,128)} %companion_ref.3, f32[16,1024]{1,0:T(8,128)} %bitcast.68, ...), custom_call_target="tpu_custom_call" | custom-call | tf_op jit(solution)/shard_map/pallas_call | solution.py:89
  21.5 1.1 copy.111
  23.0 6.8 %collective-permute-start.3 = (f32[8,384]{1,0:T(8,128)S(1)}, f32[8,384]{1,0:T(8,128)S(1)}, u32[]{:S(2)}, u32[]{:S(2)}) collective-permute-start(f32[8,384]{1,0:T(8,128)S(1)} %squeeze.56), channel_id=1, source_target_pairs={{0,32},{4,36},{8,40},{12,44},{16,48},{20,52},{24,56},{28,60},{32,6... | collective-permute-start | bytes 36872 | tf_op jit(solution)/shard_map/ppermute | solution.py:118
  29.9 3.8 %collective-permute-start.2 = (f32[8,384]{1,0:T(8,128)S(1)}, f32[8,384]{1,0:T(8,128)S(1)}, u32[]{:S(2)}, u32[]{:S(2)}) collective-permute-start(f32[8,384]{1,0:T(8,128)S(1)} %squeeze.55), channel_id=1, source_target_pairs={{0,480},{4,484},{8,488},{12,492},{16,496},{20,500},{24,504},{28,50... | collective-permute-start | bytes 36872 | tf_op jit(solution)/shard_map/ppermute | solution.py:118
  33.9 1.9 %collective-permute-start.1 = (f32[8,384]{1,0:T(8,128)S(1)}, f32[8,384]{1,0:T(8,128)S(1)}, u32[]{:S(2)}, u32[]{:S(2)}) collective-permute-start(f32[8,384]{1,0:T(8,128)S(1)} %squeeze.54), channel_id=1, source_target_pairs={{0,4},{4,8},{8,12},{12,16},{16,20},{20,24},{24,28},{28,32},{32,36}... | collective-permute-start | bytes 36872 | tf_op jit(solution)/shard_map/ppermute | solution.py:118
  35.9 3.8 %collective-permute-start = (f32[8,384]{1,0:T(8,128)S(1)}, f32[8,384]{1,0:T(8,128)S(1)}, u32[]{:S(2)}, u32[]{:S(2)}) collective-permute-start(f32[8,384]{1,0:T(8,128)S(1)} %squeeze.53), channel_id=1, source_target_pairs={{0,508},{4,0},{8,4},{12,8},{16,12},{20,16},{24,20},{28,24},{32,28}... | collective-permute-start | bytes 36872 | tf_op jit(solution)/shard_map/ppermute | solution.py:118
  40.7 0.2 collective-permute-done
  41.1 0.6 convolution_bitcast_fusion
  41.7 0.2 copy.116
  42.1 0.8 copy.118.picked_ref
  42.9 12.1 %shard_map.166 = (f32[16,1024]{1,0:T(8,128)}, f32[384,48]{1,0:T(8,128)}, f32[1,16]{1,0:T(1,128)}) custom-call(bf16[48,1,16,1024]{3,2,1,0:T(8,128)(2,1)} %grad_ref.3, f32[384,48]{1,0:T(8,128)} %copy.118.picked_ref, f32[48,1024]{1,0:T(8,128)} %add_convert_fusion.spread_ref, f32[1,1024]{1,0:T(1,128)} %companion_ref.3, f32[16,1024]{1,0:T(8,128)} %get-tuple-element.17.start_ref, ...), custom_call_target="tpu_custom_call" | custom-call | tf_op jit(solution)/shard_map/pallas_call | solution.py:89
  55.0 1.1 copy.120
  56.6 5.9 %collective-permute-start.7 = (f32[8,384]{1,0:T(8,128)S(1)}, f32[8,384]{1,0:T(8,128)S(1)}, u32[]{:S(2)}, u32[]{:S(2)}) collective-permute-start(f32[8,384]{1,0:T(8,128)S(1)} %squeeze.61), channel_id=1, source_target_pairs={{0,32},{4,36},{8,40},{12,44},{16,48},{20,52},{24,56},{28,60},{32,6... | collective-permute-start | bytes 36872 | tf_op jit(solution)/shard_map/ppermute | solution.py:118
  62.6 4.7 %collective-permute-start.6 = (f32[8,384]{1,0:T(8,128)S(1)}, f32[8,384]{1,0:T(8,128)S(1)}, u32[]{:S(2)}, u32[]{:S(2)}) collective-permute-start(f32[8,384]{1,0:T(8,128)S(1)} %squeeze.60), channel_id=1, source_target_pairs={{0,480},{4,484},{8,488},{12,492},{16,496},{20,500},{24,504},{28,50... | collective-permute-start | bytes 36872 | tf_op jit(solution)/shard_map/ppermute | solution.py:118
  67.4 3.0 %collective-permute-start.5 = (f32[8,384]{1,0:T(8,128)S(1)}, f32[8,384]{1,0:T(8,128)S(1)}, u32[]{:S(2)}, u32[]{:S(2)}) collective-permute-start(f32[8,384]{1,0:T(8,128)S(1)} %squeeze.59), channel_id=1, source_target_pairs={{0,4},{4,8},{8,12},{12,16},{16,20},{20,24},{24,28},{28,32},{32,36}... | collective-permute-start | bytes 36872 | tf_op jit(solution)/shard_map/ppermute | solution.py:118
  70.5 2.6 %collective-permute-start.4 = (f32[8,384]{1,0:T(8,128)S(1)}, f32[8,384]{1,0:T(8,128)S(1)}, u32[]{:S(2)}, u32[]{:S(2)}) collective-permute-start(f32[8,384]{1,0:T(8,128)S(1)} %squeeze.58), channel_id=1, source_target_pairs={{0,508},{4,0},{8,4},{12,8},{16,12},{20,16},{24,20},{28,24},{32,28}... | collective-permute-start | bytes 36872 | tf_op jit(solution)/shard_map/ppermute | solution.py:118
  73.1 2.5 %psum.36 = f32[16]{0:T(128)S(1)} all-reduce(f32[16]{0:T(128)S(1)} %add.68), channel_id=1, replica_groups=mesh['z_hi'=2,'x'=4,'y'=8,'core'=2,'scen'=4] {'core'}, use_global_device_ids=true, to_apply=%region_4.0 | all-reduce | flops 16 | bytes 128 | tf_op jit(solution)/shard_map/psum | solution.py:21
  75.6 20.5 %psum.37 = f32[16]{0:T(128)S(1)} all-reduce(f32[16]{0:T(128)S(1)} %psum.36), channel_id=1, replica_groups=mesh['z_hi'=2,'x'=4,'y'=8,'core'=2,'scen'=4] {'y'}, use_global_device_ids=true, to_apply=%region_5.0 | all-reduce | flops 16 | bytes 128 | tf_op jit(solution)/shard_map/psum | solution.py:21
  96.1 36.0 %psum.38 = f32[16]{0:T(128)S(1)} all-reduce(f32[16]{0:T(128)S(1)} %psum.37), channel_id=1, replica_groups=mesh['z_hi'=2,'x'=4,'y'=8,'core'=2,'scen'=4] {'x'}, use_global_device_ids=true, to_apply=%region_6.0 | all-reduce | flops 16 | bytes 128 | tf_op jit(solution)/shard_map/psum | solution.py:21
  132.4 17.8 %all-reduce = (f32[2,16]{1,0:T(2,128)S(1)}, f32[4,16]{1,0:T(4,128)S(1)}) all-reduce(f32[2,16]{1,0:T(2,128)S(1)} %broadcast_multiply_fusion.5, f32[4,16]{1,0:T(4,128)S(1)} %broadcast_multiply_fusion.4), channel_id=1, replica_groups=mesh['z_hi'=2,'x'=4,'y'=8,'core'=2,'scen'=4] {'z_hi','scen'}, use_global_device_ids=true, to_apply=%region_2.0 | all-reduce | flops 96 | bytes 768 | tf_op jit(solution)/shard_map/psum | solution.py:28
  150.2 0.6 multiply_reduce_fusion
  150.8 0.6 multiply_reduce_fusion.1
  152.1 0.9 maximum_bitcast_fusion
  (94 shorter events, 5.2 us)
Async XLA Ops:
  0.6 4.9 %copy-start.7 = (s32[1,4]{1,0:T(1,128)S(1)}, s32[1,4]{1,0:T(1,128)}, u32[]{:S(2)}) copy-start(s32[1,4]{1,0:T(1,128)} %param.19) | copy-start | bytes 52
  0.6 5.1 %copy-start.5 = (f32[1,4,8]{2,1,0:T(4,128)S(1)}, f32[1,4,8]{2,1,0:T(4,128)}, u32[]{:S(2)}) copy-start(f32[1,4,8]{2,1,0:T(4,128)} %param.21) | copy-start | bytes 388
  0.7 6.1 %copy-start.8 = (s32[16]{0:T(128)S(1)}, s32[16]{0:T(128)}, u32[]{:S(2)}) copy-start(s32[16]{0:T(128)} %param.25) | copy-start | bytes 196
  0.7 6.1 %copy-start.6 = (s32[1,16]{1,0:T(1,128)S(1)}, s32[1,16]{1,0:T(1,128)}, u32[]{:S(2)}) copy-start(s32[1,16]{1,0:T(1,128)} %param.23) | copy-start | bytes 196
  0.7 7.3 %copy-start.4 = (f32[48,16]{0,1:T(8,128)S(1)}, f32[48,16]{0,1:T(8,128)}, u32[]{:S(2)}) copy-start(f32[48,16]{0,1:T(8,128)} %param.27) | copy-start | bytes 9220
  21.5 18.2 %copy-start.3 = (f32[1,48,16,16]{1,3,2,0:T(8,128)S(1)}, f32[1,48,16,16]{1,3,2,0:T(8,128)}, u32[]{:S(2)}) copy-start(f32[1,48,16,16]{1,3,2,0:T(8,128)} %param.24) | copy-start | bytes 147460
  22.7 18.3 %copy-start = (f32[1,4,8,48,16]{3,4,2,1,0:T(8,128)S(1)}, f32[1,4,8,48,16]{3,4,2,1,0:T(8,128)}, u32[]{:S(2)}) copy-start(f32[1,4,8,48,16]{3,4,2,1,0:T(8,128)} %param.22) | copy-start | bytes 294916
  23.0 17.1 %collective-permute-start.3 = (f32[8,384]{1,0:T(8,128)S(1)}, f32[8,384]{1,0:T(8,128)S(1)}, u32[]{:S(2)}, u32[]{:S(2)}) collective-permute-start(f32[8,384]{1,0:T(8,128)S(1)} %squeeze.56), channel_id=1, source_target_pairs={{0,32},{4,36},{8,40},{12,44},{16,48},{20,52},{24,56},{28,60},{32,6... | collective-permute-start | bytes 36872 | tf_op jit(solution)/shard_map/ppermute | solution.py:118
  29.9 10.4 %collective-permute-start.2 = (f32[8,384]{1,0:T(8,128)S(1)}, f32[8,384]{1,0:T(8,128)S(1)}, u32[]{:S(2)}, u32[]{:S(2)}) collective-permute-start(f32[8,384]{1,0:T(8,128)S(1)} %squeeze.55), channel_id=1, source_target_pairs={{0,480},{4,484},{8,488},{12,492},{16,496},{20,500},{24,504},{28,50... | collective-permute-start | bytes 36872 | tf_op jit(solution)/shard_map/ppermute | solution.py:118
  33.9 6.7 %collective-permute-start.1 = (f32[8,384]{1,0:T(8,128)S(1)}, f32[8,384]{1,0:T(8,128)S(1)}, u32[]{:S(2)}, u32[]{:S(2)}) collective-permute-start(f32[8,384]{1,0:T(8,128)S(1)} %squeeze.54), channel_id=1, source_target_pairs={{0,4},{4,8},{8,12},{12,16},{16,20},{20,24},{24,28},{28,32},{32,36}... | collective-permute-start | bytes 36872 | tf_op jit(solution)/shard_map/ppermute | solution.py:118
  35.9 5.0 %collective-permute-start = (f32[8,384]{1,0:T(8,128)S(1)}, f32[8,384]{1,0:T(8,128)S(1)}, u32[]{:S(2)}, u32[]{:S(2)}) collective-permute-start(f32[8,384]{1,0:T(8,128)S(1)} %squeeze.53), channel_id=1, source_target_pairs={{0,508},{4,0},{8,4},{12,8},{16,12},{20,16},{24,20},{28,24},{32,28}... | collective-permute-start | bytes 36872 | tf_op jit(solution)/shard_map/ppermute | solution.py:118
  55.0 18.1 %copy-start.9 = (f32[1,16]{1,0:T(1,128)S(1)}, f32[1,16]{1,0:T(1,128)}, u32[]{:S(2)}) copy-start(f32[1,16]{1,0:T(1,128)} %get-tuple-element.15) | copy-start | bytes 196
  55.0 18.1 %copy-start.10 = (f32[1,16]{1,0:T(1,128)S(1)}, f32[1,16]{1,0:T(1,128)}, u32[]{:S(2)}) copy-start(f32[1,16]{1,0:T(1,128)} %get-tuple-element.20) | copy-start | bytes 196
  55.0 77.0 %copy-start.1 = (f32[384,48]{1,0:T(8,128)S(1)}, f32[384,48]{1,0:T(8,128)}, u32[]{:S(2)}) copy-start(f32[384,48]{1,0:T(8,128)} %get-tuple-element.16) | copy-start | bytes 221188
  55.0 77.0 %copy-start.2 = (f32[384,48]{1,0:T(8,128)S(1)}, f32[384,48]{1,0:T(8,128)}, u32[]{:S(2)}) copy-start(f32[384,48]{1,0:T(8,128)} %get-tuple-element.21) | copy-start | bytes 221188
  56.6 94.8 %collective-permute-start.7 = (f32[8,384]{1,0:T(8,128)S(1)}, f32[8,384]{1,0:T(8,128)S(1)}, u32[]{:S(2)}, u32[]{:S(2)}) collective-permute-start(f32[8,384]{1,0:T(8,128)S(1)} %squeeze.61), channel_id=1, source_target_pairs={{0,32},{4,36},{8,40},{12,44},{16,48},{20,52},{24,56},{28,60},{32,6... | collective-permute-start | bytes 36872 | tf_op jit(solution)/shard_map/ppermute | solution.py:118
  62.6 89.0 %collective-permute-start.6 = (f32[8,384]{1,0:T(8,128)S(1)}, f32[8,384]{1,0:T(8,128)S(1)}, u32[]{:S(2)}, u32[]{:S(2)}) collective-permute-start(f32[8,384]{1,0:T(8,128)S(1)} %squeeze.60), channel_id=1, source_target_pairs={{0,480},{4,484},{8,488},{12,492},{16,496},{20,500},{24,504},{28,50... | collective-permute-start | bytes 36872 | tf_op jit(solution)/shard_map/ppermute | solution.py:118
  67.4 84.3 %collective-permute-start.5 = (f32[8,384]{1,0:T(8,128)S(1)}, f32[8,384]{1,0:T(8,128)S(1)}, u32[]{:S(2)}, u32[]{:S(2)}) collective-permute-start(f32[8,384]{1,0:T(8,128)S(1)} %squeeze.59), channel_id=1, source_target_pairs={{0,4},{4,8},{8,12},{12,16},{16,20},{20,24},{24,28},{28,32},{32,36}... | collective-permute-start | bytes 36872 | tf_op jit(solution)/shard_map/ppermute | solution.py:118
  70.5 81.4 %collective-permute-start.4 = (f32[8,384]{1,0:T(8,128)S(1)}, f32[8,384]{1,0:T(8,128)S(1)}, u32[]{:S(2)}, u32[]{:S(2)}) collective-permute-start(f32[8,384]{1,0:T(8,128)S(1)} %squeeze.58), channel_id=1, source_target_pairs={{0,508},{4,0},{8,4},{12,8},{16,12},{20,16},{24,20},{28,24},{32,28}... | collective-permute-start | bytes 36872 | tf_op jit(solution)/shard_map/ppermute | solution.py:118

commit v12 on v11

--- a/solution.py
+++ b/solution.py
@@ -186,7 +186,7 @@
         time_table = (target[..., None] == time_iota).astype(jnp.float32)
         picked = jnp.concatenate(
             [
-                jnp.einsum("ecji,ecis->jsec", time_table, window, precision=PRECISE).reshape(
+                jnp.einsum("ecji,ecis->jsec", time_table, window, precision=lax.Precision.HIGH).reshape(
                     block_len * scen_rows, port_total
                 )
                 * line_scale[None, :],

time: 154 us -> 153 us (level)
  no operation moved by 1% of the time
where the time goes in v12:
time: 153 us
  blocking collectives  76.7 us (50%)
  starting transfers between devices  32.6 us (21%)
  Pallas kernels  24.2 us (16%)
  local copies, waits for them, and re-layouts  10.5 us (7%)
  other arithmetic  5.48 us (4%)
  matrix products  1.79 us (1%)
    psum x3, blocking collectives, sum_both(): fault_value = lax.psum(fault_value, axis)  58.9 us
    ppermute x8, starting transfers between devices, passed_along(): return lax.ppermute(value, axis, pairs)  32.6 us
    pallas_call x2, Pallas kernels, block_scan(): pl.pallas_call(functools.partial(block_scan_kernel, block_start), grid=(1...  24.2 us
    psum x1, blocking collectives, sum_both(): lax.psum((fault_mask * fault_value[None], control_mask * control_value[No...  17.8 us
  transfers between devices with their start and end apart: 8, of which 1 were waited for; matrix products, arithmetic and copies ran while one was open for 2% of the time, Pallas kernels for 0%

profile of v12, /device:TPU:10, one launch (start us, length us, event | category | flops | bytes accessed | tf_op | source)
XLA Modules:
  0.0 152.8 jit_solution(9479963988256478196)
XLA Ops:
  0.7 0.8 eq.125
  1.8 0.8 fusion.20
  3.0 0.8 add_add_fusion
  3.7 1.3 convolution_bitcast_fusion.1
  5.1 0.2 copy.106
  5.8 0.8 copy.109.picked_ref
  6.8 0.3 copy.108
  7.1 0.8 convert_element_type.38.pick_ref
  7.9 0.7 copy.110.voltage_ref
  8.6 0.7 add_convert_fusion.spread_ref
  9.3 12.1 %shard_map.165 = (f32[16,1024]{1,0:T(8,128)}, f32[384,48]{1,0:T(8,128)}, f32[1,16]{1,0:T(1,128)}) custom-call(bf16[48,1,16,1024]{3,2,1,0:T(8,128)(2,1)} %grad_ref.3, f32[384,48]{1,0:T(8,128)} %copy.109.picked_ref, f32[48,1024]{1,0:T(8,128)} %add_convert_fusion.spread_ref, f32[1,1024]{1,0:T(1,128)} %companion_ref.3, f32[16,1024]{1,0:T(8,128)} %bitcast.68, ...), custom_call_target="tpu_custom_call" | custom-call | tf_op jit(solution)/shard_map/pallas_call | solution.py:89
  21.4 1.1 copy.111
  22.9 6.8 %collective-permute-start.3 = (f32[8,384]{1,0:T(8,128)S(1)}, f32[8,384]{1,0:T(8,128)S(1)}, u32[]{:S(2)}, u32[]{:S(2)}) collective-permute-start(f32[8,384]{1,0:T(8,128)S(1)} %squeeze.56), channel_id=1, source_target_pairs={{0,32},{4,36},{8,40},{12,44},{16,48},{20,52},{24,56},{28,60},{32,6... | collective-permute-start | bytes 36872 | tf_op jit(solution)/shard_map/ppermute | solution.py:118
  29.8 3.8 %collective-permute-start.2 = (f32[8,384]{1,0:T(8,128)S(1)}, f32[8,384]{1,0:T(8,128)S(1)}, u32[]{:S(2)}, u32[]{:S(2)}) collective-permute-start(f32[8,384]{1,0:T(8,128)S(1)} %squeeze.55), channel_id=1, source_target_pairs={{0,480},{4,484},{8,488},{12,492},{16,496},{20,500},{24,504},{28,50... | collective-permute-start | bytes 36872 | tf_op jit(solution)/shard_map/ppermute | solution.py:118
  33.8 1.9 %collective-permute-start.1 = (f32[8,384]{1,0:T(8,128)S(1)}, f32[8,384]{1,0:T(8,128)S(1)}, u32[]{:S(2)}, u32[]{:S(2)}) collective-permute-start(f32[8,384]{1,0:T(8,128)S(1)} %squeeze.54), channel_id=1, source_target_pairs={{0,4},{4,8},{8,12},{12,16},{16,20},{20,24},{24,28},{28,32},{32,36}... | collective-permute-start | bytes 36872 | tf_op jit(solution)/shard_map/ppermute | solution.py:118
  35.8 3.8 %collective-permute-start = (f32[8,384]{1,0:T(8,128)S(1)}, f32[8,384]{1,0:T(8,128)S(1)}, u32[]{:S(2)}, u32[]{:S(2)}) collective-permute-start(f32[8,384]{1,0:T(8,128)S(1)} %squeeze.53), channel_id=1, source_target_pairs={{0,508},{4,0},{8,4},{12,8},{16,12},{20,16},{24,20},{28,24},{32,28}... | collective-permute-start | bytes 36872 | tf_op jit(solution)/shard_map/ppermute | solution.py:118
  40.6 0.2 collective-permute-done
  41.0 0.5 convolution_bitcast_fusion
  41.9 0.8 copy.118.picked_ref
  42.7 12.1 %shard_map.166 = (f32[16,1024]{1,0:T(8,128)}, f32[384,48]{1,0:T(8,128)}, f32[1,16]{1,0:T(1,128)}) custom-call(bf16[48,1,16,1024]{3,2,1,0:T(8,128)(2,1)} %grad_ref.3, f32[384,48]{1,0:T(8,128)} %copy.118.picked_ref, f32[48,1024]{1,0:T(8,128)} %add_convert_fusion.spread_ref, f32[1,1024]{1,0:T(1,128)} %companion_ref.3, f32[16,1024]{1,0:T(8,128)} %get-tuple-element.17.start_ref, ...), custom_call_target="tpu_custom_call" | custom-call | tf_op jit(solution)/shard_map/pallas_call | solution.py:89
  54.8 1.1 copy.120
  56.4 5.9 %collective-permute-start.7 = (f32[8,384]{1,0:T(8,128)S(1)}, f32[8,384]{1,0:T(8,128)S(1)}, u32[]{:S(2)}, u32[]{:S(2)}) collective-permute-start(f32[8,384]{1,0:T(8,128)S(1)} %squeeze.61), channel_id=1, source_target_pairs={{0,32},{4,36},{8,40},{12,44},{16,48},{20,52},{24,56},{28,60},{32,6... | collective-permute-start | bytes 36872 | tf_op jit(solution)/shard_map/ppermute | solution.py:118
  62.4 4.7 %collective-permute-start.6 = (f32[8,384]{1,0:T(8,128)S(1)}, f32[8,384]{1,0:T(8,128)S(1)}, u32[]{:S(2)}, u32[]{:S(2)}) collective-permute-start(f32[8,384]{1,0:T(8,128)S(1)} %squeeze.60), channel_id=1, source_target_pairs={{0,480},{4,484},{8,488},{12,492},{16,496},{20,500},{24,504},{28,50... | collective-permute-start | bytes 36872 | tf_op jit(solution)/shard_map/ppermute | solution.py:118
  67.2 3.0 %collective-permute-start.5 = (f32[8,384]{1,0:T(8,128)S(1)}, f32[8,384]{1,0:T(8,128)S(1)}, u32[]{:S(2)}, u32[]{:S(2)}) collective-permute-start(f32[8,384]{1,0:T(8,128)S(1)} %squeeze.59), channel_id=1, source_target_pairs={{0,4},{4,8},{8,12},{12,16},{16,20},{20,24},{24,28},{28,32},{32,36}... | collective-permute-start | bytes 36872 | tf_op jit(solution)/shard_map/ppermute | solution.py:118
  70.3 2.6 %collective-permute-start.4 = (f32[8,384]{1,0:T(8,128)S(1)}, f32[8,384]{1,0:T(8,128)S(1)}, u32[]{:S(2)}, u32[]{:S(2)}) collective-permute-start(f32[8,384]{1,0:T(8,128)S(1)} %squeeze.58), channel_id=1, source_target_pairs={{0,508},{4,0},{8,4},{12,8},{16,12},{20,16},{24,20},{28,24},{32,28}... | collective-permute-start | bytes 36872 | tf_op jit(solution)/shard_map/ppermute | solution.py:118
  72.9 2.5 %psum.36 = f32[16]{0:T(128)S(1)} all-reduce(f32[16]{0:T(128)S(1)} %add.68), channel_id=1, replica_groups=mesh['z_hi'=2,'x'=4,'y'=8,'core'=2,'scen'=4] {'core'}, use_global_device_ids=true, to_apply=%region_4.0 | all-reduce | flops 16 | bytes 128 | tf_op jit(solution)/shard_map/psum | solution.py:21
  75.4 20.5 %psum.37 = f32[16]{0:T(128)S(1)} all-reduce(f32[16]{0:T(128)S(1)} %psum.36), channel_id=1, replica_groups=mesh['z_hi'=2,'x'=4,'y'=8,'core'=2,'scen'=4] {'y'}, use_global_device_ids=true, to_apply=%region_5.0 | all-reduce | flops 16 | bytes 128 | tf_op jit(solution)/shard_map/psum | solution.py:21
  95.9 36.0 %psum.38 = f32[16]{0:T(128)S(1)} all-reduce(f32[16]{0:T(128)S(1)} %psum.37), channel_id=1, replica_groups=mesh['z_hi'=2,'x'=4,'y'=8,'core'=2,'scen'=4] {'x'}, use_global_device_ids=true, to_apply=%region_6.0 | all-reduce | flops 16 | bytes 128 | tf_op jit(solution)/shard_map/psum | solution.py:21
  132.2 17.8 %all-reduce = (f32[2,16]{1,0:T(2,128)S(1)}, f32[4,16]{1,0:T(4,128)S(1)}) all-reduce(f32[2,16]{1,0:T(2,128)S(1)} %broadcast_multiply_fusion.5, f32[4,16]{1,0:T(4,128)S(1)} %broadcast_multiply_fusion.4), channel_id=1, replica_groups=mesh['z_hi'=2,'x'=4,'y'=8,'core'=2,'scen'=4] {'z_hi','scen'}, use_global_device_ids=true, to_apply=%region_2.0 | all-reduce | flops 96 | bytes 768 | tf_op jit(solution)/shard_map/psum | solution.py:28
  150.0 0.6 multiply_reduce_fusion
  150.6 0.6 multiply_reduce_fusion.1
  151.9 0.9 maximum_bitcast_fusion
  (94 shorter events, 5.2 us)
Async XLA Ops:
  0.6 4.8 %copy-start.7 = (s32[1,4]{1,0:T(1,128)S(1)}, s32[1,4]{1,0:T(1,128)}, u32[]{:S(2)}) copy-start(s32[1,4]{1,0:T(1,128)} %param.19) | copy-start | bytes 52
  0.6 5.0 %copy-start.5 = (f32[1,4,8]{2,1,0:T(4,128)S(1)}, f32[1,4,8]{2,1,0:T(4,128)}, u32[]{:S(2)}) copy-start(f32[1,4,8]{2,1,0:T(4,128)} %param.21) | copy-start | bytes 388
  0.7 6.0 %copy-start.8 = (s32[16]{0:T(128)S(1)}, s32[16]{0:T(128)}, u32[]{:S(2)}) copy-start(s32[16]{0:T(128)} %param.25) | copy-start | bytes 196
  0.7 6.0 %copy-start.6 = (s32[1,16]{1,0:T(1,128)S(1)}, s32[1,16]{1,0:T(1,128)}, u32[]{:S(2)}) copy-start(s32[1,16]{1,0:T(1,128)} %param.23) | copy-start | bytes 196
  0.7 7.2 %copy-start.4 = (f32[48,16]{0,1:T(8,128)S(1)}, f32[48,16]{0,1:T(8,128)}, u32[]{:S(2)}) copy-start(f32[48,16]{0,1:T(8,128)} %param.27) | copy-start | bytes 9220
  21.4 18.2 %copy-start.3 = (f32[1,48,16,16]{1,3,2,0:T(8,128)S(1)}, f32[1,48,16,16]{1,3,2,0:T(8,128)}, u32[]{:S(2)}) copy-start(f32[1,48,16,16]{1,3,2,0:T(8,128)} %param.24) | copy-start | bytes 147460
  22.6 18.3 %copy-start = (f32[1,4,8,48,16]{3,4,2,1,0:T(8,128)S(1)}, f32[1,4,8,48,16]{3,4,2,1,0:T(8,128)}, u32[]{:S(2)}) copy-start(f32[1,4,8,48,16]{3,4,2,1,0:T(8,128)} %param.22) | copy-start | bytes 294916
  22.9 17.1 %collective-permute-start.3 = (f32[8,384]{1,0:T(8,128)S(1)}, f32[8,384]{1,0:T(8,128)S(1)}, u32[]{:S(2)}, u32[]{:S(2)}) collective-permute-start(f32[8,384]{1,0:T(8,128)S(1)} %squeeze.56), channel_id=1, source_target_pairs={{0,32},{4,36},{8,40},{12,44},{16,48},{20,52},{24,56},{28,60},{32,6... | collective-permute-start | bytes 36872 | tf_op jit(solution)/shard_map/ppermute | solution.py:118
  29.8 10.4 %collective-permute-start.2 = (f32[8,384]{1,0:T(8,128)S(1)}, f32[8,384]{1,0:T(8,128)S(1)}, u32[]{:S(2)}, u32[]{:S(2)}) collective-permute-start(f32[8,384]{1,0:T(8,128)S(1)} %squeeze.55), channel_id=1, source_target_pairs={{0,480},{4,484},{8,488},{12,492},{16,496},{20,500},{24,504},{28,50... | collective-permute-start | bytes 36872 | tf_op jit(solution)/shard_map/ppermute | solution.py:118
  33.8 6.7 %collective-permute-start.1 = (f32[8,384]{1,0:T(8,128)S(1)}, f32[8,384]{1,0:T(8,128)S(1)}, u32[]{:S(2)}, u32[]{:S(2)}) collective-permute-start(f32[8,384]{1,0:T(8,128)S(1)} %squeeze.54), channel_id=1, source_target_pairs={{0,4},{4,8},{8,12},{12,16},{16,20},{20,24},{24,28},{28,32},{32,36}... | collective-permute-start | bytes 36872 | tf_op jit(solution)/shard_map/ppermute | solution.py:118
  35.8 5.0 %collective-permute-start = (f32[8,384]{1,0:T(8,128)S(1)}, f32[8,384]{1,0:T(8,128)S(1)}, u32[]{:S(2)}, u32[]{:S(2)}) collective-permute-start(f32[8,384]{1,0:T(8,128)S(1)} %squeeze.53), channel_id=1, source_target_pairs={{0,508},{4,0},{8,4},{12,8},{16,12},{20,16},{24,20},{28,24},{32,28}... | collective-permute-start | bytes 36872 | tf_op jit(solution)/shard_map/ppermute | solution.py:118
  54.8 18.1 %copy-start.9 = (f32[1,16]{1,0:T(1,128)S(1)}, f32[1,16]{1,0:T(1,128)}, u32[]{:S(2)}) copy-start(f32[1,16]{1,0:T(1,128)} %get-tuple-element.15) | copy-start | bytes 196
  54.8 18.1 %copy-start.10 = (f32[1,16]{1,0:T(1,128)S(1)}, f32[1,16]{1,0:T(1,128)}, u32[]{:S(2)}) copy-start(f32[1,16]{1,0:T(1,128)} %get-tuple-element.20) | copy-start | bytes 196
  54.8 77.0 %copy-start.1 = (f32[384,48]{1,0:T(8,128)S(1)}, f32[384,48]{1,0:T(8,128)}, u32[]{:S(2)}) copy-start(f32[384,48]{1,0:T(8,128)} %get-tuple-element.16) | copy-start | bytes 221188
  54.8 77.0 %copy-start.2 = (f32[384,48]{1,0:T(8,128)S(1)}, f32[384,48]{1,0:T(8,128)}, u32[]{:S(2)}) copy-start(f32[384,48]{1,0:T(8,128)} %get-tuple-element.21) | copy-start | bytes 221188
  56.4 94.8 %collective-permute-start.7 = (f32[8,384]{1,0:T(8,128)S(1)}, f32[8,384]{1,0:T(8,128)S(1)}, u32[]{:S(2)}, u32[]{:S(2)}) collective-permute-start(f32[8,384]{1,0:T(8,128)S(1)} %squeeze.61), channel_id=1, source_target_pairs={{0,32},{4,36},{8,40},{12,44},{16,48},{20,52},{24,56},{28,60},{32,6... | collective-permute-start | bytes 36872 | tf_op jit(solution)/shard_map/ppermute | solution.py:118
  62.4 89.0 %collective-permute-start.6 = (f32[8,384]{1,0:T(8,128)S(1)}, f32[8,384]{1,0:T(8,128)S(1)}, u32[]{:S(2)}, u32[]{:S(2)}) collective-permute-start(f32[8,384]{1,0:T(8,128)S(1)} %squeeze.60), channel_id=1, source_target_pairs={{0,480},{4,484},{8,488},{12,492},{16,496},{20,500},{24,504},{28,50... | collective-permute-start | bytes 36872 | tf_op jit(solution)/shard_map/ppermute | solution.py:118
  67.2 84.3 %collective-permute-start.5 = (f32[8,384]{1,0:T(8,128)S(1)}, f32[8,384]{1,0:T(8,128)S(1)}, u32[]{:S(2)}, u32[]{:S(2)}) collective-permute-start(f32[8,384]{1,0:T(8,128)S(1)} %squeeze.59), channel_id=1, source_target_pairs={{0,4},{4,8},{8,12},{12,16},{16,20},{20,24},{24,28},{28,32},{32,36}... | collective-permute-start | bytes 36872 | tf_op jit(solution)/shard_map/ppermute | solution.py:118
  70.3 81.4 %collective-permute-start.4 = (f32[8,384]{1,0:T(8,128)S(1)}, f32[8,384]{1,0:T(8,128)S(1)}, u32[]{:S(2)}, u32[]{:S(2)}) collective-permute-start(f32[8,384]{1,0:T(8,128)S(1)} %squeeze.58), channel_id=1, source_target_pairs={{0,508},{4,0},{8,4},{12,8},{16,12},{20,16},{24,20},{28,24},{32,28}... | collective-permute-start | bytes 36872 | tf_op jit(solution)/shard_map/ppermute | solution.py:118

commit v13 on v12

--- a/solution.py
+++ b/solution.py
@@ -69,13 +69,20 @@
 
     last_ref[...] = lax.fori_loop(0, steps, one_step, start_ref[...], unroll=True)
     adjoint_block = adjoint_ref[...]
-    samples_ref[...] = jnp.dot(
+    picks = jnp.dot(
         adjoint_block, pick_ref[...], precision=lax.Precision.HIGH, preferred_element_type=jnp.float32
     )
-    fault_table = spread_ref[pl.ds(spread_ref.shape[0] - scen_rows, scen_rows), :]
-    at_fault = jnp.sum(adjoint_block.reshape(steps, scen_rows, node_count) * fault_table[None], axis=2)
+    sample_count = samples_ref.shape[1]
+    samples_ref[...] = picks[:, :sample_count]
+    at_fault = picks[:, sample_count:].reshape(steps, scen_rows, scen_rows)
+    own = (
+        lax.broadcasted_iota(jnp.int32, (scen_rows, scen_rows), 0)
+        == lax.broadcasted_iota(jnp.int32, (scen_rows, scen_rows), 1)
+    ).astype(jnp.float32)
     voltage = voltage_ref[pl.ds(block_start, steps), :]
-    fault_out_ref[...] = jnp.sum(at_fault * voltage, axis=0, keepdims=True)
+    fault_out_ref[...] = jnp.sum(
+        jnp.sum(at_fault * own[None] * voltage[:, None, :], axis=0), axis=0, keepdims=True
+    )
 
 
 def whole(array):
@@ -97,12 +104,12 @@
         + [whole(array) for array in operands[1:]],
         out_specs=(
             whole(start),
-            pl.BlockSpec((steps * scen_rows, pick.shape[1]), lambda index: (0, 0)),
+            pl.BlockSpec((steps * scen_rows, pick.shape[1] - scen_rows), lambda index: (0, 0)),
             pl.BlockSpec((1, scen_rows), lambda index: (0, 0)),
         ),
         out_shape=(
             jax.ShapeDtypeStruct(start.shape, jnp.float32),
-            jax.ShapeDtypeStruct((steps * scen_rows, pick.shape[1]), jnp.float32),
+            jax.ShapeDtypeStruct((steps * scen_rows, pick.shape[1] - scen_rows), jnp.float32),
             jax.ShapeDtypeStruct((1, scen_rows), jnp.float32),
         ),
         scratch_shapes=[
@@ -155,6 +162,7 @@
         [
             node_iota[:, None] == port_node[0].reshape(port_total)[None, :],
             node_iota[:, None] == conv_node[0][None, :],
+            node_iota[:, None] == (fault_bus - sub_index * node_count)[None, :],
         ],
         axis=1,
     ).astype(jnp.float32)

time: 153 us -> 154 us (level)
  no operation moved by 1% of the time
where the time goes in v13:
time: 154 us; the launch traced here: 153 us
  blocking collectives  76.7 us (50%)
  starting transfers between devices  32.6 us (21%)
  Pallas kernels  24.3 us (16%)
  local copies, waits for them, and re-layouts  10.3 us (7%)
  other arithmetic  5.93 us (4%)
  matrix products  1.79 us (1%)
    psum x3, blocking collectives, sum_both(): fault_value = lax.psum(fault_value, axis)  58.9 us
    ppermute x8, starting transfers between devices, passed_along(): return lax.ppermute(value, axis, pairs)  32.6 us
    pallas_call x2, Pallas kernels, block_scan(): pl.pallas_call(functools.partial(block_scan_kernel, block_start), grid=(1...  24.3 us
    psum x1, blocking collectives, sum_both(): lax.psum((fault_mask * fault_value[None], control_mask * control_value[No...  17.8 us
  transfers between devices with their start and end apart: 8, of which 1 were waited for; matrix products, arithmetic and copies ran while one was open for 2% of the time, Pallas kernels for 0%

profile of v13, /device:TPU:10, one launch (start us, length us, event | category | flops | bytes accessed | tf_op | source)
XLA Modules:
  0.0 152.9 jit_solution(15856820656388216070)
XLA Ops:
  0.7 0.8 eq.138
  1.8 0.8 fusion.20
  3.0 0.8 add_add_fusion
  3.7 1.3 convolution_bitcast_fusion.1
  5.1 0.2 copy.104
  5.8 0.8 copy.106.picked_ref
  6.9 0.7 copy.107.voltage_ref
  7.6 0.7 add_convert_fusion.1.spread_ref
  8.3 1.1 add_convert_fusion.pick_ref
  9.4 12.1 %shard_map.165 = (f32[16,1024]{1,0:T(8,128)}, f32[384,48]{1,0:T(8,128)}, f32[1,16]{1,0:T(1,128)}) custom-call(bf16[48,1,16,1024]{3,2,1,0:T(8,128)(2,1)} %grad_ref.3, f32[384,48]{1,0:T(8,128)} %copy.106.picked_ref, f32[48,1024]{1,0:T(8,128)} %add_convert_fusion.1.spread_ref, f32[1,1024]{1,0:T(1,128)} %companion_ref.3, f32[16,1024]{1,0:T(8,128)} %bitcast.68, ...), custom_call_target="tpu_custom_call" | custom-call | tf_op jit(solution)/shard_map/pallas_call | solution.py:96
  21.5 1.1 copy.108
  22.6 0.2 reshape.153
  23.0 6.8 %collective-permute-start.3 = (f32[8,384]{1,0:T(8,128)S(1)}, f32[8,384]{1,0:T(8,128)S(1)}, u32[]{:S(2)}, u32[]{:S(2)}) collective-permute-start(f32[8,384]{1,0:T(8,128)S(1)} %squeeze.56), channel_id=1, source_target_pairs={{0,32},{4,36},{8,40},{12,44},{16,48},{20,52},{24,56},{28,60},{32,6... | collective-permute-start | bytes 36872 | tf_op jit(solution)/shard_map/ppermute | solution.py:125
  30.0 3.8 %collective-permute-start.2 = (f32[8,384]{1,0:T(8,128)S(1)}, f32[8,384]{1,0:T(8,128)S(1)}, u32[]{:S(2)}, u32[]{:S(2)}) collective-permute-start(f32[8,384]{1,0:T(8,128)S(1)} %squeeze.55), channel_id=1, source_target_pairs={{0,480},{4,484},{8,488},{12,492},{16,496},{20,500},{24,504},{28,50... | collective-permute-start | bytes 36872 | tf_op jit(solution)/shard_map/ppermute | solution.py:125
  33.9 1.9 %collective-permute-start.1 = (f32[8,384]{1,0:T(8,128)S(1)}, f32[8,384]{1,0:T(8,128)S(1)}, u32[]{:S(2)}, u32[]{:S(2)}) collective-permute-start(f32[8,384]{1,0:T(8,128)S(1)} %squeeze.54), channel_id=1, source_target_pairs={{0,4},{4,8},{8,12},{12,16},{16,20},{20,24},{24,28},{28,32},{32,36}... | collective-permute-start | bytes 36872 | tf_op jit(solution)/shard_map/ppermute | solution.py:125
  35.9 3.8 %collective-permute-start = (f32[8,384]{1,0:T(8,128)S(1)}, f32[8,384]{1,0:T(8,128)S(1)}, u32[]{:S(2)}, u32[]{:S(2)}) collective-permute-start(f32[8,384]{1,0:T(8,128)S(1)} %squeeze.53), channel_id=1, source_target_pairs={{0,508},{4,0},{8,4},{12,8},{16,12},{20,16},{24,20},{28,24},{32,28}... | collective-permute-start | bytes 36872 | tf_op jit(solution)/shard_map/ppermute | solution.py:125
  41.1 0.5 convolution_bitcast_fusion
  41.6 0.2 copy.113
  42.0 0.8 copy.115.picked_ref
  42.9 12.1 %shard_map.166 = (f32[16,1024]{1,0:T(8,128)}, f32[384,48]{1,0:T(8,128)}, f32[1,16]{1,0:T(1,128)}) custom-call(bf16[48,1,16,1024]{3,2,1,0:T(8,128)(2,1)} %grad_ref.3, f32[384,48]{1,0:T(8,128)} %copy.115.picked_ref, f32[48,1024]{1,0:T(8,128)} %add_convert_fusion.1.spread_ref, f32[1,1024]{1,0:T(1,128)} %companion_ref.3, ...), custom_call_target="tpu_custom_call" | custom-call | tf_op jit(solution)/shard_map/pallas_call | solution.py:96
  55.0 1.1 copy.117
  56.5 5.9 %collective-permute-start.7 = (f32[8,384]{1,0:T(8,128)S(1)}, f32[8,384]{1,0:T(8,128)S(1)}, u32[]{:S(2)}, u32[]{:S(2)}) collective-permute-start(f32[8,384]{1,0:T(8,128)S(1)} %squeeze.61), channel_id=1, source_target_pairs={{0,32},{4,36},{8,40},{12,44},{16,48},{20,52},{24,56},{28,60},{32,6... | collective-permute-start | bytes 36872 | tf_op jit(solution)/shard_map/ppermute | solution.py:125
  62.5 4.7 %collective-permute-start.6 = (f32[8,384]{1,0:T(8,128)S(1)}, f32[8,384]{1,0:T(8,128)S(1)}, u32[]{:S(2)}, u32[]{:S(2)}) collective-permute-start(f32[8,384]{1,0:T(8,128)S(1)} %squeeze.60), channel_id=1, source_target_pairs={{0,480},{4,484},{8,488},{12,492},{16,496},{20,500},{24,504},{28,50... | collective-permute-start | bytes 36872 | tf_op jit(solution)/shard_map/ppermute | solution.py:125
  67.4 3.0 %collective-permute-start.5 = (f32[8,384]{1,0:T(8,128)S(1)}, f32[8,384]{1,0:T(8,128)S(1)}, u32[]{:S(2)}, u32[]{:S(2)}) collective-permute-start(f32[8,384]{1,0:T(8,128)S(1)} %squeeze.59), channel_id=1, source_target_pairs={{0,4},{4,8},{8,12},{12,16},{16,20},{20,24},{24,28},{28,32},{32,36}... | collective-permute-start | bytes 36872 | tf_op jit(solution)/shard_map/ppermute | solution.py:125
  70.5 2.6 %collective-permute-start.4 = (f32[8,384]{1,0:T(8,128)S(1)}, f32[8,384]{1,0:T(8,128)S(1)}, u32[]{:S(2)}, u32[]{:S(2)}) collective-permute-start(f32[8,384]{1,0:T(8,128)S(1)} %squeeze.58), channel_id=1, source_target_pairs={{0,508},{4,0},{8,4},{12,8},{16,12},{20,16},{24,20},{28,24},{32,28}... | collective-permute-start | bytes 36872 | tf_op jit(solution)/shard_map/ppermute | solution.py:125
  73.2 2.5 %psum.36 = f32[16]{0:T(128)S(1)} all-reduce(f32[16]{0:T(128)S(1)} %add.68), channel_id=1, replica_groups=mesh['z_hi'=2,'x'=4,'y'=8,'core'=2,'scen'=4] {'core'}, use_global_device_ids=true, to_apply=%region_4.0 | all-reduce | flops 16 | bytes 128 | tf_op jit(solution)/shard_map/psum | solution.py:21
  75.7 20.5 %psum.37 = f32[16]{0:T(128)S(1)} all-reduce(f32[16]{0:T(128)S(1)} %psum.36), channel_id=1, replica_groups=mesh['z_hi'=2,'x'=4,'y'=8,'core'=2,'scen'=4] {'y'}, use_global_device_ids=true, to_apply=%region_5.0 | all-reduce | flops 16 | bytes 128 | tf_op jit(solution)/shard_map/psum | solution.py:21
  96.2 36.0 %psum.38 = f32[16]{0:T(128)S(1)} all-reduce(f32[16]{0:T(128)S(1)} %psum.37), channel_id=1, replica_groups=mesh['z_hi'=2,'x'=4,'y'=8,'core'=2,'scen'=4] {'x'}, use_global_device_ids=true, to_apply=%region_6.0 | all-reduce | flops 16 | bytes 128 | tf_op jit(solution)/shard_map/psum | solution.py:21
  132.3 17.8 %all-reduce = (f32[2,16]{1,0:T(2,128)S(1)}, f32[4,16]{1,0:T(4,128)S(1)}) all-reduce(f32[2,16]{1,0:T(2,128)S(1)} %broadcast_multiply_fusion.5, f32[4,16]{1,0:T(4,128)S(1)} %broadcast_multiply_fusion.4), channel_id=1, replica_groups=mesh['z_hi'=2,'x'=4,'y'=8,'core'=2,'scen'=4] {'z_hi','scen'}, use_global_device_ids=true, to_apply=%region_2.0 | all-reduce | flops 96 | bytes 768 | tf_op jit(solution)/shard_map/psum | solution.py:28
  150.1 0.6 multiply_reduce_fusion
  150.7 0.6 multiply_reduce_fusion.1
  152.0 0.9 maximum_bitcast_fusion
  (93 shorter events, 5.0 us)
Async XLA Ops:
  0.6 4.8 %copy-start.7 = (s32[1,4]{1,0:T(1,128)S(1)}, s32[1,4]{1,0:T(1,128)}, u32[]{:S(2)}) copy-start(s32[1,4]{1,0:T(1,128)} %param.19) | copy-start | bytes 52
  0.6 5.0 %copy-start.5 = (f32[1,4,8]{2,1,0:T(4,128)S(1)}, f32[1,4,8]{2,1,0:T(4,128)}, u32[]{:S(2)}) copy-start(f32[1,4,8]{2,1,0:T(4,128)} %param.21) | copy-start | bytes 388
  0.7 6.0 %copy-start.8 = (s32[16]{0:T(128)S(1)}, s32[16]{0:T(128)}, u32[]{:S(2)}) copy-start(s32[16]{0:T(128)} %param.25) | copy-start | bytes 196
  0.7 6.0 %copy-start.6 = (s32[1,16]{1,0:T(1,128)S(1)}, s32[1,16]{1,0:T(1,128)}, u32[]{:S(2)}) copy-start(s32[1,16]{1,0:T(1,128)} %param.23) | copy-start | bytes 196
  0.7 6.2 %copy-start.4 = (f32[48,16]{0,1:T(8,128)S(1)}, f32[48,16]{0,1:T(8,128)}, u32[]{:S(2)}) copy-start(f32[48,16]{0,1:T(8,128)} %param.27) | copy-start | bytes 9220
  21.5 18.3 %copy-start.3 = (f32[1,48,16,16]{1,3,2,0:T(8,128)S(1)}, f32[1,48,16,16]{1,3,2,0:T(8,128)}, u32[]{:S(2)}) copy-start(f32[1,48,16,16]{1,3,2,0:T(8,128)} %param.24) | copy-start | bytes 147460
  21.5 18.5 %copy-start.1 = (f32[384,48]{1,0:T(8,128)S(1)}, f32[384,48]{1,0:T(8,128)}, u32[]{:S(2)}) copy-start(f32[384,48]{1,0:T(8,128)} %get-tuple-element.16) | copy-start | bytes 221188
  22.9 18.2 %copy-start = (f32[1,4,8,48,16]{3,4,2,1,0:T(8,128)S(1)}, f32[1,4,8,48,16]{3,4,2,1,0:T(8,128)}, u32[]{:S(2)}) copy-start(f32[1,4,8,48,16]{3,4,2,1,0:T(8,128)} %param.22) | copy-start | bytes 294916
  23.0 17.3 %collective-permute-start.3 = (f32[8,384]{1,0:T(8,128)S(1)}, f32[8,384]{1,0:T(8,128)S(1)}, u32[]{:S(2)}, u32[]{:S(2)}) collective-permute-start(f32[8,384]{1,0:T(8,128)S(1)} %squeeze.56), channel_id=1, source_target_pairs={{0,32},{4,36},{8,40},{12,44},{16,48},{20,52},{24,56},{28,60},{32,6... | collective-permute-start | bytes 36872 | tf_op jit(solution)/shard_map/ppermute | solution.py:125
  30.0 10.5 %collective-permute-start.2 = (f32[8,384]{1,0:T(8,128)S(1)}, f32[8,384]{1,0:T(8,128)S(1)}, u32[]{:S(2)}, u32[]{:S(2)}) collective-permute-start(f32[8,384]{1,0:T(8,128)S(1)} %squeeze.55), channel_id=1, source_target_pairs={{0,480},{4,484},{8,488},{12,492},{16,496},{20,500},{24,504},{28,50... | collective-permute-start | bytes 36872 | tf_op jit(solution)/shard_map/ppermute | solution.py:125
  33.9 6.8 %collective-permute-start.1 = (f32[8,384]{1,0:T(8,128)S(1)}, f32[8,384]{1,0:T(8,128)S(1)}, u32[]{:S(2)}, u32[]{:S(2)}) collective-permute-start(f32[8,384]{1,0:T(8,128)S(1)} %squeeze.54), channel_id=1, source_target_pairs={{0,4},{4,8},{8,12},{12,16},{16,20},{20,24},{24,28},{28,32},{32,36}... | collective-permute-start | bytes 36872 | tf_op jit(solution)/shard_map/ppermute | solution.py:125
  35.9 5.0 %collective-permute-start = (f32[8,384]{1,0:T(8,128)S(1)}, f32[8,384]{1,0:T(8,128)S(1)}, u32[]{:S(2)}, u32[]{:S(2)}) collective-permute-start(f32[8,384]{1,0:T(8,128)S(1)} %squeeze.53), channel_id=1, source_target_pairs={{0,508},{4,0},{8,4},{12,8},{16,12},{20,16},{24,20},{28,24},{32,28}... | collective-permute-start | bytes 36872 | tf_op jit(solution)/shard_map/ppermute | solution.py:125
  55.0 18.1 %copy-start.2 = (f32[384,48]{1,0:T(8,128)S(1)}, f32[384,48]{1,0:T(8,128)}, u32[]{:S(2)}) copy-start(f32[384,48]{1,0:T(8,128)} %get-tuple-element.21) | copy-start | bytes 221188
  55.0 18.2 %copy-start.9 = (f32[1,16]{1,0:T(1,128)S(1)}, f32[1,16]{1,0:T(1,128)}, u32[]{:S(2)}) copy-start(f32[1,16]{1,0:T(1,128)} %get-tuple-element.15) | copy-start | bytes 196
  55.0 18.2 %copy-start.10 = (f32[1,16]{1,0:T(1,128)S(1)}, f32[1,16]{1,0:T(1,128)}, u32[]{:S(2)}) copy-start(f32[1,16]{1,0:T(1,128)} %get-tuple-element.20) | copy-start | bytes 196
  56.5 94.8 %collective-permute-start.7 = (f32[8,384]{1,0:T(8,128)S(1)}, f32[8,384]{1,0:T(8,128)S(1)}, u32[]{:S(2)}, u32[]{:S(2)}) collective-permute-start(f32[8,384]{1,0:T(8,128)S(1)} %squeeze.61), channel_id=1, source_target_pairs={{0,32},{4,36},{8,40},{12,44},{16,48},{20,52},{24,56},{28,60},{32,6... | collective-permute-start | bytes 36872 | tf_op jit(solution)/shard_map/ppermute | solution.py:125
  62.5 88.9 %collective-permute-start.6 = (f32[8,384]{1,0:T(8,128)S(1)}, f32[8,384]{1,0:T(8,128)S(1)}, u32[]{:S(2)}, u32[]{:S(2)}) collective-permute-start(f32[8,384]{1,0:T(8,128)S(1)} %squeeze.60), channel_id=1, source_target_pairs={{0,480},{4,484},{8,488},{12,492},{16,496},{20,500},{24,504},{28,50... | collective-permute-start | bytes 36872 | tf_op jit(solution)/shard_map/ppermute | solution.py:125
  67.4 84.3 %collective-permute-start.5 = (f32[8,384]{1,0:T(8,128)S(1)}, f32[8,384]{1,0:T(8,128)S(1)}, u32[]{:S(2)}, u32[]{:S(2)}) collective-permute-start(f32[8,384]{1,0:T(8,128)S(1)} %squeeze.59), channel_id=1, source_target_pairs={{0,4},{4,8},{8,12},{12,16},{16,20},{20,24},{24,28},{28,32},{32,36}... | collective-permute-start | bytes 36872 | tf_op jit(solution)/shard_map/ppermute | solution.py:125
  70.5 81.4 %collective-permute-start.4 = (f32[8,384]{1,0:T(8,128)S(1)}, f32[8,384]{1,0:T(8,128)S(1)}, u32[]{:S(2)}, u32[]{:S(2)}) collective-permute-start(f32[8,384]{1,0:T(8,128)S(1)} %squeeze.58), channel_id=1, source_target_pairs={{0,508},{4,0},{8,4},{12,8},{16,12},{20,16},{24,20},{28,24},{32,28}... | collective-permute-start | bytes 36872 | tf_op jit(solution)/shard_map/ppermute | solution.py:125

commit v14 on v12

--- a/solution.py
+++ b/solution.py
@@ -46,12 +46,18 @@
     fault_out_ref,
     inflow_ref,
     adjoint_ref,
+    weights_vmem,
+    weights_arrived,
 ):
     steps, scen_rows, node_count = grad_ref.shape
     companion = companion_ref[...]
+    weights_copy = pltpu.make_async_copy(weights_ref, weights_vmem, weights_arrived)
+    weights_copy.start()
     inflow_ref[...] = jnp.dot(
         picked_ref[...], spread_ref[...], precision=lax.Precision.HIGH, preferred_element_type=jnp.float32
     )
+
+    weights_copy.wait()
 
     def one_step(index, adjoint_prev):
         step = steps - 1 - index
@@ -62,7 +68,7 @@
             + inflow_ref[rows]
         )
         adjoint = jnp.dot(
-            right_side.astype(jnp.bfloat16), weights_ref[...], preferred_element_type=jnp.float32
+            right_side.astype(jnp.bfloat16), weights_vmem[...], preferred_element_type=jnp.float32
         )
         adjoint_ref[rows] = adjoint
         return adjoint
@@ -94,7 +100,10 @@
                 (steps, None, scen_rows, node_count), lambda index: (block_id, 0, 0, 0)
             )
         ]
-        + [whole(array) for array in operands[1:]],
+        + [
+            pl.BlockSpec(memory_space=pl.ANY) if array is weights else whole(array)
+            for array in operands[1:]
+        ],
         out_specs=(
             whole(start),
             pl.BlockSpec((steps * scen_rows, pick.shape[1]), lambda index: (0, 0)),
@@ -108,6 +117,8 @@
         scratch_shapes=[
             pltpu.VMEM((steps * scen_rows, node_count), jnp.float32),
             pltpu.VMEM((steps * scen_rows, node_count), jnp.float32),
+            pltpu.VMEM(weights.shape, weights.dtype),
+            pltpu.SemaphoreType.DMA,
         ],
     )(*operands)
 

time: 153 us -> 153 us (level)
  no operation moved by 1% of the time
where the time goes in v14:
time: 153 us
  blocking collectives  76.7 us (50%)
  starting transfers between devices  32.6 us (21%)
  Pallas kernels  23.9 us (16%)
  local copies, waits for them, and re-layouts  10.5 us (7%)
  other arithmetic  5.48 us (4%)
  matrix products  1.79 us (1%)
    psum x3, blocking collectives, sum_both(): fault_value = lax.psum(fault_value, axis)  59 us
    ppermute x8, starting transfers between devices, passed_along(): return lax.ppermute(value, axis, pairs)  32.6 us
    pallas_call x2, Pallas kernels, block_scan(): pl.pallas_call(functools.partial(block_scan_kernel, block_start), grid=(1...  23.9 us
    psum x1, blocking collectives, sum_both(): lax.psum((fault_mask * fault_value[None], control_mask * control_value[No...  17.8 us
  transfers between devices with their start and end apart: 8, of which 1 were waited for; matrix products, arithmetic and copies ran while one was open for 2% of the time, Pallas kernels for 0%

profile of v14, /device:TPU:10, one launch (start us, length us, event | category | flops | bytes accessed | tf_op | source)
XLA Modules:
  0.0 152.5 jit_solution(15923302525384987211)
XLA Ops:
  0.7 0.8 eq.125
  1.8 0.8 fusion.20
  3.0 0.8 add_add_fusion
  3.7 1.3 convolution_bitcast_fusion.1
  5.1 0.2 copy.106
  5.8 0.8 copy.109.picked_ref
  6.8 0.3 copy.108
  7.1 0.8 convert_element_type.38.pick_ref
  7.9 0.7 copy.110.voltage_ref
  8.6 0.7 add_convert_fusion.spread_ref
  9.3 12.0 %shard_map.165 = (f32[16,1024]{1,0:T(8,128)}, f32[384,48]{1,0:T(8,128)}, f32[1,16]{1,0:T(1,128)}) custom-call(bf16[48,1,16,1024]{3,2,1,0:T(8,128)(2,1)} %grad_ref.3, f32[384,48]{1,0:T(8,128)} %copy.109.picked_ref, f32[48,1024]{1,0:T(8,128)} %add_convert_fusion.spread_ref, f32[1,1024]{1,0:T(1,128)} %companion_ref.3, f32[16,1024]{1,0:T(8,128)} %bitcast.68, ...), custom_call_target="tpu_custom_call" | custom-call | tf_op jit(solution)/shard_map/pallas_call | solution.py:95
  21.3 1.1 copy.111
  22.7 6.8 %collective-permute-start.3 = (f32[8,384]{1,0:T(8,128)S(1)}, f32[8,384]{1,0:T(8,128)S(1)}, u32[]{:S(2)}, u32[]{:S(2)}) collective-permute-start(f32[8,384]{1,0:T(8,128)S(1)} %squeeze.56), channel_id=1, source_target_pairs={{0,32},{4,36},{8,40},{12,44},{16,48},{20,52},{24,56},{28,60},{32,6... | collective-permute-start | bytes 36872 | tf_op jit(solution)/shard_map/ppermute | solution.py:129
  29.7 3.8 %collective-permute-start.2 = (f32[8,384]{1,0:T(8,128)S(1)}, f32[8,384]{1,0:T(8,128)S(1)}, u32[]{:S(2)}, u32[]{:S(2)}) collective-permute-start(f32[8,384]{1,0:T(8,128)S(1)} %squeeze.55), channel_id=1, source_target_pairs={{0,480},{4,484},{8,488},{12,492},{16,496},{20,500},{24,504},{28,50... | collective-permute-start | bytes 36872 | tf_op jit(solution)/shard_map/ppermute | solution.py:129
  33.6 1.9 %collective-permute-start.1 = (f32[8,384]{1,0:T(8,128)S(1)}, f32[8,384]{1,0:T(8,128)S(1)}, u32[]{:S(2)}, u32[]{:S(2)}) collective-permute-start(f32[8,384]{1,0:T(8,128)S(1)} %squeeze.54), channel_id=1, source_target_pairs={{0,4},{4,8},{8,12},{12,16},{16,20},{20,24},{24,28},{28,32},{32,36}... | collective-permute-start | bytes 36872 | tf_op jit(solution)/shard_map/ppermute | solution.py:129
  35.6 3.8 %collective-permute-start = (f32[8,384]{1,0:T(8,128)S(1)}, f32[8,384]{1,0:T(8,128)S(1)}, u32[]{:S(2)}, u32[]{:S(2)}) collective-permute-start(f32[8,384]{1,0:T(8,128)S(1)} %squeeze.53), channel_id=1, source_target_pairs={{0,508},{4,0},{8,4},{12,8},{16,12},{20,16},{24,20},{28,24},{32,28}... | collective-permute-start | bytes 36872 | tf_op jit(solution)/shard_map/ppermute | solution.py:129
  40.4 0.2 collective-permute-done
  40.8 0.5 convolution_bitcast_fusion
  41.7 0.8 copy.118.picked_ref
  42.6 11.9 %shard_map.166 = (f32[16,1024]{1,0:T(8,128)}, f32[384,48]{1,0:T(8,128)}, f32[1,16]{1,0:T(1,128)}) custom-call(bf16[48,1,16,1024]{3,2,1,0:T(8,128)(2,1)} %grad_ref.3, f32[384,48]{1,0:T(8,128)} %copy.118.picked_ref, f32[48,1024]{1,0:T(8,128)} %add_convert_fusion.spread_ref, f32[1,1024]{1,0:T(1,128)} %companion_ref.3, f32[16,1024]{1,0:T(8,128)} %get-tuple-element.17.start_ref, ...), custom_call_target="tpu_custom_call" | custom-call | tf_op jit(solution)/shard_map/pallas_call | solution.py:95
  54.6 1.1 copy.120
  56.1 5.9 %collective-permute-start.7 = (f32[8,384]{1,0:T(8,128)S(1)}, f32[8,384]{1,0:T(8,128)S(1)}, u32[]{:S(2)}, u32[]{:S(2)}) collective-permute-start(f32[8,384]{1,0:T(8,128)S(1)} %squeeze.61), channel_id=1, source_target_pairs={{0,32},{4,36},{8,40},{12,44},{16,48},{20,52},{24,56},{28,60},{32,6... | collective-permute-start | bytes 36872 | tf_op jit(solution)/shard_map/ppermute | solution.py:129
  62.1 4.7 %collective-permute-start.6 = (f32[8,384]{1,0:T(8,128)S(1)}, f32[8,384]{1,0:T(8,128)S(1)}, u32[]{:S(2)}, u32[]{:S(2)}) collective-permute-start(f32[8,384]{1,0:T(8,128)S(1)} %squeeze.60), channel_id=1, source_target_pairs={{0,480},{4,484},{8,488},{12,492},{16,496},{20,500},{24,504},{28,50... | collective-permute-start | bytes 36872 | tf_op jit(solution)/shard_map/ppermute | solution.py:129
  66.9 3.0 %collective-permute-start.5 = (f32[8,384]{1,0:T(8,128)S(1)}, f32[8,384]{1,0:T(8,128)S(1)}, u32[]{:S(2)}, u32[]{:S(2)}) collective-permute-start(f32[8,384]{1,0:T(8,128)S(1)} %squeeze.59), channel_id=1, source_target_pairs={{0,4},{4,8},{8,12},{12,16},{16,20},{20,24},{24,28},{28,32},{32,36}... | collective-permute-start | bytes 36872 | tf_op jit(solution)/shard_map/ppermute | solution.py:129
  70.0 2.5 %collective-permute-start.4 = (f32[8,384]{1,0:T(8,128)S(1)}, f32[8,384]{1,0:T(8,128)S(1)}, u32[]{:S(2)}, u32[]{:S(2)}) collective-permute-start(f32[8,384]{1,0:T(8,128)S(1)} %squeeze.58), channel_id=1, source_target_pairs={{0,508},{4,0},{8,4},{12,8},{16,12},{20,16},{24,20},{28,24},{32,28}... | collective-permute-start | bytes 36872 | tf_op jit(solution)/shard_map/ppermute | solution.py:129
  72.6 2.5 %psum.36 = f32[16]{0:T(128)S(1)} all-reduce(f32[16]{0:T(128)S(1)} %add.68), channel_id=1, replica_groups=mesh['z_hi'=2,'x'=4,'y'=8,'core'=2,'scen'=4] {'core'}, use_global_device_ids=true, to_apply=%region_4.0 | all-reduce | flops 16 | bytes 128 | tf_op jit(solution)/shard_map/psum | solution.py:21
  75.1 20.5 %psum.37 = f32[16]{0:T(128)S(1)} all-reduce(f32[16]{0:T(128)S(1)} %psum.36), channel_id=1, replica_groups=mesh['z_hi'=2,'x'=4,'y'=8,'core'=2,'scen'=4] {'y'}, use_global_device_ids=true, to_apply=%region_5.0 | all-reduce | flops 16 | bytes 128 | tf_op jit(solution)/shard_map/psum | solution.py:21
  95.6 36.0 %psum.38 = f32[16]{0:T(128)S(1)} all-reduce(f32[16]{0:T(128)S(1)} %psum.37), channel_id=1, replica_groups=mesh['z_hi'=2,'x'=4,'y'=8,'core'=2,'scen'=4] {'x'}, use_global_device_ids=true, to_apply=%region_6.0 | all-reduce | flops 16 | bytes 128 | tf_op jit(solution)/shard_map/psum | solution.py:21
  131.9 17.8 %all-reduce = (f32[2,16]{1,0:T(2,128)S(1)}, f32[4,16]{1,0:T(4,128)S(1)}) all-reduce(f32[2,16]{1,0:T(2,128)S(1)} %broadcast_multiply_fusion.5, f32[4,16]{1,0:T(4,128)S(1)} %broadcast_multiply_fusion.4), channel_id=1, replica_groups=mesh['z_hi'=2,'x'=4,'y'=8,'core'=2,'scen'=4] {'z_hi','scen'}, use_global_device_ids=true, to_apply=%region_2.0 | all-reduce | flops 96 | bytes 768 | tf_op jit(solution)/shard_map/psum | solution.py:28
  149.7 0.6 multiply_reduce_fusion
  150.3 0.6 multiply_reduce_fusion.1
  151.7 0.9 maximum_bitcast_fusion
  (94 shorter events, 5.2 us)
Async XLA Ops:
  0.6 4.8 %copy-start.7 = (s32[1,4]{1,0:T(1,128)S(1)}, s32[1,4]{1,0:T(1,128)}, u32[]{:S(2)}) copy-start(s32[1,4]{1,0:T(1,128)} %param.19) | copy-start | bytes 52
  0.6 5.0 %copy-start.5 = (f32[1,4,8]{2,1,0:T(4,128)S(1)}, f32[1,4,8]{2,1,0:T(4,128)}, u32[]{:S(2)}) copy-start(f32[1,4,8]{2,1,0:T(4,128)} %param.21) | copy-start | bytes 388
  0.7 6.0 %copy-start.8 = (s32[16]{0:T(128)S(1)}, s32[16]{0:T(128)}, u32[]{:S(2)}) copy-start(s32[16]{0:T(128)} %param.25) | copy-start | bytes 196
  0.7 6.0 %copy-start.6 = (s32[1,16]{1,0:T(1,128)S(1)}, s32[1,16]{1,0:T(1,128)}, u32[]{:S(2)}) copy-start(s32[1,16]{1,0:T(1,128)} %param.23) | copy-start | bytes 196
  0.7 7.2 %copy-start.4 = (f32[48,16]{0,1:T(8,128)S(1)}, f32[48,16]{0,1:T(8,128)}, u32[]{:S(2)}) copy-start(f32[48,16]{0,1:T(8,128)} %param.27) | copy-start | bytes 9220
  21.2 18.2 %copy-start.3 = (f32[1,48,16,16]{1,3,2,0:T(8,128)S(1)}, f32[1,48,16,16]{1,3,2,0:T(8,128)}, u32[]{:S(2)}) copy-start(f32[1,48,16,16]{1,3,2,0:T(8,128)} %param.24) | copy-start | bytes 147460
  22.5 18.3 %copy-start = (f32[1,4,8,48,16]{3,4,2,1,0:T(8,128)S(1)}, f32[1,4,8,48,16]{3,4,2,1,0:T(8,128)}, u32[]{:S(2)}) copy-start(f32[1,4,8,48,16]{3,4,2,1,0:T(8,128)} %param.22) | copy-start | bytes 294916
  22.7 17.1 %collective-permute-start.3 = (f32[8,384]{1,0:T(8,128)S(1)}, f32[8,384]{1,0:T(8,128)S(1)}, u32[]{:S(2)}, u32[]{:S(2)}) collective-permute-start(f32[8,384]{1,0:T(8,128)S(1)} %squeeze.56), channel_id=1, source_target_pairs={{0,32},{4,36},{8,40},{12,44},{16,48},{20,52},{24,56},{28,60},{32,6... | collective-permute-start | bytes 36872 | tf_op jit(solution)/shard_map/ppermute | solution.py:129
  29.7 10.4 %collective-permute-start.2 = (f32[8,384]{1,0:T(8,128)S(1)}, f32[8,384]{1,0:T(8,128)S(1)}, u32[]{:S(2)}, u32[]{:S(2)}) collective-permute-start(f32[8,384]{1,0:T(8,128)S(1)} %squeeze.55), channel_id=1, source_target_pairs={{0,480},{4,484},{8,488},{12,492},{16,496},{20,500},{24,504},{28,50... | collective-permute-start | bytes 36872 | tf_op jit(solution)/shard_map/ppermute | solution.py:129
  33.6 6.7 %collective-permute-start.1 = (f32[8,384]{1,0:T(8,128)S(1)}, f32[8,384]{1,0:T(8,128)S(1)}, u32[]{:S(2)}, u32[]{:S(2)}) collective-permute-start(f32[8,384]{1,0:T(8,128)S(1)} %squeeze.54), channel_id=1, source_target_pairs={{0,4},{4,8},{8,12},{12,16},{16,20},{20,24},{24,28},{28,32},{32,36}... | collective-permute-start | bytes 36872 | tf_op jit(solution)/shard_map/ppermute | solution.py:129
  35.6 5.0 %collective-permute-start = (f32[8,384]{1,0:T(8,128)S(1)}, f32[8,384]{1,0:T(8,128)S(1)}, u32[]{:S(2)}, u32[]{:S(2)}) collective-permute-start(f32[8,384]{1,0:T(8,128)S(1)} %squeeze.53), channel_id=1, source_target_pairs={{0,508},{4,0},{8,4},{12,8},{16,12},{20,16},{24,20},{28,24},{32,28}... | collective-permute-start | bytes 36872 | tf_op jit(solution)/shard_map/ppermute | solution.py:129
  54.5 18.1 %copy-start.9 = (f32[1,16]{1,0:T(1,128)S(1)}, f32[1,16]{1,0:T(1,128)}, u32[]{:S(2)}) copy-start(f32[1,16]{1,0:T(1,128)} %get-tuple-element.15) | copy-start | bytes 196
  54.5 18.1 %copy-start.10 = (f32[1,16]{1,0:T(1,128)S(1)}, f32[1,16]{1,0:T(1,128)}, u32[]{:S(2)}) copy-start(f32[1,16]{1,0:T(1,128)} %get-tuple-element.20) | copy-start | bytes 196
  54.5 77.0 %copy-start.1 = (f32[384,48]{1,0:T(8,128)S(1)}, f32[384,48]{1,0:T(8,128)}, u32[]{:S(2)}) copy-start(f32[384,48]{1,0:T(8,128)} %get-tuple-element.16) | copy-start | bytes 221188
  54.5 77.0 %copy-start.2 = (f32[384,48]{1,0:T(8,128)S(1)}, f32[384,48]{1,0:T(8,128)}, u32[]{:S(2)}) copy-start(f32[384,48]{1,0:T(8,128)} %get-tuple-element.21) | copy-start | bytes 221188
  56.1 94.8 %collective-permute-start.7 = (f32[8,384]{1,0:T(8,128)S(1)}, f32[8,384]{1,0:T(8,128)S(1)}, u32[]{:S(2)}, u32[]{:S(2)}) collective-permute-start(f32[8,384]{1,0:T(8,128)S(1)} %squeeze.61), channel_id=1, source_target_pairs={{0,32},{4,36},{8,40},{12,44},{16,48},{20,52},{24,56},{28,60},{32,6... | collective-permute-start | bytes 36872 | tf_op jit(solution)/shard_map/ppermute | solution.py:129
  62.1 89.0 %collective-permute-start.6 = (f32[8,384]{1,0:T(8,128)S(1)}, f32[8,384]{1,0:T(8,128)S(1)}, u32[]{:S(2)}, u32[]{:S(2)}) collective-permute-start(f32[8,384]{1,0:T(8,128)S(1)} %squeeze.60), channel_id=1, source_target_pairs={{0,480},{4,484},{8,488},{12,492},{16,496},{20,500},{24,504},{28,50... | collective-permute-start | bytes 36872 | tf_op jit(solution)/shard_map/ppermute | solution.py:129
  66.9 84.4 %collective-permute-start.5 = (f32[8,384]{1,0:T(8,128)S(1)}, f32[8,384]{1,0:T(8,128)S(1)}, u32[]{:S(2)}, u32[]{:S(2)}) collective-permute-start(f32[8,384]{1,0:T(8,128)S(1)} %squeeze.59), channel_id=1, source_target_pairs={{0,4},{4,8},{8,12},{12,16},{16,20},{20,24},{24,28},{28,32},{32,36}... | collective-permute-start | bytes 36872 | tf_op jit(solution)/shard_map/ppermute | solution.py:129
  70.0 81.4 %collective-permute-start.4 = (f32[8,384]{1,0:T(8,128)S(1)}, f32[8,384]{1,0:T(8,128)S(1)}, u32[]{:S(2)}, u32[]{:S(2)}) collective-permute-start(f32[8,384]{1,0:T(8,128)S(1)} %squeeze.58), channel_id=1, source_target_pairs={{0,508},{4,0},{8,4},{12,8},{16,12},{20,16},{24,20},{28,24},{32,28}... | collective-permute-start | bytes 36872 | tf_op jit(solution)/shard_map/ppermute | solution.py:129

commit v15 on v12

--- a/solution.py
+++ b/solution.py
@@ -50,7 +50,7 @@
     steps, scen_rows, node_count = grad_ref.shape
     companion = companion_ref[...]
     inflow_ref[...] = jnp.dot(
-        picked_ref[...], spread_ref[...], precision=lax.Precision.HIGH, preferred_element_type=jnp.float32
+        picked_ref[...], spread_ref[...], preferred_element_type=jnp.float32
     )
 
     def one_step(index, adjoint_prev):

time: 153 us -> 151 us (0.987)
  Pallas kernels: 24.2 us -> 21.9 us
    pallas_call x2, Pallas kernels: 24.2 us -> 21.9 us  [block_scan(): pl.pallas_call(functools.partial(block_scan_kernel, block_start), grid=(1...]
where the time goes in v15:
time: 151 us; the launch traced here: 150 us
  blocking collectives  76.8 us (51%)
  starting transfers between devices  32.6 us (22%)
  Pallas kernels  21.9 us (15%)
  local copies, waits for them, and re-layouts  10.5 us (7%)
  other arithmetic  5.48 us (4%)
  matrix products  1.79 us (1%)
    psum x3, blocking collectives, sum_both(): fault_value = lax.psum(fault_value, axis)  58.9 us
    ppermute x8, starting transfers between devices, passed_along(): return lax.ppermute(value, axis, pairs)  32.6 us
    pallas_call x2, Pallas kernels, block_scan(): pl.pallas_call(functools.partial(block_scan_kernel, block_start), grid=(1...  21.9 us
    psum x1, blocking collectives, sum_both(): lax.psum((fault_mask * fault_value[None], control_mask * control_value[No...  17.8 us
  transfers between devices with their start and end apart: 8, of which 1 were waited for; matrix products, arithmetic and copies ran while one was open for 2% of the time, Pallas kernels for 0%

profile of v15, /device:TPU:10, one launch (start us, length us, event | category | flops | bytes accessed | tf_op | source)
XLA Modules:
  0.0 150.4 jit_solution(745361403505805109)
XLA Ops:
  0.7 0.8 eq.125
  1.8 0.8 fusion.20
  3.0 0.8 add_add_fusion
  3.7 1.3 convolution_bitcast_fusion.1
  5.1 0.2 copy.106
  5.8 0.8 copy.109.picked_ref
  6.8 0.3 copy.108
  7.1 0.8 convert_element_type.38.pick_ref
  7.9 0.7 copy.110.voltage_ref
  8.6 0.7 add_convert_fusion.spread_ref
  9.3 10.9 %shard_map.165 = (f32[16,1024]{1,0:T(8,128)}, f32[384,48]{1,0:T(8,128)}, f32[1,16]{1,0:T(1,128)}) custom-call(bf16[48,1,16,1024]{3,2,1,0:T(8,128)(2,1)} %grad_ref.3, f32[384,48]{1,0:T(8,128)} %copy.109.picked_ref, f32[48,1024]{1,0:T(8,128)} %add_convert_fusion.spread_ref, f32[1,1024]{1,0:T(1,128)} %companion_ref.3, f32[16,1024]{1,0:T(8,128)} %bitcast.68, ...), custom_call_target="tpu_custom_call" | custom-call | tf_op jit(solution)/shard_map/pallas_call | solution.py:89
  20.2 1.1 copy.111
  21.7 6.8 %collective-permute-start.3 = (f32[8,384]{1,0:T(8,128)S(1)}, f32[8,384]{1,0:T(8,128)S(1)}, u32[]{:S(2)}, u32[]{:S(2)}) collective-permute-start(f32[8,384]{1,0:T(8,128)S(1)} %squeeze.56), channel_id=1, source_target_pairs={{0,32},{4,36},{8,40},{12,44},{16,48},{20,52},{24,56},{28,60},{32,6... | collective-permute-start | bytes 36872 | tf_op jit(solution)/shard_map/ppermute | solution.py:118
  28.6 3.8 %collective-permute-start.2 = (f32[8,384]{1,0:T(8,128)S(1)}, f32[8,384]{1,0:T(8,128)S(1)}, u32[]{:S(2)}, u32[]{:S(2)}) collective-permute-start(f32[8,384]{1,0:T(8,128)S(1)} %squeeze.55), channel_id=1, source_target_pairs={{0,480},{4,484},{8,488},{12,492},{16,496},{20,500},{24,504},{28,50... | collective-permute-start | bytes 36872 | tf_op jit(solution)/shard_map/ppermute | solution.py:118
  32.6 1.9 %collective-permute-start.1 = (f32[8,384]{1,0:T(8,128)S(1)}, f32[8,384]{1,0:T(8,128)S(1)}, u32[]{:S(2)}, u32[]{:S(2)}) collective-permute-start(f32[8,384]{1,0:T(8,128)S(1)} %squeeze.54), channel_id=1, source_target_pairs={{0,4},{4,8},{8,12},{12,16},{16,20},{20,24},{24,28},{28,32},{32,36}... | collective-permute-start | bytes 36872 | tf_op jit(solution)/shard_map/ppermute | solution.py:118
  34.6 3.8 %collective-permute-start = (f32[8,384]{1,0:T(8,128)S(1)}, f32[8,384]{1,0:T(8,128)S(1)}, u32[]{:S(2)}, u32[]{:S(2)}) collective-permute-start(f32[8,384]{1,0:T(8,128)S(1)} %squeeze.53), channel_id=1, source_target_pairs={{0,508},{4,0},{8,4},{12,8},{16,12},{20,16},{24,20},{28,24},{32,28}... | collective-permute-start | bytes 36872 | tf_op jit(solution)/shard_map/ppermute | solution.py:118
  39.4 0.2 collective-permute-done
  39.8 0.5 convolution_bitcast_fusion
  40.7 0.8 copy.118.picked_ref
  41.5 10.9 %shard_map.166 = (f32[16,1024]{1,0:T(8,128)}, f32[384,48]{1,0:T(8,128)}, f32[1,16]{1,0:T(1,128)}) custom-call(bf16[48,1,16,1024]{3,2,1,0:T(8,128)(2,1)} %grad_ref.3, f32[384,48]{1,0:T(8,128)} %copy.118.picked_ref, f32[48,1024]{1,0:T(8,128)} %add_convert_fusion.spread_ref, f32[1,1024]{1,0:T(1,128)} %companion_ref.3, f32[16,1024]{1,0:T(8,128)} %get-tuple-element.17.start_ref, ...), custom_call_target="tpu_custom_call" | custom-call | tf_op jit(solution)/shard_map/pallas_call | solution.py:89
  52.5 1.1 copy.120
  54.0 5.9 %collective-permute-start.7 = (f32[8,384]{1,0:T(8,128)S(1)}, f32[8,384]{1,0:T(8,128)S(1)}, u32[]{:S(2)}, u32[]{:S(2)}) collective-permute-start(f32[8,384]{1,0:T(8,128)S(1)} %squeeze.61), channel_id=1, source_target_pairs={{0,32},{4,36},{8,40},{12,44},{16,48},{20,52},{24,56},{28,60},{32,6... | collective-permute-start | bytes 36872 | tf_op jit(solution)/shard_map/ppermute | solution.py:118
  60.0 4.7 %collective-permute-start.6 = (f32[8,384]{1,0:T(8,128)S(1)}, f32[8,384]{1,0:T(8,128)S(1)}, u32[]{:S(2)}, u32[]{:S(2)}) collective-permute-start(f32[8,384]{1,0:T(8,128)S(1)} %squeeze.60), channel_id=1, source_target_pairs={{0,480},{4,484},{8,488},{12,492},{16,496},{20,500},{24,504},{28,50... | collective-permute-start | bytes 36872 | tf_op jit(solution)/shard_map/ppermute | solution.py:118
  64.8 3.0 %collective-permute-start.5 = (f32[8,384]{1,0:T(8,128)S(1)}, f32[8,384]{1,0:T(8,128)S(1)}, u32[]{:S(2)}, u32[]{:S(2)}) collective-permute-start(f32[8,384]{1,0:T(8,128)S(1)} %squeeze.59), channel_id=1, source_target_pairs={{0,4},{4,8},{8,12},{12,16},{16,20},{20,24},{24,28},{28,32},{32,36}... | collective-permute-start | bytes 36872 | tf_op jit(solution)/shard_map/ppermute | solution.py:118
  67.9 2.6 %collective-permute-start.4 = (f32[8,384]{1,0:T(8,128)S(1)}, f32[8,384]{1,0:T(8,128)S(1)}, u32[]{:S(2)}, u32[]{:S(2)}) collective-permute-start(f32[8,384]{1,0:T(8,128)S(1)} %squeeze.58), channel_id=1, source_target_pairs={{0,508},{4,0},{8,4},{12,8},{16,12},{20,16},{24,20},{28,24},{32,28}... | collective-permute-start | bytes 36872 | tf_op jit(solution)/shard_map/ppermute | solution.py:118
  70.5 2.5 %psum.36 = f32[16]{0:T(128)S(1)} all-reduce(f32[16]{0:T(128)S(1)} %add.68), channel_id=1, replica_groups=mesh['z_hi'=2,'x'=4,'y'=8,'core'=2,'scen'=4] {'core'}, use_global_device_ids=true, to_apply=%region_4.0 | all-reduce | flops 16 | bytes 128 | tf_op jit(solution)/shard_map/psum | solution.py:21
  73.0 20.5 %psum.37 = f32[16]{0:T(128)S(1)} all-reduce(f32[16]{0:T(128)S(1)} %psum.36), channel_id=1, replica_groups=mesh['z_hi'=2,'x'=4,'y'=8,'core'=2,'scen'=4] {'y'}, use_global_device_ids=true, to_apply=%region_5.0 | all-reduce | flops 16 | bytes 128 | tf_op jit(solution)/shard_map/psum | solution.py:21
  93.5 36.0 %psum.38 = f32[16]{0:T(128)S(1)} all-reduce(f32[16]{0:T(128)S(1)} %psum.37), channel_id=1, replica_groups=mesh['z_hi'=2,'x'=4,'y'=8,'core'=2,'scen'=4] {'x'}, use_global_device_ids=true, to_apply=%region_6.0 | all-reduce | flops 16 | bytes 128 | tf_op jit(solution)/shard_map/psum | solution.py:21
  129.8 17.8 %all-reduce = (f32[2,16]{1,0:T(2,128)S(1)}, f32[4,16]{1,0:T(4,128)S(1)}) all-reduce(f32[2,16]{1,0:T(2,128)S(1)} %broadcast_multiply_fusion.5, f32[4,16]{1,0:T(4,128)S(1)} %broadcast_multiply_fusion.4), channel_id=1, replica_groups=mesh['z_hi'=2,'x'=4,'y'=8,'core'=2,'scen'=4] {'z_hi','scen'}, use_global_device_ids=true, to_apply=%region_2.0 | all-reduce | flops 96 | bytes 768 | tf_op jit(solution)/shard_map/psum | solution.py:28
  147.6 0.6 multiply_reduce_fusion
  148.2 0.6 multiply_reduce_fusion.1
  149.6 0.9 maximum_bitcast_fusion
  (94 shorter events, 5.2 us)
Async XLA Ops:
  0.6 4.8 %copy-start.7 = (s32[1,4]{1,0:T(1,128)S(1)}, s32[1,4]{1,0:T(1,128)}, u32[]{:S(2)}) copy-start(s32[1,4]{1,0:T(1,128)} %param.19) | copy-start | bytes 52
  0.6 5.0 %copy-start.5 = (f32[1,4,8]{2,1,0:T(4,128)S(1)}, f32[1,4,8]{2,1,0:T(4,128)}, u32[]{:S(2)}) copy-start(f32[1,4,8]{2,1,0:T(4,128)} %param.21) | copy-start | bytes 388
  0.7 6.0 %copy-start.8 = (s32[16]{0:T(128)S(1)}, s32[16]{0:T(128)}, u32[]{:S(2)}) copy-start(s32[16]{0:T(128)} %param.25) | copy-start | bytes 196
  0.7 6.0 %copy-start.6 = (s32[1,16]{1,0:T(1,128)S(1)}, s32[1,16]{1,0:T(1,128)}, u32[]{:S(2)}) copy-start(s32[1,16]{1,0:T(1,128)} %param.23) | copy-start | bytes 196
  0.7 7.2 %copy-start.4 = (f32[48,16]{0,1:T(8,128)S(1)}, f32[48,16]{0,1:T(8,128)}, u32[]{:S(2)}) copy-start(f32[48,16]{0,1:T(8,128)} %param.27) | copy-start | bytes 9220
  20.2 18.2 %copy-start.3 = (f32[1,48,16,16]{1,3,2,0:T(8,128)S(1)}, f32[1,48,16,16]{1,3,2,0:T(8,128)}, u32[]{:S(2)}) copy-start(f32[1,48,16,16]{1,3,2,0:T(8,128)} %param.24) | copy-start | bytes 147460
  21.5 18.3 %copy-start = (f32[1,4,8,48,16]{3,4,2,1,0:T(8,128)S(1)}, f32[1,4,8,48,16]{3,4,2,1,0:T(8,128)}, u32[]{:S(2)}) copy-start(f32[1,4,8,48,16]{3,4,2,1,0:T(8,128)} %param.22) | copy-start | bytes 294916
  21.7 17.1 %collective-permute-start.3 = (f32[8,384]{1,0:T(8,128)S(1)}, f32[8,384]{1,0:T(8,128)S(1)}, u32[]{:S(2)}, u32[]{:S(2)}) collective-permute-start(f32[8,384]{1,0:T(8,128)S(1)} %squeeze.56), channel_id=1, source_target_pairs={{0,32},{4,36},{8,40},{12,44},{16,48},{20,52},{24,56},{28,60},{32,6... | collective-permute-start | bytes 36872 | tf_op jit(solution)/shard_map/ppermute | solution.py:118
  28.6 10.4 %collective-permute-start.2 = (f32[8,384]{1,0:T(8,128)S(1)}, f32[8,384]{1,0:T(8,128)S(1)}, u32[]{:S(2)}, u32[]{:S(2)}) collective-permute-start(f32[8,384]{1,0:T(8,128)S(1)} %squeeze.55), channel_id=1, source_target_pairs={{0,480},{4,484},{8,488},{12,492},{16,496},{20,500},{24,504},{28,50... | collective-permute-start | bytes 36872 | tf_op jit(solution)/shard_map/ppermute | solution.py:118
  32.6 6.7 %collective-permute-start.1 = (f32[8,384]{1,0:T(8,128)S(1)}, f32[8,384]{1,0:T(8,128)S(1)}, u32[]{:S(2)}, u32[]{:S(2)}) collective-permute-start(f32[8,384]{1,0:T(8,128)S(1)} %squeeze.54), channel_id=1, source_target_pairs={{0,4},{4,8},{8,12},{12,16},{16,20},{20,24},{24,28},{28,32},{32,36}... | collective-permute-start | bytes 36872 | tf_op jit(solution)/shard_map/ppermute | solution.py:118
  34.6 5.0 %collective-permute-start = (f32[8,384]{1,0:T(8,128)S(1)}, f32[8,384]{1,0:T(8,128)S(1)}, u32[]{:S(2)}, u32[]{:S(2)}) collective-permute-start(f32[8,384]{1,0:T(8,128)S(1)} %squeeze.53), channel_id=1, source_target_pairs={{0,508},{4,0},{8,4},{12,8},{16,12},{20,16},{24,20},{28,24},{32,28}... | collective-permute-start | bytes 36872 | tf_op jit(solution)/shard_map/ppermute | solution.py:118
  52.5 18.1 %copy-start.9 = (f32[1,16]{1,0:T(1,128)S(1)}, f32[1,16]{1,0:T(1,128)}, u32[]{:S(2)}) copy-start(f32[1,16]{1,0:T(1,128)} %get-tuple-element.15) | copy-start | bytes 196
  52.5 18.1 %copy-start.10 = (f32[1,16]{1,0:T(1,128)S(1)}, f32[1,16]{1,0:T(1,128)}, u32[]{:S(2)}) copy-start(f32[1,16]{1,0:T(1,128)} %get-tuple-element.20) | copy-start | bytes 196
  52.5 77.0 %copy-start.1 = (f32[384,48]{1,0:T(8,128)S(1)}, f32[384,48]{1,0:T(8,128)}, u32[]{:S(2)}) copy-start(f32[384,48]{1,0:T(8,128)} %get-tuple-element.16) | copy-start | bytes 221188
  52.5 77.0 %copy-start.2 = (f32[384,48]{1,0:T(8,128)S(1)}, f32[384,48]{1,0:T(8,128)}, u32[]{:S(2)}) copy-start(f32[384,48]{1,0:T(8,128)} %get-tuple-element.21) | copy-start | bytes 221188
  54.0 94.9 %collective-permute-start.7 = (f32[8,384]{1,0:T(8,128)S(1)}, f32[8,384]{1,0:T(8,128)S(1)}, u32[]{:S(2)}, u32[]{:S(2)}) collective-permute-start(f32[8,384]{1,0:T(8,128)S(1)} %squeeze.61), channel_id=1, source_target_pairs={{0,32},{4,36},{8,40},{12,44},{16,48},{20,52},{24,56},{28,60},{32,6... | collective-permute-start | bytes 36872 | tf_op jit(solution)/shard_map/ppermute | solution.py:118
  60.0 89.0 %collective-permute-start.6 = (f32[8,384]{1,0:T(8,128)S(1)}, f32[8,384]{1,0:T(8,128)S(1)}, u32[]{:S(2)}, u32[]{:S(2)}) collective-permute-start(f32[8,384]{1,0:T(8,128)S(1)} %squeeze.60), channel_id=1, source_target_pairs={{0,480},{4,484},{8,488},{12,492},{16,496},{20,500},{24,504},{28,50... | collective-permute-start | bytes 36872 | tf_op jit(solution)/shard_map/ppermute | solution.py:118
  64.8 84.4 %collective-permute-start.5 = (f32[8,384]{1,0:T(8,128)S(1)}, f32[8,384]{1,0:T(8,128)S(1)}, u32[]{:S(2)}, u32[]{:S(2)}) collective-permute-start(f32[8,384]{1,0:T(8,128)S(1)} %squeeze.59), channel_id=1, source_target_pairs={{0,4},{4,8},{8,12},{12,16},{16,20},{20,24},{24,28},{28,32},{32,36}... | collective-permute-start | bytes 36872 | tf_op jit(solution)/shard_map/ppermute | solution.py:118
  67.9 81.5 %collective-permute-start.4 = (f32[8,384]{1,0:T(8,128)S(1)}, f32[8,384]{1,0:T(8,128)S(1)}, u32[]{:S(2)}, u32[]{:S(2)}) collective-permute-start(f32[8,384]{1,0:T(8,128)S(1)} %squeeze.58), channel_id=1, source_target_pairs={{0,508},{4,0},{8,4},{12,8},{16,12},{20,16},{24,20},{28,24},{32,28}... | collective-permute-start | bytes 36872 | tf_op jit(solution)/shard_map/ppermute | solution.py:118
